TPU v7x, 256 devices: a whole 4x4x8 slice. The times are simulated.
256 devices in a mesh: phase: 2 (over core), seq: 16 (over y_hi, z), dp: 8 (over x, y_lo).
Axes of the slice: x: 4, y: 4 (y_hi: 2, y_lo: 2; y = y_hi * 2 + y_lo), z: 8, core: 2. Of those that a mesh axis runs over, the one named last changes fastest.
Arguments:
- sections: bfloat16 [2, 2, 16384, 2048], P('phase', None, ('dp', 'seq')), may hold values from -6 to 6
- head_gains: float32 [2, 32], replicated, may hold values from 1 to 2
- block_counts: int32 [8, 2, 8], P('dp'), may hold values from 1 to 4, as said below
Outputs:
- result: bfloat16 [2, 2, 16384, 2048], P('phase', None, ('dp', 'seq'))
- gain_grads: float32 [2, 32], P('phase')
Inputs may be any that keep to these rules, and one draw needn't show every extreme that they name: In every batch group both rows of block_counts sum to 16; decoder counts are at most 3 and encoder counts at most 4, both reached in every group; at every segment's start the encoder block offset exceeds the decoder block offset by 0 or 1.
All inputs are finite; a program needn't handle non-finite values.
Results may differ from a plain program's by a relative error of at most 0.013.
The roundings to bfloat16 on the way count: a program that leaves them out, or rounds other values in their place, can miss the bound.
Values may be sent and summed in bfloat16 or wider, within the bound.
No kernel may reach another device: no remote copies, remote signals or barrier semaphores. Data moves between devices by JAX's collectives and lax.ppermute only.
A program may use at most 128 MiB of HBM per device.

v0:
```python
import math

import jax
import jax.numpy as jnp
from jax import lax
from jax.sharding import PartitionSpec as P

BLOCK = 128
ENC_MOST = 4
BLK_DEV = 1
REACH_LOW = 2
REACH_HIGH = 4
WINDOW = 7


masked_score = -1e30
heads_per_pass = 4


def passed_along(value, axis, steps):
    count = lax.axis_size(axis)
    initial, last = (max(0, -steps), min(count, count - steps))
    return lax.ppermute(value, axis, [(source, source + steps) for source in range(initial, last)])


def segment_of(block_ids, block_sizes, block_total):
    starts = jnp.cumsum(block_sizes) - block_sizes
    found = jnp.sum((starts[None, :] <= block_ids[:, None]).astype(jnp.int32), axis=1) - 1
    inside = jnp.logical_and(block_ids >= 0, block_ids < block_total)
    return jnp.where(inside, found, -1)


def cross_tile(queries, upstream, key_rows, value_rows, allowed, gain_logit, gain_value):
    row_count = queries.shape[0]
    key_count = key_rows.shape[0]
    head_count = gain_logit.shape[0]
    head_size = queries.shape[1] // head_count
    inv_root = 1.0 / math.sqrt(head_size)
    query_heads = queries.reshape(row_count, head_count, head_size)
    upstream_heads = upstream.reshape(row_count, head_count, head_size)
    key_heads = key_rows.reshape(key_count, head_count, head_size)
    value_heads = value_rows.reshape(key_count, head_count, head_size)
    raw_score = (
        jnp.einsum("qhd,khd->hqk", query_heads, key_heads, preferred_element_type=jnp.float32)
        * inv_root
    )
    logits = jnp.where(allowed[None, :, :], gain_logit[:, None, None] * raw_score, masked_score)
    row_top = jnp.max(logits, axis=2, keepdims=True)
    lifted = jnp.exp(logits - row_top)
    chances = lifted / jnp.sum(lifted, axis=2, keepdims=True)
    chances_low = chances.astype(jnp.bfloat16)
    attended = (
        jnp.einsum("hqk,khd->qhd", chances_low, value_heads, preferred_element_type=jnp.float32)
        * gain_value[None, :, None]
    ).astype(jnp.bfloat16)
    slope = (
        jnp.einsum("qhd,khd->hqk", upstream_heads, value_heads, preferred_element_type=jnp.float32)
        * gain_value[:, None, None]
    )
    carried = jnp.einsum(
        "qhd,qhd->hq", upstream_heads, attended, preferred_element_type=jnp.float32
    )
    score_grad = chances * (slope - carried[:, :, None])
    score_low = score_grad.astype(jnp.bfloat16)
    factor = gain_logit * inv_root
    query_grad = (
        jnp.einsum("hqk,khd->qhd", score_low, key_heads, preferred_element_type=jnp.float32)
        * factor[None, :, None]
    )
    key_grad = (
        jnp.einsum("hqk,qhd->khd", score_low, query_heads, preferred_element_type=jnp.float32)
        * factor[None, :, None]
    )
    value_grad = (
        jnp.einsum("hqk,qhd->khd", chances_low, upstream_heads, preferred_element_type=jnp.float32)
        * gain_value[None, :, None]
    )
    gain_term = jnp.sum(score_grad * raw_score, axis=(1, 2))
    return (
        attended.reshape(row_count, -1),
        query_grad.reshape(row_count, -1),
        key_grad.reshape(key_count, -1),
        value_grad.reshape(key_count, -1),
        gain_term,
    )


def head_passes(queries, upstream, key_rows, value_rows, allowed, head_gains):
    head_count = head_gains.shape[1]
    head_size = queries.shape[1] // head_count
    results = []
    for first_head in range(0, head_count, heads_per_pass):
        low_col = first_head * head_size
        high_col = low_col + heads_per_pass * head_size
        results.append(
            cross_tile(
                queries[:, low_col:high_col],
                upstream[:, low_col:high_col],
                key_rows[:, low_col:high_col],
                value_rows[:, low_col:high_col],
                allowed,
                head_gains[0, first_head : first_head + heads_per_pass],
                head_gains[1, first_head : first_head + heads_per_pass],
            )
        )
    return tuple(
        (jnp.concatenate([piece[member] for piece in results], axis=-1) for member in range(5))
    )


def local(sections, head_gains, block_counts):
    phase_index = lax.axis_index("phase")
    shard_index = lax.axis_index("seq")
    local_pair = sections[0]
    tok_dev = local_pair.shape[1]
    inner_width = local_pair.shape[2]
    head_count = head_gains.shape[1]
    block_total = BLK_DEV * lax.axis_size("seq")
    enc_counts = block_counts[0, 0]
    dec_counts = block_counts[0, 1]
    offsets = list(range(-REACH_LOW, REACH_HIGH + 1))
    arrived = passed_along(local_pair, "phase", 1)
    pieces = []
    for offset in offsets:
        if offset == 0:
            pieces.append(arrived)
        else:
            pieces.append(passed_along(arrived, "seq", -offset))
    window = jnp.concatenate(pieces, axis=1)
    window_rows = window.shape[1]

    def decoder_work(operands):
        own_pair, window_pair = operands
        first_block = (shard_index - REACH_LOW) * BLK_DEV
        window_blocks = first_block + jnp.arange(WINDOW * BLK_DEV, dtype=jnp.int32)
        enc_segs = segment_of(window_blocks, enc_counts, block_total)
        dec_blocks = shard_index * BLK_DEV + jnp.arange(BLK_DEV, dtype=jnp.int32)
        dec_segs = segment_of(dec_blocks, dec_counts, block_total)
        enc_starts = jnp.cumsum(enc_counts) - enc_counts
        key_sum = jnp.zeros((window_rows, inner_width), jnp.float32)
        value_sum = jnp.zeros((window_rows, inner_width), jnp.float32)
        gain_term = jnp.zeros((head_count,), jnp.float32)
        segment = dec_segs[0]
        start_block = jnp.clip(enc_starts[segment] - first_block, 0, WINDOW * BLK_DEV - ENC_MOST)
        slice_segs = lax.dynamic_slice_in_dim(enc_segs, start_block, ENC_MOST)
        allowed = jnp.broadcast_to(
            jnp.repeat(slice_segs == segment, BLOCK)[None, :], (BLOCK, ENC_MOST * BLOCK)
        )
        key_slice = lax.dynamic_slice_in_dim(
            window_pair[0], start_block * BLOCK, ENC_MOST * BLOCK, 0
        )
        value_slice = lax.dynamic_slice_in_dim(
            window_pair[1], start_block * BLOCK, ENC_MOST * BLOCK, 0
        )
        attended, query_grad, key_grad, value_grad, block_gain = head_passes(
            own_pair[0, 0:BLOCK], own_pair[1, 0:BLOCK], key_slice, value_slice, allowed, head_gains
        )
        write_at = start_block * BLOCK
        key_sum = lax.dynamic_update_slice_in_dim(
            key_sum,
            lax.dynamic_slice_in_dim(key_sum, write_at, ENC_MOST * BLOCK, 0) + key_grad,
            write_at,
            0,
        )
        value_sum = lax.dynamic_update_slice_in_dim(
            value_sum,
            lax.dynamic_slice_in_dim(value_sum, write_at, ENC_MOST * BLOCK, 0) + value_grad,
            write_at,
            0,
        )
        attended_rows = [attended]
        query_rows = [query_grad.astype(jnp.bfloat16)]
        gain_term = gain_term + block_gain
        produced = jnp.stack(
            [jnp.concatenate(attended_rows, axis=0), jnp.concatenate(query_rows, axis=0)]
        )
        window_grads = jnp.stack([key_sum.astype(jnp.bfloat16), value_sum.astype(jnp.bfloat16)])
        return (produced, window_grads, gain_term)

    def encoder_rest(operands):
        return (
            jnp.zeros((2, tok_dev, inner_width), jnp.bfloat16),
            jnp.zeros((2, window_rows, inner_width), jnp.bfloat16),
            jnp.zeros((head_count,), jnp.float32),
        )

    produced, window_grads, gain_term = lax.cond(
        phase_index == 1, decoder_work, encoder_rest, (local_pair, window)
    )
    summed_grads = jnp.zeros((2, tok_dev, inner_width), jnp.float32)
    for slot, offset in enumerate(offsets):
        portion = window_grads[:, slot * tok_dev : (slot + 1) * tok_dev]
        if offset == 0:
            summed_grads = summed_grads + portion.astype(jnp.float32)
        else:
            summed_grads = summed_grads + passed_along(portion, "seq", offset).astype(jnp.float32)
    returned = passed_along(summed_grads.astype(jnp.bfloat16), "phase", -1)
    value_heads = local_pair[1].reshape(tok_dev, head_count, -1)
    value_grad_heads = returned[1].reshape(tok_dev, head_count, -1)
    value_term = (
        jnp.einsum("thd,thd->h", value_heads, value_grad_heads, preferred_element_type=jnp.float32)
        / head_gains[1]
    )
    chosen_term = jnp.where(phase_index == 0, value_term, gain_term)
    token_total = tok_dev * lax.axis_size("seq") * lax.axis_size("dp")
    gain_total = lax.psum(chosen_term, ("seq", "dp")) / math.sqrt(token_total)
    result = jnp.where(phase_index == 0, returned, produced)[None]
    return (result, gain_total[None])


def solution(mesh):
    return jax.shard_map(
        local,
        mesh=mesh,
        in_specs=(P("phase", None, ("dp", "seq"), None), P(), P("dp", None, None)),
        out_specs=(P("phase", None, ("dp", "seq"), None), P("phase", None)),
        check_vma=False,
    )
```

profile of v0, /device:TPU:8, one launch (start us, length us, event | category | flops | bytes accessed | tf_op | source)
XLA Modules:
  0.0 761.8 jit_solution(11406501469318834703)
XLA Ops:
  0.6 1.6 copy.114
  2.3 1.8 collective-permute-start
  4.1 2.2 collective-permute-done
  6.3 6.2 collective-permute-start.1
  12.4 4.8 collective-permute-start.2
  17.2 1.3 collective-permute-start.3
  18.5 1.3 collective-permute-start.4
  19.8 1.3 collective-permute-start.5
  21.1 21.6 %collective-permute-done.1 = bf16[2,128,2048]{1,2,0:T(8,128)(2,1)} collective-permute-done((bf16[2,128,2048]{1,2,0:T(8,128)(2,1)S(1)}, bf16[2,128,2048]{1,2,0:T(8,128)(2,1)}, u32[]{:S(2)}, u32[]{:S(2)}) %collective-permute-start.1) | collective-permute-done | bytes 1048608 | tf_op jit(solution)/shard_map/ppermute | solution.py:23
  42.7 1.3 collective-permute-start.6
  44.0 1.4 constant_dynamic-update-slice_fusion.40
  45.4 34.1 %collective-permute-done.2 = bf16[2,128,2048]{1,2,0:T(8,128)(2,1)} collective-permute-done((bf16[2,128,2048]{1,2,0:T(8,128)(2,1)S(1)}, bf16[2,128,2048]{1,2,0:T(8,128)(2,1)}, u32[]{:S(2)}, u32[]{:S(2)}) %collective-permute-start.2) | collective-permute-done | bytes 1048608 | tf_op jit(solution)/shard_map/ppermute | solution.py:23
  79.5 1.5 constant_dynamic-update-slice_fusion.39
  81.0 0.2 constant_dynamic-update-slice_fusion.38
  81.2 0.0 collective-permute-done.3
  81.2 1.5 constant_dynamic-update-slice_fusion.37
  82.7 8.6 %collective-permute-done.4 = bf16[2,128,2048]{1,2,0:T(8,128)(2,1)S(1)} collective-permute-done((bf16[2,128,2048]{1,2,0:T(8,128)(2,1)S(1)}, bf16[2,128,2048]{1,2,0:T(8,128)(2,1)S(1)}, u32[]{:S(2)}, u32[]{:S(2)}) %collective-permute-start.4) | collective-permute-done | bytes 1048608 | tf_op jit(solution)/shard_map/ppermute | solution.py:23
  91.3 0.2 constant_dynamic-update-slice_fusion.36
  91.5 0.0 copy-start.56
  91.6 0.0 copy-start.82
  91.6 21.7 %collective-permute-done.5 = bf16[2,128,2048]{1,2,0:T(8,128)(2,1)S(1)} collective-permute-done((bf16[2,128,2048]{1,2,0:T(8,128)(2,1)S(1)}, bf16[2,128,2048]{1,2,0:T(8,128)(2,1)S(1)}, u32[]{:S(2)}, u32[]{:S(2)}) %collective-permute-start.5) | collective-permute-done | bytes 1048608 | tf_op jit(solution)/shard_map/ppermute | solution.py:23
  113.3 0.2 constant_dynamic-update-slice_fusion.35
  113.6 0.0 collective-permute-done.6
  113.6 0.2 constant_dynamic-update-slice_fusion.34
  113.8 0.0 copy-done.56
  113.9 0.0 copy-done.82
  113.9 3.7 conditional.1
  113.9 0.1 broadcast.194
  114.0 3.5 broadcast.195
  117.5 0.0 copy-start.106
  117.5 0.5 copy-done.106
  118.0 3.3 fusion.254
  121.3 103.5 %collective-permute-start.12 = (bf16[2,128,2048]{1,2,0:T(8,128)(2,1)S(1)}, bf16[2,128,2048]{1,2,0:T(8,128)(2,1)S(1)}, u32[]{:S(2)}, u32[]{:S(2)}) collective-permute-start(bf16[2,128,2048]{1,2,0:T(8,128)(2,1)S(1)} %get-tuple-element.147), channel_id=1, source_target_pairs={{0,32},{8,40},{16,48},{24,56},{32,64},{40,72},{48,80},{56,88},{64,... | collective-permute-start | bytes 3145736 | tf_op jit(solution)/shard_map/ppermute | solution.py:23
  224.8 1.4 collective-permute-start.11
  226.2 35.7 %collective-permute-start.10 = (bf16[2,128,2048]{1,2,0:T(8,128)(2,1)S(1)}, bf16[2,128,2048]{1,2,0:T(8,128)(2,1)S(1)}, u32[]{:S(2)}, u32[]{:S(2)}) collective-permute-start(bf16[2,128,2048]{1,2,0:T(8,128)(2,1)S(1)} %get-tuple-element.149), channel_id=1, source_target_pairs={{0,16},{8,24},{16,32},{24,40},{32,48},{40,56},{48,64},{56,72},{64,... | collective-permute-start | bytes 3145736 | tf_op jit(solution)/shard_map/ppermute | solution.py:23
  261.9 1.4 collective-permute-start.9
  263.3 1.3 collective-permute-start.8
  264.6 0.0 collective-permute-done.12
  264.6 1.3 collective-permute-start.7
  265.9 12.8 %collective-permute-done.11 = bf16[2,128,2048]{1,2,0:T(8,128)(2,1)S(1)} collective-permute-done((bf16[2,128,2048]{1,2,0:T(8,128)(2,1)S(1)}, bf16[2,128,2048]{1,2,0:T(8,128)(2,1)S(1)}, u32[]{:S(2)}, u32[]{:S(2)}) %collective-permute-start.11) | collective-permute-done | bytes 1048608 | tf_op jit(solution)/shard_map/ppermute | solution.py:23
  278.6 11.2 %collective-permute-done.10 = bf16[2,128,2048]{1,2,0:T(8,128)(2,1)S(1)} collective-permute-done((bf16[2,128,2048]{1,2,0:T(8,128)(2,1)S(1)}, bf16[2,128,2048]{1,2,0:T(8,128)(2,1)S(1)}, u32[]{:S(2)}, u32[]{:S(2)}) %collective-permute-start.10) | collective-permute-done | bytes 1048608 | tf_op jit(solution)/shard_map/ppermute | solution.py:23
  289.9 11.2 %collective-permute-done.9 = bf16[2,128,2048]{1,2,0:T(8,128)(2,1)S(1)} collective-permute-done((bf16[2,128,2048]{1,2,0:T(8,128)(2,1)S(1)}, bf16[2,128,2048]{1,2,0:T(8,128)(2,1)S(1)}, u32[]{:S(2)}, u32[]{:S(2)}) %collective-permute-start.9) | collective-permute-done | bytes 1048608 | tf_op jit(solution)/shard_map/ppermute | solution.py:23
  301.1 0.0 collective-permute-done.8
  301.1 13.9 %collective-permute-done.7 = bf16[2,128,2048]{1,2,0:T(8,128)(2,1)S(1)} collective-permute-done((bf16[2,128,2048]{1,2,0:T(8,128)(2,1)S(1)}, bf16[2,128,2048]{1,2,0:T(8,128)(2,1)S(1)}, u32[]{:S(2)}, u32[]{:S(2)}) %collective-permute-start.7) | collective-permute-done | bytes 1048608 | tf_op jit(solution)/shard_map/ppermute | solution.py:23
  315.0 3.1 add_convert_fusion
  318.1 1.3 collective-permute-start.13
  319.4 0.8 slice.238
  320.2 95.7 %collective-permute-done.13 = bf16[2,128,2048]{1,2,0:T(8,128)(2,1)S(1)} collective-permute-done((bf16[2,128,2048]{1,2,0:T(8,128)(2,1)}, bf16[2,128,2048]{1,2,0:T(8,128)(2,1)S(1)}, u32[]{:S(2)}, u32[]{:S(2)}) %collective-permute-start.13) | collective-permute-done | bytes 1048608 | tf_op jit(solution)/shard_map/ppermute | solution.py:23
  415.9 0.1 select_bitcast_fusion
  416.0 0.0 copy-start.20
  416.1 0.0 copy-start.107
  416.1 1.3 copy.116
  417.4 0.0 copy-done.20
  417.4 0.3 fusion.241
  417.8 0.0 copy-done.107
  417.8 343.5 %psum.7 = f32[32]{0:T(128)S(1)} all-reduce(f32[32]{0:T(128)S(1)} %broadcast_select_fusion), channel_id=1, replica_groups=mesh['phase'=2,'seq'=16,'dp'=8] {'seq','dp'}, use_global_device_ids=true, to_apply=%region_30.31 | all-reduce | flops 32 | bytes 256 | tf_op jit(solution)/shard_map/psum | solution.py:206
  761.2 0.5 multiply_bitcast_fusion.8
  (3 shorter events, 0.0 us)
Async XLA Ops:
  2.3 4.0 collective-permute-start
  6.3 36.5 %collective-permute-start.1 = (bf16[2,128,2048]{1,2,0:T(8,128)(2,1)S(1)}, bf16[2,128,2048]{1,2,0:T(8,128)(2,1)}, u32[]{:S(2)}, u32[]{:S(2)}) collective-permute-start(bf16[2,128,2048]{1,2,0:T(8,128)(2,1)S(1)} %collective-permute-done), channel_id=1, source_target_pairs={{0,16},{8,24},{16,32},{24,40},{32,48},{40,56},{48,64},{56,72},{64,... | collective-permute-start | bytes 3145736 | tf_op jit(solution)/shard_map/ppermute | solution.py:23
  12.4 67.1 %collective-permute-start.2 = (bf16[2,128,2048]{1,2,0:T(8,128)(2,1)S(1)}, bf16[2,128,2048]{1,2,0:T(8,128)(2,1)}, u32[]{:S(2)}, u32[]{:S(2)}) collective-permute-start(bf16[2,128,2048]{1,2,0:T(8,128)(2,1)S(1)} %collective-permute-done), channel_id=1, source_target_pairs={{0,8},{8,16},{16,24},{24,32},{32,40},{40,48},{48,56},{56,64},{64,7... | collective-permute-start | bytes 3145736 | tf_op jit(solution)/shard_map/ppermute | solution.py:23
  17.2 64.0 %collective-permute-start.3 = (bf16[2,128,2048]{1,2,0:T(8,128)(2,1)S(1)}, bf16[2,128,2048]{1,2,0:T(8,128)(2,1)}, u32[]{:S(2)}, u32[]{:S(2)}) collective-permute-start(bf16[2,128,2048]{1,2,0:T(8,128)(2,1)S(1)} %collective-permute-done), channel_id=1, source_target_pairs={{8,0},{16,8},{24,16},{32,24},{40,32},{48,40},{56,48},{64,56},{72,6... | collective-permute-start | bytes 3145736 | tf_op jit(solution)/shard_map/ppermute | solution.py:23
  18.5 72.8 %collective-permute-start.4 = (bf16[2,128,2048]{1,2,0:T(8,128)(2,1)S(1)}, bf16[2,128,2048]{1,2,0:T(8,128)(2,1)S(1)}, u32[]{:S(2)}, u32[]{:S(2)}) collective-permute-start(bf16[2,128,2048]{1,2,0:T(8,128)(2,1)S(1)} %collective-permute-done), channel_id=1, source_target_pairs={{16,0},{24,8},{32,16},{40,24},{48,32},{56,40},{64,48},{72,56},{80,... | collective-permute-start | bytes 3145736 | tf_op jit(solution)/shard_map/ppermute | solution.py:23
  19.8 93.5 %collective-permute-start.5 = (bf16[2,128,2048]{1,2,0:T(8,128)(2,1)S(1)}, bf16[2,128,2048]{1,2,0:T(8,128)(2,1)S(1)}, u32[]{:S(2)}, u32[]{:S(2)}) collective-permute-start(bf16[2,128,2048]{1,2,0:T(8,128)(2,1)S(1)} %collective-permute-done), channel_id=1, source_target_pairs={{24,0},{32,8},{40,16},{48,24},{56,32},{64,40},{72,48},{80,56},{88,... | collective-permute-start | bytes 3145736 | tf_op jit(solution)/shard_map/ppermute | solution.py:23
  42.7 70.9 %collective-permute-start.6 = (bf16[2,128,2048]{1,2,0:T(8,128)(2,1)S(1)}, bf16[2,128,2048]{1,2,0:T(8,128)(2,1)S(1)}, u32[]{:S(2)}, u32[]{:S(2)}) collective-permute-start(bf16[2,128,2048]{1,2,0:T(8,128)(2,1)S(1)} %collective-permute-done), channel_id=1, source_target_pairs={{32,0},{40,8},{48,16},{56,24},{64,32},{72,40},{80,48},{88,56},{96,... | collective-permute-start | bytes 3145736 | tf_op jit(solution)/shard_map/ppermute | solution.py:23
  91.5 22.3 %copy-start.56 = (f32[2,32]{1,0:T(2,128)S(1)}, f32[2,32]{1,0:T(2,128)}, u32[]{:S(2)}) copy-start(f32[2,32]{1,0:T(2,128)} %param.6) | copy-start | bytes 772
  91.6 22.3 %copy-start.82 = (s32[1,2,8]{2,1,0:T(2,128)S(1)}, s32[1,2,8]{2,1,0:T(2,128)}, u32[]{:S(2)}) copy-start(s32[1,2,8]{2,1,0:T(2,128)} %param.7) | copy-start | bytes 196
  117.5 0.5 copy-start.106
  121.3 143.3 %collective-permute-start.12 = (bf16[2,128,2048]{1,2,0:T(8,128)(2,1)S(1)}, bf16[2,128,2048]{1,2,0:T(8,128)(2,1)S(1)}, u32[]{:S(2)}, u32[]{:S(2)}) collective-permute-start(bf16[2,128,2048]{1,2,0:T(8,128)(2,1)S(1)} %get-tuple-element.147), channel_id=1, source_target_pairs={{0,32},{8,40},{16,48},{24,56},{32,64},{40,72},{48,80},{56,88},{64,... | collective-permute-start | bytes 3145736 | tf_op jit(solution)/shard_map/ppermute | solution.py:23
  224.8 53.8 %collective-permute-start.11 = (bf16[2,128,2048]{1,2,0:T(8,128)(2,1)S(1)}, bf16[2,128,2048]{1,2,0:T(8,128)(2,1)S(1)}, u32[]{:S(2)}, u32[]{:S(2)}) collective-permute-start(bf16[2,128,2048]{1,2,0:T(8,128)(2,1)S(1)} %get-tuple-element.148), channel_id=1, source_target_pairs={{0,24},{8,32},{16,40},{24,48},{32,56},{40,64},{48,72},{56,80},{64,... | collective-permute-start | bytes 3145736 | tf_op jit(solution)/shard_map/ppermute | solution.py:23
  226.2 63.7 %collective-permute-start.10 = (bf16[2,128,2048]{1,2,0:T(8,128)(2,1)S(1)}, bf16[2,128,2048]{1,2,0:T(8,128)(2,1)S(1)}, u32[]{:S(2)}, u32[]{:S(2)}) collective-permute-start(bf16[2,128,2048]{1,2,0:T(8,128)(2,1)S(1)} %get-tuple-element.149), channel_id=1, source_target_pairs={{0,16},{8,24},{16,32},{24,40},{32,48},{40,56},{48,64},{56,72},{64,... | collective-permute-start | bytes 3145736 | tf_op jit(solution)/shard_map/ppermute | solution.py:23
  261.9 39.2 %collective-permute-start.9 = (bf16[2,128,2048]{1,2,0:T(8,128)(2,1)S(1)}, bf16[2,128,2048]{1,2,0:T(8,128)(2,1)S(1)}, u32[]{:S(2)}, u32[]{:S(2)}) collective-permute-start(bf16[2,128,2048]{1,2,0:T(8,128)(2,1)S(1)} %get-tuple-element.150), channel_id=1, source_target_pairs={{0,8},{8,16},{16,24},{24,32},{32,40},{40,48},{48,56},{56,64},{64,7... | collective-permute-start | bytes 3145736 | tf_op jit(solution)/shard_map/ppermute | solution.py:23
  263.3 37.8 %collective-permute-start.8 = (bf16[2,128,2048]{1,2,0:T(8,128)(2,1)S(1)}, bf16[2,128,2048]{1,2,0:T(8,128)(2,1)S(1)}, u32[]{:S(2)}, u32[]{:S(2)}) collective-permute-start(bf16[2,128,2048]{1,2,0:T(8,128)(2,1)S(1)} %get-tuple-element.151), channel_id=1, source_target_pairs={{8,0},{16,8},{24,16},{32,24},{40,32},{48,40},{56,48},{64,56},{72,6... | collective-permute-start | bytes 3145736 | tf_op jit(solution)/shard_map/ppermute | solution.py:23
  264.6 50.4 %collective-permute-start.7 = (bf16[2,128,2048]{1,2,0:T(8,128)(2,1)S(1)}, bf16[2,128,2048]{1,2,0:T(8,128)(2,1)S(1)}, u32[]{:S(2)}, u32[]{:S(2)}) collective-permute-start(bf16[2,128,2048]{1,2,0:T(8,128)(2,1)S(1)} %get-tuple-element.146), channel_id=1, source_target_pairs={{16,0},{24,8},{32,16},{40,24},{48,32},{56,40},{64,48},{72,56},{80,... | collective-permute-start | bytes 3145736 | tf_op jit(solution)/shard_map/ppermute | solution.py:23
  318.1 97.8 %collective-permute-start.13 = (bf16[2,128,2048]{1,2,0:T(8,128)(2,1)}, bf16[2,128,2048]{1,2,0:T(8,128)(2,1)S(1)}, u32[]{:S(2)}, u32[]{:S(2)}) collective-permute-start(bf16[2,128,2048]{1,2,0:T(8,128)(2,1)} %add_convert_fusion), channel_id=1, source_target_pairs={{128,0},{129,1},{130,2},{131,3},{132,4},{133,5},{134,6},{135,7},{1... | collective-permute-start | bytes 3145736 | tf_op jit(solution)/shard_map/ppermute | solution.py:23
  416.0 1.4 copy-start.20
  416.1 1.7 copy-start.107
where the time goes:
time: 763 us; the launch traced here: 762 us
  blocking collectives  343 us (45%)
  waiting for transfers between devices  233 us (31%)
  starting transfers between devices  164 us (21%)
  local copies, waits for them, and re-layouts  16.6 us (2%)
    psum x1, blocking collectives, local(): gain_total = lax.psum(chosen_term, ('seq', 'dp')) / math.sqrt(token_total)  343 us
    ppermute x14, waiting for transfers between devices, passed_along(): lax.ppermute(value, axis, [(source, source + steps) for source in range(i...  233 us
    ppermute x14, starting transfers between devices, passed_along(): lax.ppermute(value, axis, [(source, source + steps) for source in range(i...  164 us
  transfers between devices with their start and end apart: 14, of which 10 were waited for; matrix products, arithmetic and copies ran while one was open for 1% of the time, Pallas kernels for 0%

commit v1 on v0

--- a/solution.py
+++ b/solution.py
@@ -9,8 +9,8 @@
 ENC_MOST = 4
 BLK_DEV = 1
 REACH_LOW = 2
-REACH_HIGH = 4
-WINDOW = 7
+REACH_HIGH = 3
+WINDOW = 6
 
 
 masked_score = -1e30
@@ -21,6 +21,13 @@
     count = lax.axis_size(axis)
     initial, last = (max(0, -steps), min(count, count - steps))
     return lax.ppermute(value, axis, [(source, source + steps) for source in range(initial, last)])
+
+
+def decoder_along(value, steps):
+    count = lax.axis_size("seq")
+    initial, last = (max(0, -steps), min(count, count - steps))
+    pairs = [(count + source, count + source + steps) for source in range(initial, last)]
+    return lax.ppermute(value, ("phase", "seq"), pairs)
 
 
 def segment_of(block_ids, block_sizes, block_total):
@@ -125,7 +132,7 @@
         if offset == 0:
             pieces.append(arrived)
         else:
-            pieces.append(passed_along(arrived, "seq", -offset))
+            pieces.append(decoder_along(arrived, -offset))
     window = jnp.concatenate(pieces, axis=1)
     window_rows = window.shape[1]
 
@@ -193,7 +200,7 @@
         if offset == 0:
             summed_grads = summed_grads + portion.astype(jnp.float32)
         else:
-            summed_grads = summed_grads + passed_along(portion, "seq", offset).astype(jnp.float32)
+            summed_grads = summed_grads + decoder_along(portion, offset).astype(jnp.float32)
     returned = passed_along(summed_grads.astype(jnp.bfloat16), "phase", -1)
     value_heads = local_pair[1].reshape(tok_dev, head_count, -1)
     value_grad_heads = returned[1].reshape(tok_dev, head_count, -1)
@@ -203,7 +210,11 @@
     )
     chosen_term = jnp.where(phase_index == 0, value_term, gain_term)
     token_total = tok_dev * lax.axis_size("seq") * lax.axis_size("dp")
-    gain_total = lax.psum(chosen_term, ("seq", "dp")) / math.sqrt(token_total)
+    slots = jnp.where(
+        jnp.arange(2, dtype=jnp.int32)[:, None] == phase_index, chosen_term[None, :], 0.0
+    )
+    summed = lax.psum(slots, ("phase", "seq", "dp"))
+    gain_total = lax.dynamic_index_in_dim(summed, phase_index, 0, keepdims=False) / math.sqrt(token_total)
     result = jnp.where(phase_index == 0, returned, produced)[None]
     return (result, gain_total[None])
 

time: 763 us -> 358 us (0.47)
  blocking collectives: 343 us -> 87.7 us
  starting transfers between devices: 164 us -> 13.3 us
    psum x1, blocking collectives: 343 us -> 87.7 us  [local(): summed = lax.psum(slots, ('phase', 'seq', 'dp'))]
    ppermute x14 -> x2, starting transfers between devices: 164 us -> 3.1 us  [passed_along(): lax.ppermute(value, axis, [(source, source + steps) for source in range(i...]
    ppermute x0 -> x10, starting transfers between devices: none -> 10.2 us  [decoder_along(): return lax.ppermute(value, ('phase', 'seq'), pairs)]
    ppermute x14 -> x2, waiting for transfers between devices: 233 us -> 232 us  [passed_along(): lax.ppermute(value, axis, [(source, source + steps) for source in range(i...]
  transfers between devices with their start and end apart: 14 -> 12, of which waited for: 10 -> 2; matrix products, arithmetic and copies ran while one was open for 1% -> 1% of each run, Pallas kernels for 0% -> 0%
where the time goes in v1:
time: 358 us; the launch traced here: 353 us
  waiting for transfers between devices  232 us (65%)
  blocking collectives  87.7 us (24%)
  local copies, waits for them, and re-layouts  16 us (4%)
  starting transfers between devices  13.3 us (4%)
    ppermute x2, waiting for transfers between devices, passed_along(): lax.ppermute(value, axis, [(source, source + steps) for source in range(i...  232 us
    psum x1, blocking collectives, local(): summed = lax.psum(slots, ('phase', 'seq', 'dp'))  87.7 us
    ppermute x10, starting transfers between devices, decoder_along(): return lax.ppermute(value, ('phase', 'seq'), pairs)  10.2 us
    unnamed x15, local copies, waits for them, and re-layouts  7.93 us
  transfers between devices with their start and end apart: 12, of which 2 were waited for; matrix products, arithmetic and copies ran while one was open for 1% of the time, Pallas kernels for 0%

profile of v1, /device:TPU:8, one launch (start us, length us, event | category | flops | bytes accessed | tf_op | source)
XLA Modules:
  0.0 353.1 jit_solution(16076811871537430861)
XLA Ops:
  0.6 1.6 copy.113
  2.3 0.0 copy-start
  2.3 1.8 collective-permute-start
  4.1 2.2 collective-permute-done
  6.3 1.6 collective-permute-start.1
  7.9 1.7 collective-permute-start.2
  9.6 1.6 collective-permute-start.3
  11.2 0.7 collective-permute-start.4
  12.0 0.7 collective-permute-start.5
  12.7 0.0 collective-permute-done.1
  12.7 1.4 constant_dynamic-update-slice_fusion.39
  14.1 0.0 collective-permute-done.2
  14.1 1.5 constant_dynamic-update-slice_fusion.38
  15.6 0.2 constant_dynamic-update-slice_fusion.37
  15.9 0.0 collective-permute-done.3
  15.9 1.5 constant_dynamic-update-slice_fusion.36
  17.4 0.0 copy-start.57
  17.4 0.0 copy-start.81
  17.4 0.0 collective-permute-done.4
  17.4 0.2 constant_dynamic-update-slice_fusion.35
  17.6 0.0 collective-permute-done.5
  17.7 0.2 constant_dynamic-update-slice_fusion.34
  17.9 0.1 copy-done.57
  18.0 0.0 copy-done.81
  18.1 0.0 copy-done
  18.1 4.8 %conditional.1 = (bf16[2,128,2048]{1,2,0:T(8,128)(2,1)}, bf16[2,768,2048]{1,2,0:T(8,128)(2,1)}, f32[32]{0:T(128)}) conditional(s32[]{:T(128)} %convert_element_type.141, () %tuple.16, (bf16[2,768,2048]{1,2,0:T(8,128)(2,1)S(1)}, s32[1,2,8]{2,1,0:T(2,128)S(1)}, s32[]{:T(128)}, bf16[2,128,2048]{1,2,0:T(8,128)(2,1)S(1)}, f32[2,32]{1,0:T(2,128)S(1)}) %tuple.116), branch_computations={%region_0.0_spmd, %region_1.30_spmd} | conditional | flops 2472034816 | bytes 240882752 | solution.py:194
  18.1 1.1 broadcast.201
  19.2 3.1 broadcast.202
  22.2 0.6 broadcast.203
  22.8 3.0 fusion.254
  25.8 0.7 collective-permute-start.10
  26.5 0.7 collective-permute-start.9
  27.2 0.7 collective-permute-start.8
  28.0 0.7 collective-permute-start.7
  28.7 0.0 copy-start.1
  28.7 0.9 collective-permute-start.6
  29.6 0.0 collective-permute-done.10
  29.6 0.0 collective-permute-done.9
  29.6 0.0 collective-permute-done.8
  29.6 0.0 collective-permute-done.7
  29.6 0.0 collective-permute-done.6
  29.6 2.0 add_convert_fusion
  31.7 1.3 collective-permute-start.11
  33.0 0.0 copy-done.1
  33.1 229.9 %collective-permute-done.11 = bf16[2,128,2048]{1,2,0:T(8,128)(2,1)S(1)} collective-permute-done((bf16[2,128,2048]{1,2,0:T(8,128)(2,1)S(1)}, bf16[2,128,2048]{1,2,0:T(8,128)(2,1)S(1)}, u32[]{:S(2)}, u32[]{:S(2)}) %collective-permute-start.11) | collective-permute-done | bytes 1048608 | tf_op jit(solution)/shard_map/ppermute | solution.py:23
  263.0 0.1 select_bitcast_fusion
  263.1 1.3 copy.115
  264.4 0.3 fusion.241
  264.8 0.1 broadcast_select_fusion.1
  264.9 87.7 %psum.7 = f32[2,32]{1,0:T(2,128)S(1)} all-reduce(f32[2,32]{1,0:T(2,128)S(1)} %broadcast_select_fusion.1), channel_id=1, replica_groups=mesh['phase'=2,'seq'=16,'dp'=8] {'phase','seq','dp'}, use_global_device_ids=true, to_apply=%region_30.31 | all-reduce | flops 64 | bytes 512 | tf_op jit(solution)/shard_map/psum | solution.py:216
  352.6 0.5 dynamic-slice_multiply_fusion
  (4 shorter events, 0.1 us)
Async XLA Ops:
  2.3 15.8 %copy-start = (bf16[1,2,128,2048]{2,3,1,0:T(8,128)(2,1)}, bf16[1,2,128,2048]{2,3,1,0:T(8,128)(2,1)S(1)}, u32[]{:S(2)}) copy-start(bf16[1,2,128,2048]{2,3,1,0:T(8,128)(2,1)S(1)} %copy.113) | copy-start | bytes 3145732
  2.3 4.0 %collective-permute-start = (bf16[2,128,2048]{1,2,0:T(8,128)(2,1)S(1)}, bf16[2,128,2048]{1,2,0:T(8,128)(2,1)S(1)}, u32[]{:S(2)}, u32[]{:S(2)}) collective-permute-start(bf16[2,128,2048]{1,2,0:T(8,128)(2,1)S(1)} %bitcast.559), channel_id=1, source_target_pairs={{0,128},{1,129},{2,130},{3,131},{4,132},{5,133},{6,134},{7,135},{8... | collective-permute-start | bytes 3145736 | tf_op jit(solution)/shard_map/ppermute | solution.py:23
  6.3 6.4 %collective-permute-start.1 = (bf16[2,128,2048]{1,2,0:T(8,128)(2,1)S(1)}, bf16[2,128,2048]{1,2,0:T(8,128)(2,1)}, u32[]{:S(2)}, u32[]{:S(2)}) collective-permute-start(bf16[2,128,2048]{1,2,0:T(8,128)(2,1)S(1)} %collective-permute-done), channel_id=1, source_target_pairs={{128,144},{136,152},{144,160},{152,168},{160,176},{168,184},{176,1... | collective-permute-start | bytes 3145736 | tf_op jit(solution)/shard_map/ppermute | solution.py:30
  7.9 6.2 %collective-permute-start.2 = (bf16[2,128,2048]{1,2,0:T(8,128)(2,1)S(1)}, bf16[2,128,2048]{1,2,0:T(8,128)(2,1)}, u32[]{:S(2)}, u32[]{:S(2)}) collective-permute-start(bf16[2,128,2048]{1,2,0:T(8,128)(2,1)S(1)} %collective-permute-done), channel_id=1, source_target_pairs={{128,136},{136,144},{144,152},{152,160},{160,168},{168,176},{176,1... | collective-permute-start | bytes 3145736 | tf_op jit(solution)/shard_map/ppermute | solution.py:30
  9.6 6.3 %collective-permute-start.3 = (bf16[2,128,2048]{1,2,0:T(8,128)(2,1)S(1)}, bf16[2,128,2048]{1,2,0:T(8,128)(2,1)}, u32[]{:S(2)}, u32[]{:S(2)}) collective-permute-start(bf16[2,128,2048]{1,2,0:T(8,128)(2,1)S(1)} %collective-permute-done), channel_id=1, source_target_pairs={{136,128},{144,136},{152,144},{160,152},{168,160},{176,168},{184,1... | collective-permute-start | bytes 3145736 | tf_op jit(solution)/shard_map/ppermute | solution.py:30
  11.2 6.1 %collective-permute-start.4 = (bf16[2,128,2048]{1,2,0:T(8,128)(2,1)S(1)}, bf16[2,128,2048]{1,2,0:T(8,128)(2,1)S(1)}, u32[]{:S(2)}, u32[]{:S(2)}) collective-permute-start(bf16[2,128,2048]{1,2,0:T(8,128)(2,1)S(1)} %collective-permute-done), channel_id=1, source_target_pairs={{144,128},{152,136},{160,144},{168,152},{176,160},{184,168},{192,1... | collective-permute-start | bytes 3145736 | tf_op jit(solution)/shard_map/ppermute | solution.py:30
  12.0 5.7 %collective-permute-start.5 = (bf16[2,128,2048]{1,2,0:T(8,128)(2,1)S(1)}, bf16[2,128,2048]{1,2,0:T(8,128)(2,1)S(1)}, u32[]{:S(2)}, u32[]{:S(2)}) collective-permute-start(bf16[2,128,2048]{1,2,0:T(8,128)(2,1)S(1)} %collective-permute-done), channel_id=1, source_target_pairs={{152,128},{160,136},{168,144},{176,152},{184,160},{192,168},{200,1... | collective-permute-start | bytes 3145736 | tf_op jit(solution)/shard_map/ppermute | solution.py:30
  17.4 0.7 copy-start.57
  17.4 0.7 copy-start.81
  25.8 3.8 %collective-permute-start.10 = (bf16[2,128,2048]{1,2,0:T(8,128)(2,1)S(1)}, bf16[2,128,2048]{1,2,0:T(8,128)(2,1)S(1)}, u32[]{:S(2)}, u32[]{:S(2)}) collective-permute-start(bf16[2,128,2048]{1,2,0:T(8,128)(2,1)S(1)} %get-tuple-element.147), channel_id=1, source_target_pairs={{128,152},{136,160},{144,168},{152,176},{160,184},{168,192},{176,2... | collective-permute-start | bytes 3145736 | tf_op jit(solution)/shard_map/ppermute | solution.py:30
  26.5 3.1 collective-permute-start.9
  27.2 2.4 collective-permute-start.8
  28.0 1.6 collective-permute-start.7
  28.7 4.3 %copy-start.1 = (bf16[1,2,128,2048]{2,3,1,0:T(8,128)(2,1)S(1)}, bf16[1,2,128,2048]{2,3,1,0:T(8,128)(2,1)}, u32[]{:S(2)}) copy-start(bf16[1,2,128,2048]{2,3,1,0:T(8,128)(2,1)} %copy-done) | copy-start | bytes 3145732
  28.7 0.9 collective-permute-start.6
  31.7 231.3 %collective-permute-start.11 = (bf16[2,128,2048]{1,2,0:T(8,128)(2,1)S(1)}, bf16[2,128,2048]{1,2,0:T(8,128)(2,1)S(1)}, u32[]{:S(2)}, u32[]{:S(2)}) collective-permute-start(bf16[2,128,2048]{1,2,0:T(8,128)(2,1)S(1)} %add_convert_fusion), channel_id=1, source_target_pairs={{128,0},{129,1},{130,2},{131,3},{132,4},{133,5},{134,6},{135,7},{1... | collective-permute-start | bytes 3145736 | tf_op jit(solution)/shard_map/ppermute | solution.py:23

commit v2 on v1

--- a/solution.py
+++ b/solution.py
@@ -3,6 +3,8 @@
 import jax
 import jax.numpy as jnp
 from jax import lax
+from jax.experimental import pallas as pl
+from jax.experimental.pallas import tpu as pltpu
 from jax.sharding import PartitionSpec as P
 
 BLOCK = 128
@@ -17,10 +19,114 @@
 heads_per_pass = 4
 
 
+def attention_kernel(gains_ref, q_ref, do_ref, k_ref, v_ref, allow_ref,
+                     att_ref, dq_ref, dk_ref, dv_ref, gain_ref):
+    pair = pl.program_id(0)
+    width = q_ref.shape[1]
+    half = width // 2
+    inv_root = 1.0 / math.sqrt(half)
+    q = q_ref[...]
+    do = do_ref[...]
+    k = k_ref[...]
+    v = v_ref[...]
+    allowed = allow_ref[...] > 0
+    lane = lax.broadcasted_iota(jnp.int32, (1, width), 1)
+    first = lane < half
+    zero_q = jnp.zeros_like(q)
+    att_f = []
+    p_lows = []
+    raws = []
+    chances_all = []
+    for j in range(2):
+        head = pair * 2 + j
+        g_logit = gains_ref[0, head]
+        g_value = gains_ref[1, head]
+        mine = first if j == 0 else jnp.logical_not(first)
+        q_h = jnp.where(mine, q, zero_q)
+        raw = lax.dot_general(q_h, k, (((1,), (1,)), ((), ())), preferred_element_type=jnp.float32) * inv_root
+        logits = jnp.where(allowed, g_logit * raw, masked_score)
+        top = jnp.max(logits, axis=1, keepdims=True)
+        lifted = jnp.exp(logits - top)
+        chances = lifted / jnp.sum(lifted, axis=1, keepdims=True)
+        p_low = chances.astype(jnp.bfloat16)
+        att_full = jnp.dot(p_low, v, preferred_element_type=jnp.float32) * g_value
+        att_f.append(att_full)
+        p_lows.append(p_low)
+        raws.append(raw)
+        chances_all.append(chances)
+    attended = jnp.where(first, att_f[0], att_f[1]).astype(jnp.bfloat16)
+    att_ref[...] = attended
+    prod = do.astype(jnp.float32) * attended.astype(jnp.float32)
+    dq_parts, dk_parts, dv_parts, gain_vals = [], [], [], []
+    zero_do = jnp.zeros_like(do)
+    for j in range(2):
+        head = pair * 2 + j
+        g_logit = gains_ref[0, head]
+        g_value = gains_ref[1, head]
+        mine = first if j == 0 else jnp.logical_not(first)
+        do_h = jnp.where(mine, do, zero_do)
+        slope = lax.dot_general(do_h, v, (((1,), (1,)), ((), ())), preferred_element_type=jnp.float32) * g_value
+        carried = jnp.sum(jnp.where(mine, prod, 0.0), axis=1, keepdims=True)
+        score_grad = chances_all[j] * (slope - carried)
+        score_low = score_grad.astype(jnp.bfloat16)
+        factor = g_logit * inv_root
+        dq_parts.append(jnp.dot(score_low, k, preferred_element_type=jnp.float32) * factor)
+        dk_parts.append(lax.dot_general(score_low, q, (((0,), (0,)), ((), ())), preferred_element_type=jnp.float32) * factor)
+        dv_parts.append(lax.dot_general(p_lows[j], do, (((0,), (0,)), ((), ())), preferred_element_type=jnp.float32) * g_value)
+        gain_vals.append(jnp.sum(score_grad * raws[j]))
+    dq_ref[...] = jnp.where(first, dq_parts[0], dq_parts[1]).astype(dq_ref.dtype)
+    dk_ref[...] = jnp.where(first, dk_parts[0], dk_parts[1]).astype(dk_ref.dtype)
+    dv_ref[...] = jnp.where(first, dv_parts[0], dv_parts[1]).astype(dv_ref.dtype)
+    glane = lax.broadcasted_iota(jnp.int32, gain_ref.shape, 2)
+    gain_ref[...] = jnp.where(glane == 0, gain_vals[0], jnp.where(glane == 1, gain_vals[1], 0.0))
+
+
+def attention_block(q, do, k, v, allowed_keys, head_gains):
+    rows, inner = q.shape
+    keys = k.shape[0]
+    head_count = head_gains.shape[1]
+    width = 2 * (inner // head_count)
+    pairs = inner // width
+    row_spec = pl.BlockSpec((rows, width), lambda i, g: (0, i))
+    key_spec = pl.BlockSpec((keys, width), lambda i, g: (0, i))
+    grid_spec = pltpu.PrefetchScalarGridSpec(
+        num_scalar_prefetch=1,
+        grid=(pairs,),
+        in_specs=[row_spec, row_spec, key_spec, key_spec, pl.BlockSpec((1, keys), lambda i, g: (0, 0))],
+        out_specs=[row_spec, row_spec, key_spec, key_spec, pl.BlockSpec((1, 8, 128), lambda i, g: (i, 0, 0))],
+    )
+    flops = 2 * rows * keys * width * 6 * pairs * 2
+    cost = pl.CostEstimate(flops=flops, transcendentals=rows * keys * head_count,
+                           bytes_accessed=2 * (4 * rows * inner + 4 * keys * inner))
+    att, dq, dk, dv, gains = pl.pallas_call(
+        attention_kernel,
+        grid_spec=grid_spec,
+        out_shape=[
+            jax.ShapeDtypeStruct((rows, inner), jnp.bfloat16),
+            jax.ShapeDtypeStruct((rows, inner), jnp.bfloat16),
+            jax.ShapeDtypeStruct((keys, inner), jnp.bfloat16),
+            jax.ShapeDtypeStruct((keys, inner), jnp.bfloat16),
+            jax.ShapeDtypeStruct((pairs, 8, 128), jnp.float32),
+        ],
+        cost_estimate=cost,
+    )(head_gains, q, do, k, v, allowed_keys.astype(jnp.int32)[None, :])
+    gain_term = gains[:, 0, :2].reshape(-1)
+    return att, dq, dk, dv, gain_term
+
+
 def passed_along(value, axis, steps):
     count = lax.axis_size(axis)
     initial, last = (max(0, -steps), min(count, count - steps))
     return lax.ppermute(value, axis, [(source, source + steps) for source in range(initial, last)])
+
+
+def butterfly_sum(value, axis):
+    count = lax.axis_size(axis)
+    stride = 1
+    while stride < count:
+        value = value + lax.ppermute(value, axis, [(i, i ^ stride) for i in range(count)])
+        stride *= 2
+    return value
 
 
 def decoder_along(value, steps):
@@ -144,44 +250,25 @@
         dec_blocks = shard_index * BLK_DEV + jnp.arange(BLK_DEV, dtype=jnp.int32)
         dec_segs = segment_of(dec_blocks, dec_counts, block_total)
         enc_starts = jnp.cumsum(enc_counts) - enc_counts
-        key_sum = jnp.zeros((window_rows, inner_width), jnp.float32)
-        value_sum = jnp.zeros((window_rows, inner_width), jnp.float32)
-        gain_term = jnp.zeros((head_count,), jnp.float32)
         segment = dec_segs[0]
         start_block = jnp.clip(enc_starts[segment] - first_block, 0, WINDOW * BLK_DEV - ENC_MOST)
         slice_segs = lax.dynamic_slice_in_dim(enc_segs, start_block, ENC_MOST)
-        allowed = jnp.broadcast_to(
-            jnp.repeat(slice_segs == segment, BLOCK)[None, :], (BLOCK, ENC_MOST * BLOCK)
-        )
+        allowed_keys = jnp.repeat(slice_segs == segment, BLOCK)
         key_slice = lax.dynamic_slice_in_dim(
             window_pair[0], start_block * BLOCK, ENC_MOST * BLOCK, 0
         )
         value_slice = lax.dynamic_slice_in_dim(
             window_pair[1], start_block * BLOCK, ENC_MOST * BLOCK, 0
         )
-        attended, query_grad, key_grad, value_grad, block_gain = head_passes(
-            own_pair[0, 0:BLOCK], own_pair[1, 0:BLOCK], key_slice, value_slice, allowed, head_gains
+        attended, query_grad, key_grad, value_grad, gain_term = attention_block(
+            own_pair[0, 0:BLOCK], own_pair[1, 0:BLOCK], key_slice, value_slice, allowed_keys, head_gains
         )
         write_at = start_block * BLOCK
-        key_sum = lax.dynamic_update_slice_in_dim(
-            key_sum,
-            lax.dynamic_slice_in_dim(key_sum, write_at, ENC_MOST * BLOCK, 0) + key_grad,
-            write_at,
-            0,
-        )
-        value_sum = lax.dynamic_update_slice_in_dim(
-            value_sum,
-            lax.dynamic_slice_in_dim(value_sum, write_at, ENC_MOST * BLOCK, 0) + value_grad,
-            write_at,
-            0,
-        )
-        attended_rows = [attended]
-        query_rows = [query_grad.astype(jnp.bfloat16)]
-        gain_term = gain_term + block_gain
-        produced = jnp.stack(
-            [jnp.concatenate(attended_rows, axis=0), jnp.concatenate(query_rows, axis=0)]
-        )
-        window_grads = jnp.stack([key_sum.astype(jnp.bfloat16), value_sum.astype(jnp.bfloat16)])
+        grads = jnp.stack([key_grad, value_grad])
+        window_grads = lax.dynamic_update_slice_in_dim(
+            jnp.zeros((2, window_rows, inner_width), jnp.bfloat16), grads, write_at, 1
+        )
+        produced = jnp.stack([attended, query_grad])
         return (produced, window_grads, gain_term)
 
     def encoder_rest(operands):
@@ -210,11 +297,8 @@
     )
     chosen_term = jnp.where(phase_index == 0, value_term, gain_term)
     token_total = tok_dev * lax.axis_size("seq") * lax.axis_size("dp")
-    slots = jnp.where(
-        jnp.arange(2, dtype=jnp.int32)[:, None] == phase_index, chosen_term[None, :], 0.0
-    )
-    summed = lax.psum(slots, ("phase", "seq", "dp"))
-    gain_total = lax.dynamic_index_in_dim(summed, phase_index, 0, keepdims=False) / math.sqrt(token_total)
+    summed = butterfly_sum(butterfly_sum(chosen_term, "dp"), "seq")
+    gain_total = summed / math.sqrt(token_total)
     result = jnp.where(phase_index == 0, returned, produced)[None]
     return (result, gain_total[None])
 

time: 358 us -> 264 us (0.74)
  blocking collectives: 87.7 us -> 0 us
  waiting for transfers between devices: 232 us -> 174 us
  starting transfers between devices: 13.3 us -> 54.1 us
  local copies, waits for them, and re-layouts: 16 us -> 28.9 us
    psum x1 -> x0, blocking collectives: 87.7 us -> none  [local(): summed = lax.psum(slots, ('phase', 'seq', 'dp'))]
    ppermute x2, waiting for transfers between devices: 232 us -> 163 us  [passed_along(): lax.ppermute(value, axis, [(source, source + steps) for source in range(i...]
    ppermute x0 -> x7, starting transfers between devices: none -> 40.7 us  [butterfly_sum(): lax.ppermute(value, axis, [(i, i ^ stride) for i in range(count)])]
    ppermute x0 -> x7, waiting for transfers between devices: none -> 11 us  [butterfly_sum(): lax.ppermute(value, axis, [(i, i ^ stride) for i in range(count)])]
    cond x0 -> x1, local copies, waits for them, and re-layouts: none -> 8.66 us  [local(): lax.cond(phase_index == 1, decoder_work, encoder_rest, (local_pair, window))]
    unnamed x15 -> x13, local copies, waits for them, and re-layouts: 7.93 us -> 11.8 us
  transfers between devices with their start and end apart: 12 -> 19, of which waited for: 2 -> 9; matrix products, arithmetic and copies ran while one was open for 1% -> 5% of each run, Pallas kernels for 0% -> 0%
where the time goes in v2:
time: 264 us; the launch traced here: 262 us
  waiting for transfers between devices  174 us (66%)
  starting transfers between devices  54.1 us (20%)
  local copies, waits for them, and re-layouts  28.9 us (11%)
  other arithmetic  3.99 us (2%)
    ppermute x2, waiting for transfers between devices, passed_along(): lax.ppermute(value, axis, [(source, source + steps) for source in range(i...  163 us
    ppermute x7, starting transfers between devices, butterfly_sum(): lax.ppermute(value, axis, [(i, i ^ stride) for i in range(count)])  40.7 us
    unnamed x13, local copies, waits for them, and re-layouts  11.8 us
    ppermute x7, waiting for transfers between devices, butterfly_sum(): lax.ppermute(value, axis, [(i, i ^ stride) for i in range(count)])  11 us
    ppermute x10, starting transfers between devices, decoder_along(): return lax.ppermute(value, ('phase', 'seq'), pairs)  10.3 us
    cond x1, local copies, waits for them, and re-layouts, local(): lax.cond(phase_index == 1, decoder_work, encoder_rest, (local_pair, window))  8.66 us
  transfers between devices with their start and end apart: 19, of which 9 were waited for; matrix products, arithmetic and copies ran while one was open for 5% of the time, Pallas kernels for 0%

profile of v2, /device:TPU:8, one launch (start us, length us, event | category | flops | bytes accessed | tf_op | source)
XLA Modules:
  0.0 261.7 jit_solution(14917463768572843430)
XLA Ops:
  0.6 1.8 collective-permute-start
  2.4 2.4 collective-permute-done
  4.9 1.7 collective-permute-start.1
  6.6 1.7 collective-permute-start.2
  8.2 1.7 collective-permute-start.3
  9.9 0.7 collective-permute-start.4
  10.6 0.0 copy-start
  10.7 0.0 copy-start.3
  10.7 0.0 copy-start.4
  10.7 0.9 collective-permute-start.5
  11.5 0.0 collective-permute-done.1
  11.6 2.3 constant_dynamic-update-slice_fusion.5
  13.9 0.0 collective-permute-done.2
  13.9 2.3 constant_dynamic-update-slice_fusion.4
  16.2 1.1 constant_dynamic-update-slice_fusion.3
  17.3 0.0 collective-permute-done.3
  17.3 2.3 constant_dynamic-update-slice_fusion.2
  19.6 0.0 collective-permute-done.4
  19.6 1.1 constant_dynamic-update-slice_fusion.1
  20.7 0.0 collective-permute-done.5
  20.7 1.1 constant_dynamic-update-slice_fusion
  21.8 0.0 copy-done
  21.8 0.0 copy-done.3
  21.8 0.0 copy-done.4
  21.8 3.6 %conditional.1 = (bf16[2,768,2048]{2,1,0:T(8,128)(2,1)}, f32[32]{0:T(128)S(1)}, bf16[2,128,2048]{1,2,0:T(8,128)(2,1)S(1)}) conditional(s32[]{:T(128)} %convert_element_type.45, () %tuple.16, (bf16[2,128,2048]{2,1,0:T(8,128)(2,1)S(1)}, bf16[2,768,2048]{2,1,0:T(8,128)(2,1)}, s32[1,2,8]{2,1,0:T(2,128)S(1)}, s32[]{:T(128)}, f32[2,32]{1,0:T(2,128)S(1)}) %tuple.36), branch_computations={%region_0.0_spmd, %region_1.6_spmd} | conditional | flops 3230138624 | bytes 69209496 | solution.py:281
  21.8 3.4 %broadcast.26 = bf16[2,768,2048]{2,1,0:T(8,128)(2,1)} broadcast(bf16[]{:T(256)} %constant.23.clone), dimensions={} | broadcast | bytes 6291458 | tf_op jit(solution)/shard_map/broadcast.4
  25.2 0.1 broadcast.25.clone
  25.4 8.7 %copy.15 = bf16[2,768,2048]{1,2,0:T(8,128)(2,1)} copy(bf16[2,768,2048]{2,1,0:T(8,128)(2,1)} %get-tuple-element.30) | data formatting | bytes 12582912 | tf_op jit(solution)/shard_map/cond | solution.py:281
  34.0 3.0 %fusion.3 = (bf16[2,128,2048]{1,2,0:T(8,128)(2,1)S(1)}, bf16[2,128,2048]{1,2,0:T(8,128)(2,1)S(1)}, bf16[2,128,2048]{1,2,0:T(8,128)(2,1)S(1)}, bf16[2,128,2048]{1,2,0:T(8,128)(2,1)S(1)}, bf16[2,128,2048]{1,2,0:T(8,128)(2,1)S(1)}) fusion(bf16[2,768,2048]{1,2,0:T(8,128)(2,1)} %copy.15), kind=kLoop, calls=%fused_computation.31 | loop fusion | bytes 10485760 | tf_op jit(solution)/shard_map/slice | solution.py:286
  37.0 0.7 collective-permute-start.10
  37.7 0.7 collective-permute-start.6
  38.5 0.7 collective-permute-start.7
  39.2 0.7 collective-permute-start.8
  39.9 0.7 collective-permute-start.9
  40.7 0.0 collective-permute-done.10
  40.7 0.0 collective-permute-done.6
  40.7 0.0 collective-permute-done.7
  40.7 0.0 collective-permute-done.8
  40.7 0.0 collective-permute-done.9
  40.7 3.0 %add_convert_fusion = bf16[2,128,2048]{1,2,0:T(8,128)(2,1)} fusion(bf16[2,128,2048]{1,2,0:T(8,128)(2,1)S(1)} %collective-permute-done.10, bf16[2,128,2048]{1,2,0:T(8,128)(2,1)S(1)} %collective-permute-done.9, bf16[2,128,2048]{1,2,0:T(8,128)(2,1)S(1)} %collective-permute-done.8, bf16[2,128,2048]{1,2,0:T(8,128)(2,1)S(1)} %collective-permute-done.7, ...), kind=kLoop, calls=%fused_computation.17 | loop fusion | flops 6291456 | bytes 7340032 | tf_op jit(solution)/shard_map/convert_element_type | solution.py:291
  43.7 1.3 collective-permute-start.11
  45.0 0.8 slice.58
  45.9 1.3 copy.33
  47.2 160.4 %collective-permute-done.11 = bf16[2,128,2048]{1,2,0:T(8,128)(2,1)S(1)} collective-permute-done((bf16[2,128,2048]{1,2,0:T(8,128)(2,1)}, bf16[2,128,2048]{1,2,0:T(8,128)(2,1)S(1)}, u32[]{:S(2)}, u32[]{:S(2)}) %collective-permute-start.11) | collective-permute-done | bytes 1048608 | tf_op jit(solution)/shard_map/ppermute | solution.py:120
  207.7 0.3 fusion.1
  208.0 1.2 collective-permute-start.12
  209.2 2.4 collective-permute-done.12
  211.6 1.6 collective-permute-start.13
  213.3 1.9 collective-permute-done.13
  215.2 3.2 %collective-permute-start.14 = (f32[32]{0:T(128)S(1)}, f32[32]{0:T(128)S(1)}, u32[]{:S(2)}, u32[]{:S(2)}) collective-permute-start(f32[32]{0:T(128)S(1)} %add.67), channel_id=1, source_target_pairs={{0,4},{1,5},{2,6},{3,7},{4,0},{5,1},{6,2},{7,3},{8,12},{9,13},{10,... | collective-permute-start | bytes 392 | tf_op jit(solution)/shard_map/ppermute | solution.py:127
  218.4 1.9 collective-permute-done.14
  220.3 7.4 %collective-permute-start.15 = (f32[32]{0:T(128)S(1)}, f32[32]{0:T(128)S(1)}, u32[]{:S(2)}, u32[]{:S(2)}) collective-permute-start(f32[32]{0:T(128)S(1)} %add.68), channel_id=1, source_target_pairs={{0,8},{8,0},{16,24},{24,16},{32,40},{40,32},{48,56},{56,48},{64,72... | collective-permute-start | bytes 392 | tf_op jit(solution)/shard_map/ppermute | solution.py:127
  227.7 1.5 collective-permute-done.15
  229.3 13.6 %collective-permute-start.16 = (f32[32]{0:T(128)S(1)}, f32[32]{0:T(128)S(1)}, u32[]{:S(2)}, u32[]{:S(2)}) collective-permute-start(f32[32]{0:T(128)S(1)} %add.69), channel_id=1, source_target_pairs={{0,16},{8,24},{16,0},{24,8},{32,48},{40,56},{48,32},{56,40},{64,80... | collective-permute-start | bytes 392 | tf_op jit(solution)/shard_map/ppermute | solution.py:127
  242.8 1.5 collective-permute-done.16
  244.4 6.7 %collective-permute-start.17 = (f32[32]{0:T(128)S(1)}, f32[32]{0:T(128)S(1)}, u32[]{:S(2)}, u32[]{:S(2)}) collective-permute-start(f32[32]{0:T(128)S(1)} %add.70), channel_id=1, source_target_pairs={{0,32},{8,40},{16,48},{24,56},{32,0},{40,8},{48,16},{56,24},{64,96... | collective-permute-start | bytes 392 | tf_op jit(solution)/shard_map/ppermute | solution.py:127
  251.0 1.5 collective-permute-done.17
  252.6 7.0 %collective-permute-start.18 = (f32[32]{0:T(128)S(1)}, f32[32]{0:T(128)S(1)}, u32[]{:S(2)}, u32[]{:S(2)}) collective-permute-start(f32[32]{0:T(128)S(1)} %add.71), channel_id=1, source_target_pairs={{0,64},{8,72},{16,80},{24,88},{32,96},{40,104},{48,112},{56,120},{... | collective-permute-start | bytes 392 | tf_op jit(solution)/shard_map/ppermute | solution.py:127
  259.6 0.1 select_bitcast_fusion
  259.7 1.3 copy.23
  261.0 0.1 collective-permute-done.18
  261.2 0.5 multiply_bitcast_fusion
  (9 shorter events, 0.1 us)
Async XLA Ops:
  0.6 4.2 %collective-permute-start = (bf16[2,128,2048]{2,1,0:T(8,128)(2,1)}, bf16[2,128,2048]{2,1,0:T(8,128)(2,1)S(1)}, u32[]{:S(2)}, u32[]{:S(2)}) collective-permute-start(bf16[2,128,2048]{2,1,0:T(8,128)(2,1)} %bitcast.43), channel_id=1, source_target_pairs={{0,128},{1,129},{2,130},{3,131},{4,132},{5,133},{6,134},{7,135},{8... | collective-permute-start | bytes 3145736 | tf_op jit(solution)/shard_map/ppermute | solution.py:120
  4.9 6.7 %collective-permute-start.1 = (bf16[2,128,2048]{2,1,0:T(8,128)(2,1)S(1)}, bf16[2,128,2048]{2,1,0:T(8,128)(2,1)}, u32[]{:S(2)}, u32[]{:S(2)}) collective-permute-start(bf16[2,128,2048]{2,1,0:T(8,128)(2,1)S(1)} %collective-permute-done), channel_id=1, source_target_pairs={{128,144},{136,152},{144,160},{152,168},{160,176},{168,184},{176,1... | collective-permute-start | bytes 3145736 | tf_op jit(solution)/shard_map/ppermute | solution.py:136
  6.6 7.3 %collective-permute-start.2 = (bf16[2,128,2048]{2,1,0:T(8,128)(2,1)S(1)}, bf16[2,128,2048]{2,1,0:T(8,128)(2,1)}, u32[]{:S(2)}, u32[]{:S(2)}) collective-permute-start(bf16[2,128,2048]{2,1,0:T(8,128)(2,1)S(1)} %collective-permute-done), channel_id=1, source_target_pairs={{128,136},{136,144},{144,152},{152,160},{160,168},{168,176},{176,1... | collective-permute-start | bytes 3145736 | tf_op jit(solution)/shard_map/ppermute | solution.py:136
  8.2 9.0 %collective-permute-start.3 = (bf16[2,128,2048]{2,1,0:T(8,128)(2,1)S(1)}, bf16[2,128,2048]{2,1,0:T(8,128)(2,1)}, u32[]{:S(2)}, u32[]{:S(2)}) collective-permute-start(bf16[2,128,2048]{2,1,0:T(8,128)(2,1)S(1)} %collective-permute-done), channel_id=1, source_target_pairs={{136,128},{144,136},{152,144},{160,152},{168,160},{176,168},{184,1... | collective-permute-start | bytes 3145736 | tf_op jit(solution)/shard_map/ppermute | solution.py:136
  9.9 9.7 %collective-permute-start.4 = (bf16[2,128,2048]{2,1,0:T(8,128)(2,1)S(1)}, bf16[2,128,2048]{2,1,0:T(8,128)(2,1)S(1)}, u32[]{:S(2)}, u32[]{:S(2)}) collective-permute-start(bf16[2,128,2048]{2,1,0:T(8,128)(2,1)S(1)} %collective-permute-done), channel_id=1, source_target_pairs={{144,128},{152,136},{160,144},{168,152},{176,160},{184,168},{192,1... | collective-permute-start | bytes 3145736 | tf_op jit(solution)/shard_map/ppermute | solution.py:136
  10.6 11.1 %copy-start = (bf16[1,2,128,2048]{3,2,1,0:T(8,128)(2,1)S(1)}, bf16[1,2,128,2048]{3,2,1,0:T(8,128)(2,1)}, u32[]{:S(2)}) copy-start(bf16[1,2,128,2048]{3,2,1,0:T(8,128)(2,1)} %param.5) | copy-start | bytes 3145732
  10.7 11.1 %copy-start.3 = (s32[1,2,8]{2,1,0:T(2,128)S(1)}, s32[1,2,8]{2,1,0:T(2,128)}, u32[]{:S(2)}) copy-start(s32[1,2,8]{2,1,0:T(2,128)} %param.7) | copy-start | bytes 196
  10.7 11.1 %copy-start.4 = (f32[2,32]{1,0:T(2,128)S(1)}, f32[2,32]{1,0:T(2,128)}, u32[]{:S(2)}) copy-start(f32[2,32]{1,0:T(2,128)} %param.6) | copy-start | bytes 772
  10.7 10.0 %collective-permute-start.5 = (bf16[2,128,2048]{2,1,0:T(8,128)(2,1)S(1)}, bf16[2,128,2048]{2,1,0:T(8,128)(2,1)S(1)}, u32[]{:S(2)}, u32[]{:S(2)}) collective-permute-start(bf16[2,128,2048]{2,1,0:T(8,128)(2,1)S(1)} %collective-permute-done), channel_id=1, source_target_pairs={{152,128},{160,136},{168,144},{176,152},{184,160},{192,168},{200,1... | collective-permute-start | bytes 3145736 | tf_op jit(solution)/shard_map/ppermute | solution.py:136
  37.0 3.7 %collective-permute-start.10 = (bf16[2,128,2048]{1,2,0:T(8,128)(2,1)S(1)}, bf16[2,128,2048]{1,2,0:T(8,128)(2,1)S(1)}, u32[]{:S(2)}, u32[]{:S(2)}) collective-permute-start(bf16[2,128,2048]{1,2,0:T(8,128)(2,1)S(1)} %get-tuple-element.51), channel_id=1, source_target_pairs={{128,152},{136,160},{144,168},{152,176},{160,184},{168,192},{176,2... | collective-permute-start | bytes 3145736 | tf_op jit(solution)/shard_map/ppermute | solution.py:136
  37.7 3.0 %collective-permute-start.6 = (bf16[2,128,2048]{1,2,0:T(8,128)(2,1)S(1)}, bf16[2,128,2048]{1,2,0:T(8,128)(2,1)S(1)}, u32[]{:S(2)}, u32[]{:S(2)}) collective-permute-start(bf16[2,128,2048]{1,2,0:T(8,128)(2,1)S(1)} %get-tuple-element.50), channel_id=1, source_target_pairs={{144,128},{152,136},{160,144},{168,152},{176,160},{184,168},{192,1... | collective-permute-start | bytes 3145736 | tf_op jit(solution)/shard_map/ppermute | solution.py:136
  38.5 2.2 collective-permute-start.7
  39.2 1.5 collective-permute-start.8
  39.9 0.8 collective-permute-start.9
  43.7 163.9 %collective-permute-start.11 = (bf16[2,128,2048]{1,2,0:T(8,128)(2,1)}, bf16[2,128,2048]{1,2,0:T(8,128)(2,1)S(1)}, u32[]{:S(2)}, u32[]{:S(2)}) collective-permute-start(bf16[2,128,2048]{1,2,0:T(8,128)(2,1)} %add_convert_fusion), channel_id=1, source_target_pairs={{128,0},{129,1},{130,2},{131,3},{132,4},{133,5},{134,6},{135,7},{1... | collective-permute-start | bytes 3145736 | tf_op jit(solution)/shard_map/ppermute | solution.py:120
  208.0 3.6 %collective-permute-start.12 = (f32[32]{0:T(128)S(1)}, f32[32]{0:T(128)S(1)}, u32[]{:S(2)}, u32[]{:S(2)}) collective-permute-start(f32[32]{0:T(128)S(1)} %broadcast_select_fusion), channel_id=1, source_target_pairs={{0,1},{1,0},{2,3},{3,2},{4,5},{5,4},{6,7},{7,6},{8,9},{9,8},{10,11... | collective-permute-start | bytes 392 | tf_op jit(solution)/shard_map/ppermute | solution.py:127
  211.6 3.6 %collective-permute-start.13 = (f32[32]{0:T(128)S(1)}, f32[32]{0:T(128)S(1)}, u32[]{:S(2)}, u32[]{:S(2)}) collective-permute-start(f32[32]{0:T(128)S(1)} %add.66), channel_id=1, source_target_pairs={{0,2},{1,3},{2,0},{3,1},{4,6},{5,7},{6,4},{7,5},{8,10},{9,11},{10,... | collective-permute-start | bytes 392 | tf_op jit(solution)/shard_map/ppermute | solution.py:127
  215.2 5.1 %collective-permute-start.14 = (f32[32]{0:T(128)S(1)}, f32[32]{0:T(128)S(1)}, u32[]{:S(2)}, u32[]{:S(2)}) collective-permute-start(f32[32]{0:T(128)S(1)} %add.67), channel_id=1, source_target_pairs={{0,4},{1,5},{2,6},{3,7},{4,0},{5,1},{6,2},{7,3},{8,12},{9,13},{10,... | collective-permute-start | bytes 392 | tf_op jit(solution)/shard_map/ppermute | solution.py:127
  220.3 9.0 %collective-permute-start.15 = (f32[32]{0:T(128)S(1)}, f32[32]{0:T(128)S(1)}, u32[]{:S(2)}, u32[]{:S(2)}) collective-permute-start(f32[32]{0:T(128)S(1)} %add.68), channel_id=1, source_target_pairs={{0,8},{8,0},{16,24},{24,16},{32,40},{40,32},{48,56},{56,48},{64,72... | collective-permute-start | bytes 392 | tf_op jit(solution)/shard_map/ppermute | solution.py:127
  229.3 15.1 %collective-permute-start.16 = (f32[32]{0:T(128)S(1)}, f32[32]{0:T(128)S(1)}, u32[]{:S(2)}, u32[]{:S(2)}) collective-permute-start(f32[32]{0:T(128)S(1)} %add.69), channel_id=1, source_target_pairs={{0,16},{8,24},{16,0},{24,8},{32,48},{40,56},{48,32},{56,40},{64,80... | collective-permute-start | bytes 392 | tf_op jit(solution)/shard_map/ppermute | solution.py:127
  244.4 8.2 %collective-permute-start.17 = (f32[32]{0:T(128)S(1)}, f32[32]{0:T(128)S(1)}, u32[]{:S(2)}, u32[]{:S(2)}) collective-permute-start(f32[32]{0:T(128)S(1)} %add.70), channel_id=1, source_target_pairs={{0,32},{8,40},{16,48},{24,56},{32,0},{40,8},{48,16},{56,24},{64,96... | collective-permute-start | bytes 392 | tf_op jit(solution)/shard_map/ppermute | solution.py:127
  252.6 8.6 %collective-permute-start.18 = (f32[32]{0:T(128)S(1)}, f32[32]{0:T(128)S(1)}, u32[]{:S(2)}, u32[]{:S(2)}) collective-permute-start(f32[32]{0:T(128)S(1)} %add.71), channel_id=1, source_target_pairs={{0,64},{8,72},{16,80},{24,88},{32,96},{40,104},{48,112},{56,120},{... | collective-permute-start | bytes 392 | tf_op jit(solution)/shard_map/ppermute | solution.py:127

commit v3 on v2

v3 whole, which is shorter than its diff:
```python
import math

import jax
import jax.numpy as jnp
from jax import lax
from jax.experimental import pallas as pl
from jax.experimental.pallas import tpu as pltpu
from jax.sharding import PartitionSpec as P

BLOCK = 128
ENC_MOST = 4
REACH_LOW = 2
REACH_HIGH = 3
WINDOW = REACH_LOW + REACH_HIGH + 1

masked_score = -1e30


def attention_kernel(start_ref, gains_ref, own_ref, *refs):
    window_refs = refs[:WINDOW]
    allow_ref = refs[WINDOW]
    out_ref = refs[WINDOW + 1]
    grad_refs = refs[WINDOW + 2 : 2 * WINDOW + 2]
    gain_ref = refs[2 * WINDOW + 2]
    pair = pl.program_id(0)
    start = start_ref[0]
    width = own_ref.shape[2]
    half = width // 2
    inv_root = 1.0 / math.sqrt(half)
    q = own_ref[0]
    do = own_ref[1]
    blocks = [ref[...] for ref in window_refs]

    def pick(slot):
        chosen = blocks[slot + WINDOW - ENC_MOST]
        for shift in range(WINDOW - ENC_MOST - 1, -1, -1):
            chosen = jnp.where(start == shift, blocks[slot + shift], chosen)
        return chosen

    slots = [pick(slot) for slot in range(ENC_MOST)]
    k = jnp.concatenate([piece[0] for piece in slots], axis=0)
    v = jnp.concatenate([piece[1] for piece in slots], axis=0)
    allowed = allow_ref[...] > 0
    lane = lax.broadcasted_iota(jnp.int32, (1, width), 1)
    first = lane < half
    heads = []
    att_parts = []
    for j in range(2):
        head = pair * 2 + j
        g_logit = gains_ref[0, head]
        g_value = gains_ref[1, head]
        mine = first if j == 0 else jnp.logical_not(first)
        q_h = jnp.where(mine, q, jnp.zeros_like(q))
        raw = lax.dot_general(q_h, k, (((1,), (1,)), ((), ())), preferred_element_type=jnp.float32) * inv_root
        logits = jnp.where(allowed, g_logit * raw, masked_score)
        top = jnp.max(logits, axis=1, keepdims=True)
        lifted = jnp.exp(logits - top)
        chances = lifted / jnp.sum(lifted, axis=1, keepdims=True)
        p_low = chances.astype(jnp.bfloat16)
        att_parts.append(jnp.dot(p_low, v, preferred_element_type=jnp.float32) * g_value)
        heads.append((g_logit, g_value, mine, raw, chances, p_low))
    attended = jnp.where(first, att_parts[0], att_parts[1]).astype(jnp.bfloat16)
    out_ref[0] = attended
    prod = do.astype(jnp.float32) * attended.astype(jnp.float32)
    dq_parts, dk_parts, dv_parts, logit_terms = [], [], [], []
    for g_logit, g_value, mine, raw, chances, p_low in heads:
        do_h = jnp.where(mine, do, jnp.zeros_like(do))
        slope = lax.dot_general(do_h, v, (((1,), (1,)), ((), ())), preferred_element_type=jnp.float32) * g_value
        carried = jnp.sum(jnp.where(mine, prod, 0.0), axis=1, keepdims=True)
        score_grad = chances * (slope - carried)
        score_low = score_grad.astype(jnp.bfloat16)
        factor = g_logit * inv_root
        dq_parts.append(jnp.dot(score_low, k, preferred_element_type=jnp.float32) * factor)
        dk_parts.append(lax.dot_general(score_low, q, (((0,), (0,)), ((), ())), preferred_element_type=jnp.float32) * factor)
        dv_parts.append(lax.dot_general(p_low, do, (((0,), (0,)), ((), ())), preferred_element_type=jnp.float32) * g_value)
        logit_terms.append(jnp.sum(score_grad * raw))
    out_ref[1] = jnp.where(first, dq_parts[0], dq_parts[1]).astype(jnp.bfloat16)
    key_grad = jnp.where(first, dk_parts[0], dk_parts[1]).astype(jnp.bfloat16)
    value_grad = jnp.where(first, dv_parts[0], dv_parts[1]).astype(jnp.bfloat16)
    value_prod = v.astype(jnp.float32) * value_grad.astype(jnp.float32)
    value_terms = [jnp.sum(jnp.where(first, value_prod, 0.0)), jnp.sum(jnp.where(first, 0.0, value_prod))]
    zero_block = jnp.zeros((BLOCK, width), jnp.bfloat16)
    for position in range(WINDOW):
        key_block = zero_block
        value_block = zero_block
        for slot in range(ENC_MOST):
            if 0 <= position - slot <= WINDOW - ENC_MOST:
                rows = slice(slot * BLOCK, (slot + 1) * BLOCK)
                key_block = jnp.where(start == position - slot, key_grad[rows], key_block)
                value_block = jnp.where(start == position - slot, value_grad[rows], value_block)
        grad_refs[position][0] = key_block
        grad_refs[position][1] = value_block
    glane = lax.broadcasted_iota(jnp.int32, gain_ref.shape, 2)
    terms = value_terms + logit_terms
    packed = jnp.zeros(gain_ref.shape, jnp.float32)
    for index, term in enumerate(terms):
        packed = jnp.where(glane == index, term, packed)
    gain_ref[...] = packed


def attention_block(start, head_gains, own, window, allowed_keys):
    _, rows, inner = own.shape
    keys = ENC_MOST * BLOCK
    head_count = head_gains.shape[1]
    width = 2 * (inner // head_count)
    pairs = inner // width
    block_spec = pl.BlockSpec((2, rows, width), lambda i, s, g: (0, 0, i))
    grid_spec = pltpu.PrefetchScalarGridSpec(
        num_scalar_prefetch=2,
        grid=(pairs,),
        in_specs=[block_spec] * (WINDOW + 1) + [pl.BlockSpec((1, keys), lambda i, s, g: (0, 0))],
        out_specs=[block_spec] * (WINDOW + 1) + [pl.BlockSpec((1, 8, 128), lambda i, s, g: (i, 0, 0))],
    )
    flops = 2 * rows * keys * width * 6 * pairs * 2
    cost = pl.CostEstimate(
        flops=flops,
        transcendentals=rows * keys * head_count,
        bytes_accessed=2 * 2 * rows * inner * (2 * WINDOW + 2),
    )
    outs = pl.pallas_call(
        attention_kernel,
        grid_spec=grid_spec,
        out_shape=[jax.ShapeDtypeStruct(own.shape, jnp.bfloat16)] * (WINDOW + 1)
        + [jax.ShapeDtypeStruct((pairs, 8, 128), jnp.float32)],
        cost_estimate=cost,
    )(start, head_gains, own, *window, allowed_keys.astype(jnp.int32)[None, :])
    produced = outs[0]
    grads = tuple(outs[1 : WINDOW + 1])
    packed = outs[WINDOW + 1]
    terms = jnp.stack([packed[:, 0, 0:2].reshape(-1), packed[:, 0, 2:4].reshape(-1)])
    return produced, grads, terms


def butterfly_sum(value, axis):
    count = lax.axis_size(axis)
    stride = 1
    while stride < count:
        value = value + lax.ppermute(value, axis, [(i, i ^ stride) for i in range(count)])
        stride *= 2
    return value


def segment_of(block_ids, block_sizes, block_total):
    starts = jnp.cumsum(block_sizes) - block_sizes
    found = jnp.sum((starts[None, :] <= block_ids[:, None]).astype(jnp.int32), axis=1) - 1
    inside = jnp.logical_and(block_ids >= 0, block_ids < block_total)
    return jnp.where(inside, found, -1)


def local(sections, head_gains, block_counts):
    phase_index = lax.axis_index("phase")
    shard_index = lax.axis_index("seq")
    count = lax.axis_size("seq")
    local_pair = sections[0]
    tok_dev = local_pair.shape[1]
    head_count = head_gains.shape[1]
    enc_counts = block_counts[0, 0]
    dec_counts = block_counts[0, 1]

    def enc(s):
        return s

    def dec(s):
        return count + s

    def across(value, pairs):
        return lax.ppermute(value, ("phase", "seq"), pairs)

    lower = range(count - 1)
    upper = range(1, count)
    at_home = across(local_pair, [(enc(s), dec(s)) for s in range(count)])
    minus_1 = across(local_pair, [(enc(s + 1), dec(s)) for s in lower])
    plus_1 = across(local_pair, [(enc(s - 1), dec(s)) for s in upper])
    minus_2 = across(minus_1, [(dec(s + 1), dec(s)) for s in lower])
    plus_2 = across(plus_1, [(dec(s - 1), dec(s)) for s in upper])
    minus_3 = across(minus_2, [(dec(s + 1), dec(s)) for s in lower])
    window = [plus_2, plus_1, at_home, minus_1, minus_2, minus_3]

    first_block = shard_index - REACH_LOW
    window_blocks = first_block + jnp.arange(WINDOW, dtype=jnp.int32)
    enc_segs = segment_of(window_blocks, enc_counts, count)
    segment = segment_of(jnp.reshape(shard_index, (1,)), dec_counts, count)[0]
    enc_starts = jnp.cumsum(enc_counts) - enc_counts
    start_block = jnp.clip(enc_starts[segment] - first_block, 0, WINDOW - ENC_MOST).astype(jnp.int32)
    slice_segs = lax.dynamic_slice_in_dim(enc_segs, start_block, ENC_MOST)
    allowed_keys = jnp.repeat(slice_segs == segment, BLOCK)

    def decoder_work(operands):
        own, pieces = operands
        return attention_block(jnp.reshape(start_block, (1,)), head_gains, own, pieces, allowed_keys)

    def encoder_rest(operands):
        own, pieces = operands
        zeros = jnp.zeros_like(own)
        return (zeros, (zeros,) * WINDOW, jnp.zeros((2, head_count), jnp.float32))

    produced, grads, terms = lax.cond(
        phase_index == 1, decoder_work, encoder_rest, (local_pair, window)
    )

    def added(a, b):
        return (a.astype(jnp.float32) + b.astype(jnp.float32)).astype(jnp.bfloat16)

    back_minus = across(grads[0], [(dec(s + 1), dec(s)) for s in lower])
    back_plus = across(grads[5], [(dec(s - 1), dec(s)) for s in upper])
    minus_sum = across(added(back_minus, grads[1]), [(dec(s + 1), enc(s)) for s in lower])
    back_plus = across(added(back_plus, grads[4]), [(dec(s - 1), dec(s)) for s in upper])
    plus_sum = across(added(back_plus, grads[3]), [(dec(s - 1), enc(s)) for s in upper])
    own_sum = across(grads[2], [(dec(s), enc(s)) for s in range(count)])
    returned = (
        own_sum.astype(jnp.float32) + minus_sum.astype(jnp.float32) + plus_sum.astype(jnp.float32)
    ).astype(jnp.bfloat16)

    token_total = tok_dev * count * lax.axis_size("dp")
    summed = butterfly_sum(butterfly_sum(butterfly_sum(terms, "phase"), "dp"), "seq")
    chosen = lax.dynamic_index_in_dim(summed, phase_index, 0, keepdims=False)
    scale = jnp.where(phase_index == 0, head_gains[1], 1.0) * math.sqrt(token_total)
    gain_total = chosen / scale
    result = jnp.where(phase_index == 0, returned, produced)[None]
    return (result, gain_total[None])


def solution(mesh):
    return jax.shard_map(
        local,
        mesh=mesh,
        in_specs=(P("phase", None, ("dp", "seq"), None), P(), P("dp", None, None)),
        out_specs=(P("phase", None, ("dp", "seq"), None), P("phase", None)),
        check_vma=False,
    )
```

time: 264 us -> 181 us (0.69)
  waiting for transfers between devices: 174 us -> 14.4 us
  starting transfers between devices: 54.1 us -> 145 us
  local copies, waits for them, and re-layouts: 28.9 us -> 7.64 us
  other arithmetic: 3.99 us -> 11.4 us
    ppermute x12, waiting for transfers between devices: 163 us -> 0.03 us  [across(): return lax.ppermute(value, ('phase', 'seq'), pairs)]
    ppermute x7 -> x8, starting transfers between devices: 40.7 us -> 116 us  [butterfly_sum(): lax.ppermute(value, axis, [(i, i ^ stride) for i in range(count)])]
    ppermute x12, starting transfers between devices: 13.4 us -> 29.1 us  [across(): return lax.ppermute(value, ('phase', 'seq'), pairs)]
    unnamed x13 -> x4, local copies, waits for them, and re-layouts: 11.8 us -> 0.01 us
    cond x1 -> x0, local copies, waits for them, and re-layouts: 8.66 us -> none  [local(): lax.cond(phase_index == 1, decoder_work, encoder_rest, (local_pair, window))]
    another operation x3 -> x9, local copies, waits for them, and re-layouts: 3.58 us -> 7.63 us
    convert_element_type x1 -> x5, other arithmetic: 3.01 us -> 6.88 us  [the longest x3 6.13 us: added(): return (a.astype(jnp.float32) + b.astype(jnp.float32)).astype(jnp.bfloat16)]
    slice x3 -> x0, local copies, waits for them, and re-layouts: 3.81 us -> none  [the longest x1 2.95 us: local(): portion = window_grads[:, slot * tok_dev:(slot + 1) * tok_dev]]
  transfers between devices with their start and end apart: 19 -> 20, of which waited for: 9 -> 8; matrix products, arithmetic and copies ran while one was open for 5% -> 5% of each run, Pallas kernels for 0% -> 0%
where the time goes in v3:
time: 181 us; the launch traced here: 179 us
  starting transfers between devices  145 us (80%)
  waiting for transfers between devices  14.4 us (8%)
  other arithmetic  11.4 us (6%)
  local copies, waits for them, and re-layouts  7.64 us (4%)
    ppermute x8, starting transfers between devices, butterfly_sum(): lax.ppermute(value, axis, [(i, i ^ stride) for i in range(count)])  116 us
    ppermute x12, starting transfers between devices, across(): return lax.ppermute(value, ('phase', 'seq'), pairs)  29.1 us
    ppermute x8, waiting for transfers between devices, butterfly_sum(): lax.ppermute(value, axis, [(i, i ^ stride) for i in range(count)])  14.3 us
    another operation x9, local copies, waits for them, and re-layouts  7.63 us
    convert_element_type x3, other arithmetic, added(): return (a.astype(jnp.float32) + b.astype(jnp.float32)).astype(jnp.bfloat16)  6.13 us
  transfers between devices with their start and end apart: 20, of which 8 were waited for; matrix products, arithmetic and copies ran while one was open for 5% of the time, Pallas kernels for 0%

profile of v3, /device:TPU:8, one launch (start us, length us, event | category | flops | bytes accessed | tf_op | source)
XLA Modules:
  0.0 179.0 jit_solution(7066640463821442466)
XLA Ops:
  0.6 0.7 collective-permute-start.3
  1.4 3.9 %collective-permute-start = (bf16[2,128,2048]{2,1,0:T(8,128)(2,1)}, bf16[2,128,2048]{2,1,0:T(8,128)(2,1)S(1)}, u32[]{:S(2)}, u32[]{:S(2)}) collective-permute-start(bf16[2,128,2048]{2,1,0:T(8,128)(2,1)} %bitcast.18), channel_id=1, source_target_pairs={{0,136},{8,144},{16,152},{24,160},{32,168},{40,176},{48,184},{56,1... | collective-permute-start | bytes 3145736 | tf_op jit(solution)/shard_map/ppermute | solution.py:167
  5.3 0.0 collective-permute-done.3
  5.3 0.0 copy-start.3
  5.3 0.7 collective-permute-start.4
  6.0 15.0 %collective-permute-start.2 = (bf16[2,128,2048]{2,1,0:T(8,128)(2,1)}, bf16[2,128,2048]{2,1,0:T(8,128)(2,1)}, u32[]{:S(2)}, u32[]{:S(2)}) collective-permute-start(bf16[2,128,2048]{2,1,0:T(8,128)(2,1)} %bitcast.19), channel_id=1, source_target_pairs={{0,128},{8,136},{16,144},{24,152},{32,160},{40,168},{48,176},{56,1... | collective-permute-start | bytes 3145736 | tf_op jit(solution)/shard_map/ppermute | solution.py:167
  21.0 0.0 collective-permute-done
  21.0 1.6 collective-permute-start.1
  22.6 0.0 collective-permute-done.4
  22.6 1.7 collective-permute-start.5
  24.3 0.0 copy-done.3
  24.3 0.8 slice_bitcast_fusion.1
  25.0 0.2 reduce-window.8
  25.2 0.2 reduce-window_1_clone.1
  25.4 0.7 bitcast_subtract_fusion
  26.1 0.7 compare_convert_fusion.2
  26.8 0.1 compare_convert_fusion.1
  26.9 0.0 collective-permute-done.2
  26.9 0.0 collective-permute-done.1
  26.9 0.0 collective-permute-done.5
  26.9 6.9 %conditional.1 = (bf16[2,128,2048]{2,1,0:T(8,128)(2,1)S(1)}, bf16[2,128,2048]{2,1,0:T(8,128)(2,1)}, bf16[2,128,2048]{2,1,0:T(8,128)(2,1)}, bf16[2,128,2048]{2,1,...) conditional(s32[]{:T(128)} %convert_element_type.91, () %tuple.51, ...), branch_computations={%region_2.3_spmd, %region_3.6_spmd} | conditional | flops 3222798336 | bytes 32510076 | solution.py:197
  26.9 0.2 broadcast.49
  27.1 1.6 broadcast.49.clone
  28.7 1.6 broadcast.49.clone.1
  30.3 0.1 broadcast.47
  30.4 1.1 broadcast.47.clone
  31.5 1.2 broadcast.47.clone.1
  32.7 1.1 broadcast.47.clone.2
  33.8 0.7 collective-permute-start.9
  34.5 0.7 collective-permute-start.7
  35.2 0.0 collective-permute-done.9
  35.2 1.9 %add_convert_fusion.2 = bf16[2,128,2048]{2,1,0:T(8,128)(2,1)S(1)} fusion(f32[2,128,2048]{2,1,0:T(8,128)} %get-tuple-element.243, bf16[2,128,2048]{2,1,0:T(8,128)(2,1)S(1)} %collective-permute-done.9), kind=kLoop, calls=%fused_computation.7 | loop fusion | flops 1572864 | bytes 4194304 | tf_op jit(solution)/shard_map/convert_element_type | solution.py:202
  37.2 0.7 collective-permute-start.10
  37.9 1.3 collective-permute-start.6
  39.2 0.0 collective-permute-done.7
  39.2 1.3 add_convert_fusion.3
  40.5 1.3 collective-permute-start.8
  41.8 0.0 collective-permute-done.10
  41.8 0.0 copy-start.2
  41.8 2.9 %add_convert_fusion.1 = bf16[2,128,2048]{2,1,0:T(8,128)(2,1)} fusion(f32[2,128,2048]{2,1,0:T(8,128)} %get-tuple-element.244, bf16[2,128,2048]{2,1,0:T(8,128)(2,1)S(1)} %collective-permute-done.10), kind=kLoop, calls=%fused_computation.6 | loop fusion | flops 1572864 | bytes 4194304 | tf_op jit(solution)/shard_map/convert_element_type | solution.py:202
  44.7 0.7 collective-permute-start.11
  45.5 80.6 %collective-permute-start.12 = (f32[2,32]{1,0:T(2,128)S(1)}, f32[2,32]{1,0:T(2,128)S(1)}, u32[]{:S(2)}, u32[]{:S(2)}) collective-permute-start(f32[2,32]{1,0:T(2,128)S(1)} %get-tuple-element.246), channel_id=1, source_target_pairs={{0,128},{128,0},{1,129},{129,1},{2,130},{130,2},{3,131},{131,3},{4... | collective-permute-start | bytes 776 | tf_op jit(solution)/shard_map/ppermute | solution.py:138
  126.1 0.8 collective-permute-done.12
  126.9 0.4 collective-permute-start.13
  127.3 3.2 %collective-permute-done.13 = f32[2,32]{1,0:T(2,128)S(1)} collective-permute-done((f32[2,32]{1,0:T(2,128)S(1)}, f32[2,32]{1,0:T(2,128)S(1)}, u32[]{:S(2)}, u32[]{:S(2)}) %collective-permute-start.13) | collective-permute-done | bytes 288 | tf_op jit(solution)/shard_map/ppermute | solution.py:138
  130.5 1.5 collective-permute-start.14
  132.0 2.1 %collective-permute-done.14 = f32[2,32]{1,0:T(2,128)S(1)} collective-permute-done((f32[2,32]{1,0:T(2,128)S(1)}, f32[2,32]{1,0:T(2,128)S(1)}, u32[]{:S(2)}, u32[]{:S(2)}) %collective-permute-start.14) | collective-permute-done | bytes 288 | tf_op jit(solution)/shard_map/ppermute | solution.py:138
  134.1 3.0 %collective-permute-start.15 = (f32[2,32]{1,0:T(2,128)S(1)}, f32[2,32]{1,0:T(2,128)S(1)}, u32[]{:S(2)}, u32[]{:S(2)}) collective-permute-start(f32[2,32]{1,0:T(2,128)S(1)} %add.82), channel_id=1, source_target_pairs={{0,4},{1,5},{2,6},{3,7},{4,0},{5,1},{6,2},{7,3},{8,12},{9,13},{10,... | collective-permute-start | bytes 776 | tf_op jit(solution)/shard_map/ppermute | solution.py:138
  137.1 2.1 %collective-permute-done.15 = f32[2,32]{1,0:T(2,128)S(1)} collective-permute-done((f32[2,32]{1,0:T(2,128)S(1)}, f32[2,32]{1,0:T(2,128)S(1)}, u32[]{:S(2)}, u32[]{:S(2)}) %collective-permute-start.15) | collective-permute-done | bytes 288 | tf_op jit(solution)/shard_map/ppermute | solution.py:138
  139.2 2.9 %collective-permute-start.16 = (f32[2,32]{1,0:T(2,128)S(1)}, f32[2,32]{1,0:T(2,128)S(1)}, u32[]{:S(2)}, u32[]{:S(2)}) collective-permute-start(f32[2,32]{1,0:T(2,128)S(1)} %add.83), channel_id=1, source_target_pairs={{0,8},{8,0},{16,24},{24,16},{32,40},{40,32},{48,56},{56,48},{64,72... | collective-permute-start | bytes 776 | tf_op jit(solution)/shard_map/ppermute | solution.py:138
  142.1 1.6 collective-permute-done.16
  143.6 4.0 %collective-permute-start.17 = (f32[2,32]{1,0:T(2,128)S(1)}, f32[2,32]{1,0:T(2,128)S(1)}, u32[]{:S(2)}, u32[]{:S(2)}) collective-permute-start(f32[2,32]{1,0:T(2,128)S(1)} %add.84), channel_id=1, source_target_pairs={{0,16},{8,24},{16,0},{24,8},{32,48},{40,56},{48,32},{56,40},{64,80... | collective-permute-start | bytes 776 | tf_op jit(solution)/shard_map/ppermute | solution.py:138
  147.6 1.6 collective-permute-done.17
  149.2 13.1 %collective-permute-start.18 = (f32[2,32]{1,0:T(2,128)S(1)}, f32[2,32]{1,0:T(2,128)S(1)}, u32[]{:S(2)}, u32[]{:S(2)}) collective-permute-start(f32[2,32]{1,0:T(2,128)S(1)} %add.85), channel_id=1, source_target_pairs={{0,32},{8,40},{16,48},{24,56},{32,0},{40,8},{48,16},{56,24},{64,96... | collective-permute-start | bytes 776 | tf_op jit(solution)/shard_map/ppermute | solution.py:138
  162.3 1.6 collective-permute-done.18
  163.9 10.2 %collective-permute-start.19 = (f32[2,32]{1,0:T(2,128)S(1)}, f32[2,32]{1,0:T(2,128)S(1)}, u32[]{:S(2)}, u32[]{:S(2)}) collective-permute-start(f32[2,32]{1,0:T(2,128)S(1)} %add.86), channel_id=1, source_target_pairs={{0,64},{8,72},{16,80},{24,88},{32,96},{40,104},{48,112},{56,120},{... | collective-permute-start | bytes 776 | tf_op jit(solution)/shard_map/ppermute | solution.py:138
  174.1 1.6 collective-permute-done.19
  175.6 0.0 copy-done.2
  175.6 0.5 fusion.3
  176.1 0.0 collective-permute-done.6
  176.1 0.0 collective-permute-done.8
  176.1 0.0 collective-permute-done.11
  176.1 2.9 %fusion.1 = bf16[1,2,128,2048]{3,2,1,0:T(8,128)(2,1)} fusion(bf16[2,128,2048]{2,1,0:T(8,128)(2,1)S(1)} %get-tuple-element.245, bf16[2,128,2048]{2,1,0:T(8,128)(2,1)S(1)} %collective-permute-done.11, bf16[2,128,2048]{2,1,0:T(8,128)(2,1)S(1)} %collective-permute-done.8, bf16[2,128,2048]{2,1,0:T(8,128)(2,1)} %collective-permute-done.6, pred[]{:T(512)S(6)} %eq.23), kind=kLoop, calls=%fused_computation.10 | loop fusion | flops 3670016 | bytes 5242881 | tf_op jit(solution)/shard_map/broadcast_in_dim | solution.py:219
  (10 shorter events, 0.0 us)
Async XLA Ops:
  0.6 4.6 %collective-permute-start.3 = (bf16[2,128,2048]{2,1,0:T(8,128)(2,1)}, bf16[2,128,2048]{2,1,0:T(8,128)(2,1)S(1)}, u32[]{:S(2)}, u32[]{:S(2)}) collective-permute-start(bf16[2,128,2048]{2,1,0:T(8,128)(2,1)} %bitcast.17), channel_id=1, source_target_pairs={{8,128},{16,136},{24,144},{32,152},{40,160},{48,168},{56,176},{64,... | collective-permute-start | bytes 3145736 | tf_op jit(solution)/shard_map/ppermute | solution.py:167
  1.4 19.6 %collective-permute-start = (bf16[2,128,2048]{2,1,0:T(8,128)(2,1)}, bf16[2,128,2048]{2,1,0:T(8,128)(2,1)S(1)}, u32[]{:S(2)}, u32[]{:S(2)}) collective-permute-start(bf16[2,128,2048]{2,1,0:T(8,128)(2,1)} %bitcast.18), channel_id=1, source_target_pairs={{0,136},{8,144},{16,152},{24,160},{32,168},{40,176},{48,184},{56,1... | collective-permute-start | bytes 3145736 | tf_op jit(solution)/shard_map/ppermute | solution.py:167
  5.3 19.0 %copy-start.3 = (bf16[2,128,2048]{2,1,0:T(8,128)(2,1)}, bf16[2,128,2048]{2,1,0:T(8,128)(2,1)S(1)}, u32[]{:S(2)}) copy-start(bf16[2,128,2048]{2,1,0:T(8,128)(2,1)S(1)} %collective-permute-done.3) | copy-start | bytes 3145732
  5.3 17.3 %collective-permute-start.4 = (bf16[2,128,2048]{2,1,0:T(8,128)(2,1)S(1)}, bf16[2,128,2048]{2,1,0:T(8,128)(2,1)S(1)}, u32[]{:S(2)}, u32[]{:S(2)}) collective-permute-start(bf16[2,128,2048]{2,1,0:T(8,128)(2,1)S(1)} %collective-permute-done.3), channel_id=1, source_target_pairs={{136,128},{144,136},{152,144},{160,152},{168,160},{176,168},{184,1... | collective-permute-start | bytes 3145736 | tf_op jit(solution)/shard_map/ppermute | solution.py:167
  6.0 20.8 %collective-permute-start.2 = (bf16[2,128,2048]{2,1,0:T(8,128)(2,1)}, bf16[2,128,2048]{2,1,0:T(8,128)(2,1)}, u32[]{:S(2)}, u32[]{:S(2)}) collective-permute-start(bf16[2,128,2048]{2,1,0:T(8,128)(2,1)} %bitcast.19), channel_id=1, source_target_pairs={{0,128},{8,136},{16,144},{24,152},{32,160},{40,168},{48,176},{56,1... | collective-permute-start | bytes 3145736 | tf_op jit(solution)/shard_map/ppermute | solution.py:167
  21.0 5.9 %collective-permute-start.1 = (bf16[2,128,2048]{2,1,0:T(8,128)(2,1)S(1)}, bf16[2,128,2048]{2,1,0:T(8,128)(2,1)}, u32[]{:S(2)}, u32[]{:S(2)}) collective-permute-start(bf16[2,128,2048]{2,1,0:T(8,128)(2,1)S(1)} %collective-permute-done), channel_id=1, source_target_pairs={{128,136},{136,144},{144,152},{152,160},{160,168},{168,176},{176,1... | collective-permute-start | bytes 3145736 | tf_op jit(solution)/shard_map/ppermute | solution.py:167
  22.6 4.2 %collective-permute-start.5 = (bf16[2,128,2048]{2,1,0:T(8,128)(2,1)S(1)}, bf16[2,128,2048]{2,1,0:T(8,128)(2,1)}, u32[]{:S(2)}, u32[]{:S(2)}) collective-permute-start(bf16[2,128,2048]{2,1,0:T(8,128)(2,1)S(1)} %collective-permute-done.4), channel_id=1, source_target_pairs={{136,128},{144,136},{152,144},{160,152},{168,160},{176,168},{184,1... | collective-permute-start | bytes 3145736 | tf_op jit(solution)/shard_map/ppermute | solution.py:167
  33.8 1.5 collective-permute-start.9
  34.5 4.7 %collective-permute-start.7 = (bf16[2,128,2048]{2,1,0:T(8,128)(2,1)}, bf16[2,128,2048]{2,1,0:T(8,128)(2,1)S(1)}, u32[]{:S(2)}, u32[]{:S(2)}) collective-permute-start(bf16[2,128,2048]{2,1,0:T(8,128)(2,1)} %get-tuple-element.240), channel_id=1, source_target_pairs={{136,128},{144,136},{152,144},{160,152},{168,160},{176,168},{184,1... | collective-permute-start | bytes 3145736 | tf_op jit(solution)/shard_map/ppermute | solution.py:167
  37.2 4.7 %collective-permute-start.10 = (bf16[2,128,2048]{2,1,0:T(8,128)(2,1)S(1)}, bf16[2,128,2048]{2,1,0:T(8,128)(2,1)S(1)}, u32[]{:S(2)}, u32[]{:S(2)}) collective-permute-start(bf16[2,128,2048]{2,1,0:T(8,128)(2,1)S(1)} %add_convert_fusion.2), channel_id=1, source_target_pairs={{128,136},{136,144},{144,152},{152,160},{160,168},{168,176},{176,1... | collective-permute-start | bytes 3145736 | tf_op jit(solution)/shard_map/ppermute | solution.py:167
  37.9 138.2 %collective-permute-start.6 = (bf16[2,128,2048]{2,1,0:T(8,128)(2,1)}, bf16[2,128,2048]{2,1,0:T(8,128)(2,1)}, u32[]{:S(2)}, u32[]{:S(2)}) collective-permute-start(bf16[2,128,2048]{2,1,0:T(8,128)(2,1)} %get-tuple-element.239), channel_id=1, source_target_pairs={{128,0},{136,8},{144,16},{152,24},{160,32},{168,40},{176,48},{184,... | collective-permute-start | bytes 3145736 | tf_op jit(solution)/shard_map/ppermute | solution.py:167
  40.5 135.6 %collective-permute-start.8 = (bf16[2,128,2048]{2,1,0:T(8,128)(2,1)}, bf16[2,128,2048]{2,1,0:T(8,128)(2,1)S(1)}, u32[]{:S(2)}, u32[]{:S(2)}) collective-permute-start(bf16[2,128,2048]{2,1,0:T(8,128)(2,1)} %add_convert_fusion.3), channel_id=1, source_target_pairs={{136,0},{144,8},{152,16},{160,24},{168,32},{176,40},{184,48},{192,... | collective-permute-start | bytes 3145736 | tf_op jit(solution)/shard_map/ppermute | solution.py:167
  41.8 133.8 %copy-start.2 = (f32[2,32]{1,0:T(2,128)S(1)}, f32[2,32]{1,0:T(2,128)}, u32[]{:S(2)}) copy-start(f32[2,32]{1,0:T(2,128)} %param.6) | copy-start | bytes 772
  44.7 131.4 %collective-permute-start.11 = (bf16[2,128,2048]{2,1,0:T(8,128)(2,1)}, bf16[2,128,2048]{2,1,0:T(8,128)(2,1)S(1)}, u32[]{:S(2)}, u32[]{:S(2)}) collective-permute-start(bf16[2,128,2048]{2,1,0:T(8,128)(2,1)} %add_convert_fusion.1), channel_id=1, source_target_pairs={{128,8},{136,16},{144,24},{152,32},{160,40},{168,48},{176,56},{184... | collective-permute-start | bytes 3145736 | tf_op jit(solution)/shard_map/ppermute | solution.py:167
  45.5 81.4 %collective-permute-start.12 = (f32[2,32]{1,0:T(2,128)S(1)}, f32[2,32]{1,0:T(2,128)S(1)}, u32[]{:S(2)}, u32[]{:S(2)}) collective-permute-start(f32[2,32]{1,0:T(2,128)S(1)} %get-tuple-element.246), channel_id=1, source_target_pairs={{0,128},{128,0},{1,129},{129,1},{2,130},{130,2},{3,131},{131,3},{4... | collective-permute-start | bytes 776 | tf_op jit(solution)/shard_map/ppermute | solution.py:138
  126.9 3.6 %collective-permute-start.13 = (f32[2,32]{1,0:T(2,128)S(1)}, f32[2,32]{1,0:T(2,128)S(1)}, u32[]{:S(2)}, u32[]{:S(2)}) collective-permute-start(f32[2,32]{1,0:T(2,128)S(1)} %add.80), channel_id=1, source_target_pairs={{0,1},{1,0},{2,3},{3,2},{4,5},{5,4},{6,7},{7,6},{8,9},{9,8},{10,11... | collective-permute-start | bytes 776 | tf_op jit(solution)/shard_map/ppermute | solution.py:138
  130.5 3.6 %collective-permute-start.14 = (f32[2,32]{1,0:T(2,128)S(1)}, f32[2,32]{1,0:T(2,128)S(1)}, u32[]{:S(2)}, u32[]{:S(2)}) collective-permute-start(f32[2,32]{1,0:T(2,128)S(1)} %add.81), channel_id=1, source_target_pairs={{0,2},{1,3},{2,0},{3,1},{4,6},{5,7},{6,4},{7,5},{8,10},{9,11},{10,... | collective-permute-start | bytes 776 | tf_op jit(solution)/shard_map/ppermute | solution.py:138
  134.1 5.1 %collective-permute-start.15 = (f32[2,32]{1,0:T(2,128)S(1)}, f32[2,32]{1,0:T(2,128)S(1)}, u32[]{:S(2)}, u32[]{:S(2)}) collective-permute-start(f32[2,32]{1,0:T(2,128)S(1)} %add.82), channel_id=1, source_target_pairs={{0,4},{1,5},{2,6},{3,7},{4,0},{5,1},{6,2},{7,3},{8,12},{9,13},{10,... | collective-permute-start | bytes 776 | tf_op jit(solution)/shard_map/ppermute | solution.py:138
  139.2 4.4 %collective-permute-start.16 = (f32[2,32]{1,0:T(2,128)S(1)}, f32[2,32]{1,0:T(2,128)S(1)}, u32[]{:S(2)}, u32[]{:S(2)}) collective-permute-start(f32[2,32]{1,0:T(2,128)S(1)} %add.83), channel_id=1, source_target_pairs={{0,8},{8,0},{16,24},{24,16},{32,40},{40,32},{48,56},{56,48},{64,72... | collective-permute-start | bytes 776 | tf_op jit(solution)/shard_map/ppermute | solution.py:138
  143.6 5.5 %collective-permute-start.17 = (f32[2,32]{1,0:T(2,128)S(1)}, f32[2,32]{1,0:T(2,128)S(1)}, u32[]{:S(2)}, u32[]{:S(2)}) collective-permute-start(f32[2,32]{1,0:T(2,128)S(1)} %add.84), channel_id=1, source_target_pairs={{0,16},{8,24},{16,0},{24,8},{32,48},{40,56},{48,32},{56,40},{64,80... | collective-permute-start | bytes 776 | tf_op jit(solution)/shard_map/ppermute | solution.py:138
  149.2 14.7 %collective-permute-start.18 = (f32[2,32]{1,0:T(2,128)S(1)}, f32[2,32]{1,0:T(2,128)S(1)}, u32[]{:S(2)}, u32[]{:S(2)}) collective-permute-start(f32[2,32]{1,0:T(2,128)S(1)} %add.85), channel_id=1, source_target_pairs={{0,32},{8,40},{16,48},{24,56},{32,0},{40,8},{48,16},{56,24},{64,96... | collective-permute-start | bytes 776 | tf_op jit(solution)/shard_map/ppermute | solution.py:138
  163.9 11.8 %collective-permute-start.19 = (f32[2,32]{1,0:T(2,128)S(1)}, f32[2,32]{1,0:T(2,128)S(1)}, u32[]{:S(2)}, u32[]{:S(2)}) collective-permute-start(f32[2,32]{1,0:T(2,128)S(1)} %add.86), channel_id=1, source_target_pairs={{0,64},{8,72},{16,80},{24,88},{32,96},{40,104},{48,112},{56,120},{... | collective-permute-start | bytes 776 | tf_op jit(solution)/shard_map/ppermute | solution.py:138

commit v4 on v3

--- a/solution.py
+++ b/solution.py
@@ -131,13 +131,9 @@
     return produced, grads, terms
 
 
-def butterfly_sum(value, axis):
+def exchange_add(value, axis, stride):
     count = lax.axis_size(axis)
-    stride = 1
-    while stride < count:
-        value = value + lax.ppermute(value, axis, [(i, i ^ stride) for i in range(count)])
-        stride *= 2
-    return value
+    return value + lax.ppermute(value, axis, [(i, i ^ stride) for i in range(count)])
 
 
 def segment_of(block_ids, block_sizes, block_total):
@@ -201,18 +197,22 @@
     def added(a, b):
         return (a.astype(jnp.float32) + b.astype(jnp.float32)).astype(jnp.bfloat16)
 
+    token_total = tok_dev * count * lax.axis_size("dp")
+    summed = exchange_add(terms, "phase", 1)
     back_minus = across(grads[0], [(dec(s + 1), dec(s)) for s in lower])
     back_plus = across(grads[5], [(dec(s - 1), dec(s)) for s in upper])
+    own_sum = across(grads[2], [(dec(s), enc(s)) for s in range(count)])
+    summed = exchange_add(exchange_add(summed, "dp", 1), "dp", 2)
+    summed, back_minus, back_plus = lax.optimization_barrier((summed, back_minus, back_plus))
     minus_sum = across(added(back_minus, grads[1]), [(dec(s + 1), enc(s)) for s in lower])
     back_plus = across(added(back_plus, grads[4]), [(dec(s - 1), dec(s)) for s in upper])
+    summed = exchange_add(exchange_add(exchange_add(summed, "dp", 4), "seq", 1), "seq", 2)
+    summed, back_plus = lax.optimization_barrier((summed, back_plus))
     plus_sum = across(added(back_plus, grads[3]), [(dec(s - 1), enc(s)) for s in upper])
-    own_sum = across(grads[2], [(dec(s), enc(s)) for s in range(count)])
+    summed = exchange_add(exchange_add(summed, "seq", 4), "seq", 8)
     returned = (
         own_sum.astype(jnp.float32) + minus_sum.astype(jnp.float32) + plus_sum.astype(jnp.float32)
     ).astype(jnp.bfloat16)
-
-    token_total = tok_dev * count * lax.axis_size("dp")
-    summed = butterfly_sum(butterfly_sum(butterfly_sum(terms, "phase"), "dp"), "seq")
     chosen = lax.dynamic_index_in_dim(summed, phase_index, 0, keepdims=False)
     scale = jnp.where(phase_index == 0, head_gains[1], 1.0) * math.sqrt(token_total)
     gain_total = chosen / scale

time: 181 us -> 171 us (0.945)
  the two profiles are of different devices: /device:TPU:8 before, /device:TPU:1 now
where the time goes in v4:
time: 171 us; the launch traced here: 170 us
  waiting for transfers between devices  62.2 us (36%)
  starting transfers between devices  56.7 us (33%)
  Pallas kernels  29.3 us (17%)
  other arithmetic  16.9 us (10%)
  local copies, waits for them, and re-layouts  3.17 us (2%)
    ppermute x12, waiting for transfers between devices, across(): return lax.ppermute(value, ('phase', 'seq'), pairs)  40.7 us
    ppermute x8, starting transfers between devices, exchange_add(): lax.ppermute(value, axis, [(i, i ^ stride) for i in range(count)])  29.8 us
    pallas_call x1, Pallas kernels, attention_block(): pl.pallas_call(attention_kernel, grid_spec=grid_spec, out_shape=[jax.Shap...  29.3 us
    ppermute x12, starting transfers between devices, across(): return lax.ppermute(value, ('phase', 'seq'), pairs)  26.9 us
    ppermute x8, waiting for transfers between devices, exchange_add(): lax.ppermute(value, axis, [(i, i ^ stride) for i in range(count)])  21.5 us
    convert_element_type x6, other arithmetic, added(): return (a.astype(jnp.float32) + b.astype(jnp.float32)).astype(jnp.bfloat16)  10.8 us
  transfers between devices with their start and end apart: 20, of which 12 were waited for; matrix products, arithmetic and copies ran while one was open for 4% of the time, Pallas kernels for 0%

profile of v4, /device:TPU:1, one launch (start us, length us, event | category | flops | bytes accessed | tf_op | source)
XLA Modules:
  0.0 170.3 jit_solution(8015799580205095494)
XLA Ops:
  0.6 1.3 collective-permute-start.3
  1.9 0.7 collective-permute-start
  2.7 15.0 %collective-permute-done.3 = bf16[2,128,2048]{2,1,0:T(8,128)(2,1)S(1)} collective-permute-done((bf16[2,128,2048]{2,1,0:T(8,128)(2,1)}, bf16[2,128,2048]{2,1,0:T(8,128)(2,1)S(1)}, u32[]{:S(2)}, u32[]{:S(2)}) %collective-permute-start.3) | collective-permute-done | bytes 1048608 | tf_op jit(solution)/shard_map/ppermute | solution.py:163
  17.6 1.3 collective-permute-start.4
  18.9 1.3 collective-permute-start.2
  20.2 0.0 collective-permute-done
  20.2 5.3 %collective-permute-start.1 = (bf16[2,128,2048]{2,1,0:T(8,128)(2,1)S(1)}, bf16[2,128,2048]{2,1,0:T(8,128)(2,1)}, u32[]{:S(2)}, u32[]{:S(2)}) collective-permute-start(bf16[2,128,2048]{2,1,0:T(8,128)(2,1)S(1)} %collective-permute-done), channel_id=1, source_target_pairs={{128,136},{136,144},{144,152},{152,160},{160,168},{168,176},{176,1... | collective-permute-start | bytes 3145736 | tf_op jit(solution)/shard_map/ppermute | solution.py:163
  25.5 8.0 %collective-permute-done.4 = bf16[2,128,2048]{2,1,0:T(8,128)(2,1)S(1)} collective-permute-done((bf16[2,128,2048]{2,1,0:T(8,128)(2,1)S(1)}, bf16[2,128,2048]{2,1,0:T(8,128)(2,1)S(1)}, u32[]{:S(2)}, u32[]{:S(2)}) %collective-permute-start.4) | collective-permute-done | bytes 1048608 | tf_op jit(solution)/shard_map/ppermute | solution.py:163
  33.5 1.3 collective-permute-start.5
  34.8 0.8 slice_bitcast_fusion.1
  35.6 0.2 reduce-window.8
  35.7 0.2 reduce-window_1_clone.1
  35.9 0.7 bitcast_subtract_fusion
  36.6 0.7 compare_convert_fusion.2
  37.3 0.1 compare_convert_fusion.1
  37.4 0.0 collective-permute-done.2
  37.4 0.0 collective-permute-done.1
  37.4 11.9 %collective-permute-done.5 = bf16[2,128,2048]{2,1,0:T(8,128)(2,1)} collective-permute-done((bf16[2,128,2048]{2,1,0:T(8,128)(2,1)S(1)}, bf16[2,128,2048]{2,1,0:T(8,128)(2,1)}, u32[]{:S(2)}, u32[]{:S(2)}) %collective-permute-start.5) | collective-permute-done | bytes 1048608 | tf_op jit(solution)/shard_map/ppermute | solution.py:163
  49.3 38.4 %conditional.1 = (bf16[2,128,2048]{2,1,0:T(8,128)(2,1)S(1)}, bf16[2,128,2048]{2,1,0:T(8,128)(2,1)}, bf16[2,128,2048]{2,1,0:T(8,128)(2,1)}, bf16[2,128,2048]{2,1,...) conditional(s32[]{:T(128)} %convert_element_type.91, () %tuple.53, ...), branch_computations={%region_2.3_spmd, %region_3.6_spmd} | conditional | flops 3222798336 | bytes 32510076 | solution.py:193
  49.3 0.6 reduce_sum.21
  50.5 0.6 dynamic_slice.16
  51.6 0.1 reduce_sum.22
  51.7 0.1 compare_convert_fusion
  51.8 0.6 broadcast_in_dim.21
  52.4 29.3 %branch_1_fun.5 = (bf16[2,128,2048]{2,1,0:T(8,128)(2,1)S(1)}, bf16[2,128,2048]{2,1,0:T(8,128)(2,1)}, bf16[2,128,2048]{2,1,0:T(8,128)(2,1)}, bf16[2,128,2048]{2,1...) custom-call(s32[1]{0:T(128)} %bitcast.1.start_ref, ...), custom_call_target="tpu_custom_call" | custom-call | flops 3221225472 | bytes 14680064 | tf_op jit(solution)/shard_map/cond/branch_1_fun/pallas_call | solution.py:120
  81.8 1.0 slice_reduce_fusion.1
  82.8 0.1 squeeze.31
  82.9 0.1 squeeze.32
  83.0 1.5 convert_element_type.75
  84.6 1.6 convert_element_type.76
  86.1 1.6 convert_element_type.77
  87.7 1.3 collective-permute-start.10
  89.0 5.4 %collective-permute-start.11 = (bf16[2,128,2048]{2,1,0:T(8,128)(2,1)}, bf16[2,128,2048]{2,1,0:T(8,128)(2,1)S(1)}, u32[]{:S(2)}, u32[]{:S(2)}) collective-permute-start(bf16[2,128,2048]{2,1,0:T(8,128)(2,1)} %get-tuple-element.247), channel_id=1, source_target_pairs={{128,136},{136,144},{144,152},{152,160},{160,168},{168,176},{176,1... | collective-permute-start | bytes 3145736 | tf_op jit(solution)/shard_map/ppermute | solution.py:163
  94.4 0.1 collective-permute-start.7
  94.5 1.1 collective-permute-done.7
  95.7 1.3 collective-permute-start.8
  97.0 1.1 collective-permute-done.8
  98.1 1.2 collective-permute-start.9
  99.3 1.2 collective-permute-done.9
  100.6 4.3 %collective-permute-done.10 = bf16[2,128,2048]{2,1,0:T(8,128)(2,1)S(1)} collective-permute-done((bf16[2,128,2048]{2,1,0:T(8,128)(2,1)}, bf16[2,128,2048]{2,1,0:T(8,128)(2,1)S(1)}, u32[]{:S(2)}, u32[]{:S(2)}) %collective-permute-start.10) | collective-permute-done | bytes 1048608 | tf_op jit(solution)/shard_map/ppermute | solution.py:163
  104.8 1.6 collective-permute-done.11
  106.4 1.9 %add_convert_fusion.2 = bf16[2,128,2048]{2,1,0:T(8,128)(2,1)S(1)} fusion(f32[2,128,2048]{2,1,0:T(8,128)} %get-tuple-element.252, bf16[2,128,2048]{2,1,0:T(8,128)(2,1)S(1)} %collective-permute-done.11), kind=kLoop, calls=%fused_computation.7 | loop fusion | flops 1572864 | bytes 4194304 | tf_op jit(solution)/shard_map/convert_element_type | solution.py:198
  108.3 4.6 %collective-permute-start.16 = (bf16[2,128,2048]{2,1,0:T(8,128)(2,1)S(1)}, bf16[2,128,2048]{2,1,0:T(8,128)(2,1)S(1)}, u32[]{:S(2)}, u32[]{:S(2)}) collective-permute-start(bf16[2,128,2048]{2,1,0:T(8,128)(2,1)S(1)} %add_convert_fusion.2), channel_id=1, source_target_pairs={{128,136},{136,144},{144,152},{152,160},{160,168},{168,176},{176,1... | collective-permute-start | bytes 3145736 | tf_op jit(solution)/shard_map/ppermute | solution.py:163
  113.0 2.8 %collective-permute-start.13 = (f32[2,32]{1,0:T(2,128)S(1)}, f32[2,32]{1,0:T(2,128)S(1)}, u32[]{:S(2)}, u32[]{:S(2)}) collective-permute-start(f32[2,32]{1,0:T(2,128)S(1)} %add.77), channel_id=1, source_target_pairs={{0,4},{1,5},{2,6},{3,7},{4,0},{5,1},{6,2},{7,3},{8,12},{9,13},{10,... | collective-permute-start | bytes 776 | tf_op jit(solution)/shard_map/ppermute | solution.py:136
  115.8 1.2 collective-permute-done.13
  117.0 2.6 %collective-permute-start.14 = (f32[2,32]{1,0:T(2,128)S(1)}, f32[2,32]{1,0:T(2,128)S(1)}, u32[]{:S(2)}, u32[]{:S(2)}) collective-permute-start(f32[2,32]{1,0:T(2,128)S(1)} %add.80), channel_id=1, source_target_pairs={{0,8},{8,0},{16,24},{24,16},{32,40},{40,32},{48,56},{56,48},{64,72... | collective-permute-start | bytes 776 | tf_op jit(solution)/shard_map/ppermute | solution.py:136
  119.6 2.3 %collective-permute-start.6 = (bf16[2,128,2048]{2,1,0:T(8,128)(2,1)}, bf16[2,128,2048]{2,1,0:T(8,128)(2,1)}, u32[]{:S(2)}, u32[]{:S(2)}) collective-permute-start(bf16[2,128,2048]{2,1,0:T(8,128)(2,1)} %get-tuple-element.244), channel_id=1, source_target_pairs={{128,0},{136,8},{144,16},{152,24},{160,32},{168,40},{176,48},{184,... | collective-permute-start | bytes 3145736 | tf_op jit(solution)/shard_map/ppermute | solution.py:163
  121.9 2.8 %collective-permute-done.14 = f32[2,32]{1,0:T(2,128)S(1)} collective-permute-done((f32[2,32]{1,0:T(2,128)S(1)}, f32[2,32]{1,0:T(2,128)S(1)}, u32[]{:S(2)}, u32[]{:S(2)}) %collective-permute-start.14) | collective-permute-done | bytes 288 | tf_op jit(solution)/shard_map/ppermute | solution.py:136
  124.7 5.0 %collective-permute-start.15 = (f32[2,32]{1,0:T(2,128)S(1)}, f32[2,32]{1,0:T(2,128)S(1)}, u32[]{:S(2)}, u32[]{:S(2)}) collective-permute-start(f32[2,32]{1,0:T(2,128)S(1)} %add.81), channel_id=1, source_target_pairs={{0,16},{8,24},{16,0},{24,8},{32,48},{40,56},{48,32},{56,40},{64,80... | collective-permute-start | bytes 776 | tf_op jit(solution)/shard_map/ppermute | solution.py:136
  129.7 1.3 add_convert_fusion.3
  131.1 0.7 collective-permute-start.12
  131.8 0.0 collective-permute-done.15
  131.8 0.0 collective-permute-done.16
  131.8 0.0 copy-start.2
  131.8 2.9 %add_convert_fusion.1 = bf16[2,128,2048]{2,1,0:T(8,128)(2,1)} fusion(f32[2,128,2048]{2,1,0:T(8,128)} %get-tuple-element.254, bf16[2,128,2048]{2,1,0:T(8,128)(2,1)S(1)} %collective-permute-done.16), kind=kLoop, calls=%fused_computation.6 | loop fusion | flops 1572864 | bytes 4194304 | tf_op jit(solution)/shard_map/convert_element_type | solution.py:198
  134.7 1.3 collective-permute-start.17
  136.1 14.5 %collective-permute-start.18 = (f32[2,32]{1,0:T(2,128)S(1)}, f32[2,32]{1,0:T(2,128)S(1)}, u32[]{:S(2)}, u32[]{:S(2)}) collective-permute-start(f32[2,32]{1,0:T(2,128)S(1)} %add.82), channel_id=1, source_target_pairs={{0,32},{8,40},{16,48},{24,56},{32,0},{40,8},{48,16},{56,24},{64,96... | collective-permute-start | bytes 776 | tf_op jit(solution)/shard_map/ppermute | solution.py:136
  150.6 12.2 %collective-permute-done.18 = f32[2,32]{1,0:T(2,128)S(1)} collective-permute-done((f32[2,32]{1,0:T(2,128)S(1)}, f32[2,32]{1,0:T(2,128)S(1)}, u32[]{:S(2)}, u32[]{:S(2)}) %collective-permute-start.18) | collective-permute-done | bytes 288 | tf_op jit(solution)/shard_map/ppermute | solution.py:136
  162.9 2.2 %collective-permute-start.19 = (f32[2,32]{1,0:T(2,128)S(1)}, f32[2,32]{1,0:T(2,128)S(1)}, u32[]{:S(2)}, u32[]{:S(2)}) collective-permute-start(f32[2,32]{1,0:T(2,128)S(1)} %add.86), channel_id=1, source_target_pairs={{0,64},{8,72},{16,80},{24,88},{32,96},{40,104},{48,112},{56,120},{... | collective-permute-start | bytes 776 | tf_op jit(solution)/shard_map/ppermute | solution.py:136
  165.0 1.7 %collective-permute-done.19 = f32[2,32]{1,0:T(2,128)S(1)} collective-permute-done((f32[2,32]{1,0:T(2,128)S(1)}, f32[2,32]{1,0:T(2,128)S(1)}, u32[]{:S(2)}, u32[]{:S(2)}) %collective-permute-start.19) | collective-permute-done | bytes 288 | tf_op jit(solution)/shard_map/ppermute | solution.py:136
  166.8 0.5 fusion.3
  167.3 0.0 collective-permute-done.6
  167.3 0.0 collective-permute-done.12
  167.3 3.0 %fusion.1 = bf16[1,2,128,2048]{3,2,1,0:T(8,128)(2,1)} fusion(bf16[2,128,2048]{2,1,0:T(8,128)(2,1)S(1)} %get-tuple-element.255, bf16[2,128,2048]{2,1,0:T(8,128)(2,1)S(1)} %collective-permute-done.17, bf16[2,128,2048]{2,1,0:T(8,128)(2,1)S(1)} %collective-permute-done.12, bf16[2,128,2048]{2,1,0:T(8,128)(2,1)} %collective-permute-done.6, pred[]{:T(512)S(6)} %eq.23), kind=kLoop, calls=%fused_computation.10 | loop fusion | flops 3670016 | bytes 5242881 | tf_op jit(solution)/shard_map/broadcast_in_dim | solution.py:219
  (19 shorter events, 0.1 us)
Async XLA Ops:
  0.6 17.0 %collective-permute-start.3 = (bf16[2,128,2048]{2,1,0:T(8,128)(2,1)}, bf16[2,128,2048]{2,1,0:T(8,128)(2,1)S(1)}, u32[]{:S(2)}, u32[]{:S(2)}) collective-permute-start(bf16[2,128,2048]{2,1,0:T(8,128)(2,1)} %bitcast.17), channel_id=1, source_target_pairs={{8,128},{16,136},{24,144},{32,152},{40,160},{48,168},{56,176},{64,... | collective-permute-start | bytes 3145736 | tf_op jit(solution)/shard_map/ppermute | solution.py:163
  1.9 18.3 %collective-permute-start = (bf16[2,128,2048]{2,1,0:T(8,128)(2,1)}, bf16[2,128,2048]{2,1,0:T(8,128)(2,1)S(1)}, u32[]{:S(2)}, u32[]{:S(2)}) collective-permute-start(bf16[2,128,2048]{2,1,0:T(8,128)(2,1)} %bitcast.18), channel_id=1, source_target_pairs={{0,136},{8,144},{16,152},{24,160},{32,168},{40,176},{48,184},{56,1... | collective-permute-start | bytes 3145736 | tf_op jit(solution)/shard_map/ppermute | solution.py:163
  17.6 17.2 %copy-start.3 = (bf16[2,128,2048]{2,1,0:T(8,128)(2,1)}, bf16[2,128,2048]{2,1,0:T(8,128)(2,1)S(1)}, u32[]{:S(2)}) copy-start(bf16[2,128,2048]{2,1,0:T(8,128)(2,1)S(1)} %collective-permute-done.3) | copy-start | bytes 3145732
  17.6 15.9 %collective-permute-start.4 = (bf16[2,128,2048]{2,1,0:T(8,128)(2,1)S(1)}, bf16[2,128,2048]{2,1,0:T(8,128)(2,1)S(1)}, u32[]{:S(2)}, u32[]{:S(2)}) collective-permute-start(bf16[2,128,2048]{2,1,0:T(8,128)(2,1)S(1)} %collective-permute-done.3), channel_id=1, source_target_pairs={{136,128},{144,136},{152,144},{160,152},{168,160},{176,168},{184,1... | collective-permute-start | bytes 3145736 | tf_op jit(solution)/shard_map/ppermute | solution.py:163
  18.9 18.5 %collective-permute-start.2 = (bf16[2,128,2048]{2,1,0:T(8,128)(2,1)}, bf16[2,128,2048]{2,1,0:T(8,128)(2,1)}, u32[]{:S(2)}, u32[]{:S(2)}) collective-permute-start(bf16[2,128,2048]{2,1,0:T(8,128)(2,1)} %bitcast.19), channel_id=1, source_target_pairs={{0,128},{8,136},{16,144},{24,152},{32,160},{40,168},{48,176},{56,1... | collective-permute-start | bytes 3145736 | tf_op jit(solution)/shard_map/ppermute | solution.py:163
  20.2 17.2 %collective-permute-start.1 = (bf16[2,128,2048]{2,1,0:T(8,128)(2,1)S(1)}, bf16[2,128,2048]{2,1,0:T(8,128)(2,1)}, u32[]{:S(2)}, u32[]{:S(2)}) collective-permute-start(bf16[2,128,2048]{2,1,0:T(8,128)(2,1)S(1)} %collective-permute-done), channel_id=1, source_target_pairs={{128,136},{136,144},{144,152},{152,160},{160,168},{168,176},{176,1... | collective-permute-start | bytes 3145736 | tf_op jit(solution)/shard_map/ppermute | solution.py:163
  33.5 15.8 %collective-permute-start.5 = (bf16[2,128,2048]{2,1,0:T(8,128)(2,1)S(1)}, bf16[2,128,2048]{2,1,0:T(8,128)(2,1)}, u32[]{:S(2)}, u32[]{:S(2)}) collective-permute-start(bf16[2,128,2048]{2,1,0:T(8,128)(2,1)S(1)} %collective-permute-done.4), channel_id=1, source_target_pairs={{136,128},{144,136},{152,144},{160,152},{168,160},{176,168},{184,1... | collective-permute-start | bytes 3145736 | tf_op jit(solution)/shard_map/ppermute | solution.py:163
  83.0 1.6 copy-start.1
  84.5 1.6 copy-start
  87.7 17.1 %collective-permute-start.10 = (bf16[2,128,2048]{2,1,0:T(8,128)(2,1)}, bf16[2,128,2048]{2,1,0:T(8,128)(2,1)S(1)}, u32[]{:S(2)}, u32[]{:S(2)}) collective-permute-start(bf16[2,128,2048]{2,1,0:T(8,128)(2,1)} %get-tuple-element.246), channel_id=1, source_target_pairs={{136,128},{144,136},{152,144},{160,152},{168,160},{176,168},{184,1... | collective-permute-start | bytes 3145736 | tf_op jit(solution)/shard_map/ppermute | solution.py:163
  89.0 17.4 %collective-permute-start.11 = (bf16[2,128,2048]{2,1,0:T(8,128)(2,1)}, bf16[2,128,2048]{2,1,0:T(8,128)(2,1)S(1)}, u32[]{:S(2)}, u32[]{:S(2)}) collective-permute-start(bf16[2,128,2048]{2,1,0:T(8,128)(2,1)} %get-tuple-element.247), channel_id=1, source_target_pairs={{128,136},{136,144},{144,152},{152,160},{160,168},{168,176},{176,1... | collective-permute-start | bytes 3145736 | tf_op jit(solution)/shard_map/ppermute | solution.py:163
  94.4 1.2 collective-permute-start.7
  95.7 2.4 %collective-permute-start.8 = (f32[2,32]{1,0:T(2,128)S(1)}, f32[2,32]{1,0:T(2,128)S(1)}, u32[]{:S(2)}, u32[]{:S(2)}) collective-permute-start(f32[2,32]{1,0:T(2,128)S(1)} %add.75), channel_id=1, source_target_pairs={{0,1},{1,0},{2,3},{3,2},{4,5},{5,4},{6,7},{7,6},{8,9},{9,8},{10,11... | collective-permute-start | bytes 776 | tf_op jit(solution)/shard_map/ppermute | solution.py:136
  98.1 2.4 %collective-permute-start.9 = (f32[2,32]{1,0:T(2,128)S(1)}, f32[2,32]{1,0:T(2,128)S(1)}, u32[]{:S(2)}, u32[]{:S(2)}) collective-permute-start(f32[2,32]{1,0:T(2,128)S(1)} %add.76), channel_id=1, source_target_pairs={{0,2},{1,3},{2,0},{3,1},{4,6},{5,7},{6,4},{7,5},{8,10},{9,11},{10,... | collective-permute-start | bytes 776 | tf_op jit(solution)/shard_map/ppermute | solution.py:136
  108.3 23.5 %collective-permute-start.16 = (bf16[2,128,2048]{2,1,0:T(8,128)(2,1)S(1)}, bf16[2,128,2048]{2,1,0:T(8,128)(2,1)S(1)}, u32[]{:S(2)}, u32[]{:S(2)}) collective-permute-start(bf16[2,128,2048]{2,1,0:T(8,128)(2,1)S(1)} %add_convert_fusion.2), channel_id=1, source_target_pairs={{128,136},{136,144},{144,152},{152,160},{160,168},{168,176},{176,1... | collective-permute-start | bytes 3145736 | tf_op jit(solution)/shard_map/ppermute | solution.py:163
  113.0 4.0 %collective-permute-start.13 = (f32[2,32]{1,0:T(2,128)S(1)}, f32[2,32]{1,0:T(2,128)S(1)}, u32[]{:S(2)}, u32[]{:S(2)}) collective-permute-start(f32[2,32]{1,0:T(2,128)S(1)} %add.77), channel_id=1, source_target_pairs={{0,4},{1,5},{2,6},{3,7},{4,0},{5,1},{6,2},{7,3},{8,12},{9,13},{10,... | collective-permute-start | bytes 776 | tf_op jit(solution)/shard_map/ppermute | solution.py:136
  117.0 7.7 %collective-permute-start.14 = (f32[2,32]{1,0:T(2,128)S(1)}, f32[2,32]{1,0:T(2,128)S(1)}, u32[]{:S(2)}, u32[]{:S(2)}) collective-permute-start(f32[2,32]{1,0:T(2,128)S(1)} %add.80), channel_id=1, source_target_pairs={{0,8},{8,0},{16,24},{24,16},{32,40},{40,32},{48,56},{56,48},{64,72... | collective-permute-start | bytes 776 | tf_op jit(solution)/shard_map/ppermute | solution.py:136
  119.6 47.7 %collective-permute-start.6 = (bf16[2,128,2048]{2,1,0:T(8,128)(2,1)}, bf16[2,128,2048]{2,1,0:T(8,128)(2,1)}, u32[]{:S(2)}, u32[]{:S(2)}) collective-permute-start(bf16[2,128,2048]{2,1,0:T(8,128)(2,1)} %get-tuple-element.244), channel_id=1, source_target_pairs={{128,0},{136,8},{144,16},{152,24},{160,32},{168,40},{176,48},{184,... | collective-permute-start | bytes 3145736 | tf_op jit(solution)/shard_map/ppermute | solution.py:163
  124.7 7.1 %collective-permute-start.15 = (f32[2,32]{1,0:T(2,128)S(1)}, f32[2,32]{1,0:T(2,128)S(1)}, u32[]{:S(2)}, u32[]{:S(2)}) collective-permute-start(f32[2,32]{1,0:T(2,128)S(1)} %add.81), channel_id=1, source_target_pairs={{0,16},{8,24},{16,0},{24,8},{32,48},{40,56},{48,32},{56,40},{64,80... | collective-permute-start | bytes 776 | tf_op jit(solution)/shard_map/ppermute | solution.py:136
  131.1 36.3 %collective-permute-start.12 = (bf16[2,128,2048]{2,1,0:T(8,128)(2,1)}, bf16[2,128,2048]{2,1,0:T(8,128)(2,1)S(1)}, u32[]{:S(2)}, u32[]{:S(2)}) collective-permute-start(bf16[2,128,2048]{2,1,0:T(8,128)(2,1)} %add_convert_fusion.3), channel_id=1, source_target_pairs={{136,0},{144,8},{152,16},{160,24},{168,32},{176,40},{184,48},{192,... | collective-permute-start | bytes 3145736 | tf_op jit(solution)/shard_map/ppermute | solution.py:163
  131.8 35.0 %copy-start.2 = (f32[2,32]{1,0:T(2,128)S(1)}, f32[2,32]{1,0:T(2,128)}, u32[]{:S(2)}) copy-start(f32[2,32]{1,0:T(2,128)} %param.6) | copy-start | bytes 772
  134.7 32.6 %collective-permute-start.17 = (bf16[2,128,2048]{2,1,0:T(8,128)(2,1)}, bf16[2,128,2048]{2,1,0:T(8,128)(2,1)S(1)}, u32[]{:S(2)}, u32[]{:S(2)}) collective-permute-start(bf16[2,128,2048]{2,1,0:T(8,128)(2,1)} %add_convert_fusion.1), channel_id=1, source_target_pairs={{128,8},{136,16},{144,24},{152,32},{160,40},{168,48},{176,56},{184... | collective-permute-start | bytes 3145736 | tf_op jit(solution)/shard_map/ppermute | solution.py:163
  136.1 26.8 %collective-permute-start.18 = (f32[2,32]{1,0:T(2,128)S(1)}, f32[2,32]{1,0:T(2,128)S(1)}, u32[]{:S(2)}, u32[]{:S(2)}) collective-permute-start(f32[2,32]{1,0:T(2,128)S(1)} %add.82), channel_id=1, source_target_pairs={{0,32},{8,40},{16,48},{24,56},{32,0},{40,8},{48,16},{56,24},{64,96... | collective-permute-start | bytes 776 | tf_op jit(solution)/shard_map/ppermute | solution.py:136
  162.9 3.9 %collective-permute-start.19 = (f32[2,32]{1,0:T(2,128)S(1)}, f32[2,32]{1,0:T(2,128)S(1)}, u32[]{:S(2)}, u32[]{:S(2)}) collective-permute-start(f32[2,32]{1,0:T(2,128)S(1)} %add.86), channel_id=1, source_target_pairs={{0,64},{8,72},{16,80},{24,88},{32,96},{40,104},{48,112},{56,120},{... | collective-permute-start | bytes 776 | tf_op jit(solution)/shard_map/ppermute | solution.py:136

commit v5 on v4

--- a/solution.py
+++ b/solution.py
@@ -12,6 +12,7 @@
 REACH_LOW = 2
 REACH_HIGH = 3
 WINDOW = REACH_LOW + REACH_HIGH + 1
+RING = 8
 
 masked_score = -1e30
 
@@ -131,6 +132,29 @@
     return produced, grads, terms
 
 
+def ring_shift(value, steps):
+    count = lax.axis_size("seq")
+    pairs = []
+    for source in range(count):
+        base = source - source % RING
+        pairs.append((source, base + (source - steps) % RING))
+    return lax.ppermute(value, "seq", pairs)
+
+
+def ring_total(value, shard_index):
+    gathered = value[None]
+    gathered = jnp.concatenate([gathered, ring_shift(gathered, 1)], axis=0)
+    gathered = jnp.concatenate([gathered, ring_shift(gathered, 2)], axis=0)
+    while gathered.shape[0] < RING:
+        have = gathered.shape[0]
+        gathered = jnp.concatenate([gathered, ring_shift(gathered, 2)[have - 2 : have]], axis=0)
+    ordered = jnp.roll(gathered, shard_index % RING, axis=0)
+    total = ordered[0]
+    for index in range(1, RING):
+        total = total + ordered[index]
+    return total
+
+
 def exchange_add(value, axis, stride):
     count = lax.axis_size(axis)
     return value + lax.ppermute(value, axis, [(i, i ^ stride) for i in range(count)])
@@ -202,14 +226,14 @@
     back_minus = across(grads[0], [(dec(s + 1), dec(s)) for s in lower])
     back_plus = across(grads[5], [(dec(s - 1), dec(s)) for s in upper])
     own_sum = across(grads[2], [(dec(s), enc(s)) for s in range(count)])
-    summed = exchange_add(exchange_add(summed, "dp", 1), "dp", 2)
+    summed = exchange_add(exchange_add(exchange_add(summed, "dp", 1), "dp", 2), "dp", 4)
     summed, back_minus, back_plus = lax.optimization_barrier((summed, back_minus, back_plus))
     minus_sum = across(added(back_minus, grads[1]), [(dec(s + 1), enc(s)) for s in lower])
     back_plus = across(added(back_plus, grads[4]), [(dec(s - 1), dec(s)) for s in upper])
-    summed = exchange_add(exchange_add(exchange_add(summed, "dp", 4), "seq", 1), "seq", 2)
+    summed = exchange_add(summed, "seq", RING)
     summed, back_plus = lax.optimization_barrier((summed, back_plus))
     plus_sum = across(added(back_plus, grads[3]), [(dec(s - 1), enc(s)) for s in upper])
-    summed = exchange_add(exchange_add(summed, "seq", 4), "seq", 8)
+    summed = ring_total(summed, shard_index)
     returned = (
         own_sum.astype(jnp.float32) + minus_sum.astype(jnp.float32) + plus_sum.astype(jnp.float32)
     ).astype(jnp.bfloat16)

time: 171 us -> 181 us (1.058)
  the two profiles are of different devices: /device:TPU:1 before, /device:TPU:58 now
where the time goes in v5:
time: 181 us; the launch traced here: 180 us
  starting transfers between devices  112 us (62%)
  waiting for transfers between devices  49.2 us (27%)
  other arithmetic  10.6 us (6%)
  local copies, waits for them, and re-layouts  7.71 us (4%)
    ppermute x5, starting transfers between devices, exchange_add(): lax.ppermute(value, axis, [(i, i ^ stride) for i in range(count)])  68.1 us
    ppermute x12, waiting for transfers between devices, across(): return lax.ppermute(value, ('phase', 'seq'), pairs)  32.7 us
    ppermute x12, starting transfers between devices, across(): return lax.ppermute(value, ('phase', 'seq'), pairs)  22.6 us
    ppermute x4, starting transfers between devices, ring_shift(): return lax.ppermute(value, 'seq', pairs)  20.9 us
    ppermute x5, waiting for transfers between devices, exchange_add(): lax.ppermute(value, axis, [(i, i ^ stride) for i in range(count)])  12.6 us
    another operation x9, local copies, waits for them, and re-layouts  7.62 us
    convert_element_type x3, other arithmetic, added(): return (a.astype(jnp.float32) + b.astype(jnp.float32)).astype(jnp.bfloat16)  6.52 us
    ppermute x4, waiting for transfers between devices, ring_shift(): return lax.ppermute(value, 'seq', pairs)  3.92 us
  transfers between devices with their start and end apart: 21, of which 10 were waited for; matrix products, arithmetic and copies ran while one was open for 4% of the time, Pallas kernels for 0%

profile of v5, /device:TPU:58, one launch (start us, length us, event | category | flops | bytes accessed | tf_op | source)
XLA Modules:
  0.0 180.0 jit_solution(4622358252121617963)
XLA Ops:
  0.6 1.5 collective-permute-start.3
  2.2 3.1 %collective-permute-start = (bf16[2,128,2048]{2,1,0:T(8,128)(2,1)}, bf16[2,128,2048]{2,1,0:T(8,128)(2,1)S(1)}, u32[]{:S(2)}, u32[]{:S(2)}) collective-permute-start(bf16[2,128,2048]{2,1,0:T(8,128)(2,1)} %bitcast.29), channel_id=1, source_target_pairs={{0,136},{8,144},{16,152},{24,160},{32,168},{40,176},{48,184},{56,1... | collective-permute-start | bytes 3145736 | tf_op jit(solution)/shard_map/ppermute | solution.py:187
  5.3 9.4 %collective-permute-done.3 = bf16[2,128,2048]{2,1,0:T(8,128)(2,1)S(1)} collective-permute-done((bf16[2,128,2048]{2,1,0:T(8,128)(2,1)}, bf16[2,128,2048]{2,1,0:T(8,128)(2,1)S(1)}, u32[]{:S(2)}, u32[]{:S(2)}) %collective-permute-start.3) | collective-permute-done | bytes 1048608 | tf_op jit(solution)/shard_map/ppermute | solution.py:187
  14.7 0.0 copy-start.3
  14.7 0.7 collective-permute-start.4
  15.4 6.2 %collective-permute-start.2 = (bf16[2,128,2048]{2,1,0:T(8,128)(2,1)}, bf16[2,128,2048]{2,1,0:T(8,128)(2,1)}, u32[]{:S(2)}, u32[]{:S(2)}) collective-permute-start(bf16[2,128,2048]{2,1,0:T(8,128)(2,1)} %bitcast.30), channel_id=1, source_target_pairs={{0,128},{8,136},{16,144},{24,152},{32,160},{40,168},{48,176},{56,1... | collective-permute-start | bytes 3145736 | tf_op jit(solution)/shard_map/ppermute | solution.py:187
  21.6 0.0 collective-permute-done
  21.6 1.6 collective-permute-start.1
  23.3 0.0 collective-permute-done.4
  23.3 1.7 collective-permute-start.5
  24.9 0.0 copy-done.3
  24.9 0.8 slice_bitcast_fusion.1
  25.7 0.2 reduce-window.8
  25.9 0.2 reduce-window_1_clone.1
  26.0 0.7 bitcast_subtract_fusion
  26.7 0.7 compare_convert_fusion.2
  27.4 0.1 compare_convert_fusion.1
  27.5 0.0 collective-permute-done.2
  27.5 0.0 collective-permute-done.1
  27.5 0.0 collective-permute-done.5
  27.5 6.9 %conditional.1 = (bf16[2,128,2048]{2,1,0:T(8,128)(2,1)S(1)}, bf16[2,128,2048]{2,1,0:T(8,128)(2,1)}, bf16[2,128,2048]{2,1,0:T(8,128)(2,1)}, bf16[2,128,2048]{2,1,...) conditional(s32[]{:T(128)} %convert_element_type.91, () %tuple.51, ...), branch_computations={%region_2.3_spmd, %region_3.6_spmd} | conditional | flops 3222798336 | bytes 32510076 | solution.py:217
  27.5 0.2 broadcast.51
  27.7 1.6 broadcast.51.clone
  29.3 1.6 broadcast.51.clone.1
  30.9 0.1 broadcast.49
  31.0 1.1 broadcast.49.clone
  32.1 1.2 broadcast.49.clone.1
  33.3 1.1 broadcast.49.clone.2
  34.4 1.6 collective-permute-start.11
  36.0 0.7 collective-permute-start.12
  36.7 65.3 %collective-permute-start.7 = (f32[2,32]{1,0:T(2,128)S(1)}, f32[2,32]{1,0:T(2,128)S(1)}, u32[]{:S(2)}, u32[]{:S(2)}) collective-permute-start(f32[2,32]{1,0:T(2,128)S(1)} %get-tuple-element.251), channel_id=1, source_target_pairs={{0,128},{128,0},{1,129},{129,1},{2,130},{130,2},{3,131},{131,3},{4... | collective-permute-start | bytes 776 | tf_op jit(solution)/shard_map/ppermute | solution.py:160
  102.1 0.8 collective-permute-done.7
  102.9 0.0 collective-permute-start.8
  102.9 3.6 %collective-permute-done.8 = f32[2,32]{1,0:T(2,128)S(1)} collective-permute-done((f32[2,32]{1,0:T(2,128)S(1)}, f32[2,32]{1,0:T(2,128)S(1)}, u32[]{:S(2)}, u32[]{:S(2)}) %collective-permute-start.8) | collective-permute-done | bytes 288 | tf_op jit(solution)/shard_map/ppermute | solution.py:160
  106.5 0.5 collective-permute-start.9
  107.0 3.0 %collective-permute-done.9 = f32[2,32]{1,0:T(2,128)S(1)} collective-permute-done((f32[2,32]{1,0:T(2,128)S(1)}, f32[2,32]{1,0:T(2,128)S(1)}, u32[]{:S(2)}, u32[]{:S(2)}) %collective-permute-start.9) | collective-permute-done | bytes 288 | tf_op jit(solution)/shard_map/ppermute | solution.py:160
  110.1 2.1 %collective-permute-start.10 = (f32[2,32]{1,0:T(2,128)S(1)}, f32[2,32]{1,0:T(2,128)S(1)}, u32[]{:S(2)}, u32[]{:S(2)}) collective-permute-start(f32[2,32]{1,0:T(2,128)S(1)} %add.109), channel_id=1, source_target_pairs={{0,4},{1,5},{2,6},{3,7},{4,0},{5,1},{6,2},{7,3},{8,12},{9,13},{10,... | collective-permute-start | bytes 776 | tf_op jit(solution)/shard_map/ppermute | solution.py:160
  112.2 3.0 %collective-permute-done.10 = f32[2,32]{1,0:T(2,128)S(1)} collective-permute-done((f32[2,32]{1,0:T(2,128)S(1)}, f32[2,32]{1,0:T(2,128)S(1)}, u32[]{:S(2)}, u32[]{:S(2)}) %collective-permute-start.10) | collective-permute-done | bytes 288 | tf_op jit(solution)/shard_map/ppermute | solution.py:160
  115.1 0.0 collective-permute-done.11
  115.1 0.0 collective-permute-done.12
  115.1 2.9 %add_convert_fusion.2 = bf16[2,128,2048]{2,1,0:T(8,128)(2,1)} fusion(f32[2,128,2048]{2,1,0:T(8,128)} %get-tuple-element.258, bf16[2,128,2048]{2,1,0:T(8,128)(2,1)S(1)} %collective-permute-done.12), kind=kLoop, calls=%fused_computation.7 | loop fusion | flops 1572864 | bytes 4194304 | tf_op jit(solution)/shard_map/convert_element_type | solution.py:222
  118.0 1.6 collective-permute-start.15
  119.6 1.3 collective-permute-start.6
  120.9 0.1 collective-permute-start.14
  121.0 1.5 add_convert_fusion.3
  122.5 1.3 collective-permute-start.13
  123.8 2.3 %collective-permute-done.14 = f32[2,32]{1,0:T(2,128)S(1)} collective-permute-done((f32[2,32]{1,0:T(2,128)S(1)}, f32[2,32]{1,0:T(2,128)S(1)}, u32[]{:S(2)}, u32[]{:S(2)}) %collective-permute-start.14) | collective-permute-done | bytes 288 | tf_op jit(solution)/shard_map/ppermute | solution.py:160
  126.1 0.0 collective-permute-done.15
  126.1 5.9 %collective-permute-start.17 = (f32[1,2,32]{2,1,0:T(2,128)S(1)}, f32[1,2,32]{2,1,0:T(2,128)S(1)}, u32[]{:S(2)}, u32[]{:S(2)}) collective-permute-start(f32[1,2,32]{2,1,0:T(2,128)S(1)} %bitcast.23), channel_id=1, source_target_pairs={{0,56},{8,0},{16,8},{24,16},{32,24},{40,32},{48,40},{56,48},{64,12... | collective-permute-start | bytes 776 | tf_op jit(solution)/shard_map/ppermute | solution.py:141
  132.0 1.3 collective-permute-done.17
  133.3 6.1 %collective-permute-start.18 = (f32[2,2,32]{2,1,0:T(2,128)S(1)}, f32[2,2,32]{2,1,0:T(2,128)S(1)}, u32[]{:S(2)}, u32[]{:S(2)}) collective-permute-start(f32[2,2,32]{2,1,0:T(2,128)S(1)} %pad_maximum_fusion.3), channel_id=1, source_target_pairs={{0,48},{8,56},{16,0},{24,8},{32,16},{40,24},{48,32},{56,40},{64,11... | collective-permute-start | bytes 1544 | tf_op jit(solution)/shard_map/ppermute | solution.py:141
  139.4 1.3 collective-permute-done.18
  140.7 4.4 %collective-permute-start.19 = (f32[4,2,32]{2,1,0:T(2,128)S(1)}, f32[4,2,32]{2,1,0:T(2,128)S(1)}, u32[]{:S(2)}, u32[]{:S(2)}) collective-permute-start(f32[4,2,32]{2,1,0:T(2,128)S(1)} %pad_maximum_fusion.2), channel_id=1, source_target_pairs={{0,48},{8,56},{16,0},{24,8},{32,16},{40,24},{48,32},{56,40},{64,11... | collective-permute-start | bytes 3080 | tf_op jit(solution)/shard_map/ppermute | solution.py:141
  145.2 1.3 collective-permute-done.19
  146.5 4.5 %collective-permute-start.20 = (f32[6,2,32]{2,1,0:T(2,128)S(1)}, f32[6,2,32]{2,1,0:T(2,128)S(1)}, u32[]{:S(2)}, u32[]{:S(2)}) collective-permute-start(f32[6,2,32]{2,1,0:T(2,128)S(1)} %pad_maximum_fusion.1), channel_id=1, source_target_pairs={{0,48},{8,56},{16,0},{24,8},{32,16},{40,24},{48,32},{56,40},{64,11... | collective-permute-start | bytes 4616 | tf_op jit(solution)/shard_map/ppermute | solution.py:141
  151.0 2.1 %add_convert_fusion.1 = bf16[2,128,2048]{2,1,0:T(8,128)(2,1)S(1)} fusion(f32[2,128,2048]{2,1,0:T(8,128)} %get-tuple-element.260, bf16[2,128,2048]{2,1,0:T(8,128)(2,1)} %collective-permute-done.15), kind=kLoop, calls=%fused_computation.6 | loop fusion | flops 1572864 | bytes 4194304 | tf_op jit(solution)/shard_map/convert_element_type | solution.py:222
  153.1 1.3 collective-permute-start.16
  154.4 0.0 collective-permute-done.20
  154.5 0.0 copy-done.2
  154.5 0.5 fusion.10
  155.1 0.0 collective-permute-done.6
  155.1 0.0 collective-permute-done.13
  155.1 23.2 %collective-permute-done.16 = bf16[2,128,2048]{2,1,0:T(8,128)(2,1)S(1)} collective-permute-done((bf16[2,128,2048]{2,1,0:T(8,128)(2,1)S(1)}, bf16[2,128,2048]{2,1,0:T(8,128)(2,1)S(1)}, u32[]{:S(2)}, u32[]{:S(2)}) %collective-permute-start.16) | collective-permute-done | bytes 1048608 | tf_op jit(solution)/shard_map/ppermute | solution.py:187
  178.3 1.7 fusion.1
  (22 shorter events, 0.1 us)
Async XLA Ops:
  0.6 14.1 %collective-permute-start.3 = (bf16[2,128,2048]{2,1,0:T(8,128)(2,1)}, bf16[2,128,2048]{2,1,0:T(8,128)(2,1)S(1)}, u32[]{:S(2)}, u32[]{:S(2)}) collective-permute-start(bf16[2,128,2048]{2,1,0:T(8,128)(2,1)} %bitcast.28), channel_id=1, source_target_pairs={{8,128},{16,136},{24,144},{32,152},{40,160},{48,168},{56,176},{64,... | collective-permute-start | bytes 3145736 | tf_op jit(solution)/shard_map/ppermute | solution.py:187
  2.2 19.5 %collective-permute-start = (bf16[2,128,2048]{2,1,0:T(8,128)(2,1)}, bf16[2,128,2048]{2,1,0:T(8,128)(2,1)S(1)}, u32[]{:S(2)}, u32[]{:S(2)}) collective-permute-start(bf16[2,128,2048]{2,1,0:T(8,128)(2,1)} %bitcast.29), channel_id=1, source_target_pairs={{0,136},{8,144},{16,152},{24,160},{32,168},{40,176},{48,184},{56,1... | collective-permute-start | bytes 3145736 | tf_op jit(solution)/shard_map/ppermute | solution.py:187
  14.7 10.2 %copy-start.3 = (bf16[2,128,2048]{2,1,0:T(8,128)(2,1)}, bf16[2,128,2048]{2,1,0:T(8,128)(2,1)S(1)}, u32[]{:S(2)}) copy-start(bf16[2,128,2048]{2,1,0:T(8,128)(2,1)S(1)} %collective-permute-done.3) | copy-start | bytes 3145732
  14.7 8.6 %collective-permute-start.4 = (bf16[2,128,2048]{2,1,0:T(8,128)(2,1)S(1)}, bf16[2,128,2048]{2,1,0:T(8,128)(2,1)S(1)}, u32[]{:S(2)}, u32[]{:S(2)}) collective-permute-start(bf16[2,128,2048]{2,1,0:T(8,128)(2,1)S(1)} %collective-permute-done.3), channel_id=1, source_target_pairs={{136,128},{144,136},{152,144},{160,152},{168,160},{176,168},{184,1... | collective-permute-start | bytes 3145736 | tf_op jit(solution)/shard_map/ppermute | solution.py:187
  15.4 12.1 %collective-permute-start.2 = (bf16[2,128,2048]{2,1,0:T(8,128)(2,1)}, bf16[2,128,2048]{2,1,0:T(8,128)(2,1)}, u32[]{:S(2)}, u32[]{:S(2)}) collective-permute-start(bf16[2,128,2048]{2,1,0:T(8,128)(2,1)} %bitcast.30), channel_id=1, source_target_pairs={{0,128},{8,136},{16,144},{24,152},{32,160},{40,168},{48,176},{56,1... | collective-permute-start | bytes 3145736 | tf_op jit(solution)/shard_map/ppermute | solution.py:187
  21.6 5.9 %collective-permute-start.1 = (bf16[2,128,2048]{2,1,0:T(8,128)(2,1)S(1)}, bf16[2,128,2048]{2,1,0:T(8,128)(2,1)}, u32[]{:S(2)}, u32[]{:S(2)}) collective-permute-start(bf16[2,128,2048]{2,1,0:T(8,128)(2,1)S(1)} %collective-permute-done), channel_id=1, source_target_pairs={{128,136},{136,144},{144,152},{152,160},{160,168},{168,176},{176,1... | collective-permute-start | bytes 3145736 | tf_op jit(solution)/shard_map/ppermute | solution.py:187
  23.3 4.2 %collective-permute-start.5 = (bf16[2,128,2048]{2,1,0:T(8,128)(2,1)S(1)}, bf16[2,128,2048]{2,1,0:T(8,128)(2,1)}, u32[]{:S(2)}, u32[]{:S(2)}) collective-permute-start(bf16[2,128,2048]{2,1,0:T(8,128)(2,1)S(1)} %collective-permute-done.4), channel_id=1, source_target_pairs={{136,128},{144,136},{152,144},{160,152},{168,160},{176,168},{184,1... | collective-permute-start | bytes 3145736 | tf_op jit(solution)/shard_map/ppermute | solution.py:187
  34.4 80.7 %collective-permute-start.11 = (bf16[2,128,2048]{2,1,0:T(8,128)(2,1)}, bf16[2,128,2048]{2,1,0:T(8,128)(2,1)}, u32[]{:S(2)}, u32[]{:S(2)}) collective-permute-start(bf16[2,128,2048]{2,1,0:T(8,128)(2,1)} %get-tuple-element.252), channel_id=1, source_target_pairs={{136,128},{144,136},{152,144},{160,152},{168,160},{176,168},{184,1... | collective-permute-start | bytes 3145736 | tf_op jit(solution)/shard_map/ppermute | solution.py:187
  36.0 79.1 %collective-permute-start.12 = (bf16[2,128,2048]{2,1,0:T(8,128)(2,1)}, bf16[2,128,2048]{2,1,0:T(8,128)(2,1)S(1)}, u32[]{:S(2)}, u32[]{:S(2)}) collective-permute-start(bf16[2,128,2048]{2,1,0:T(8,128)(2,1)} %get-tuple-element.253), channel_id=1, source_target_pairs={{128,136},{136,144},{144,152},{152,160},{160,168},{168,176},{176,1... | collective-permute-start | bytes 3145736 | tf_op jit(solution)/shard_map/ppermute | solution.py:187
  36.7 66.2 %collective-permute-start.7 = (f32[2,32]{1,0:T(2,128)S(1)}, f32[2,32]{1,0:T(2,128)S(1)}, u32[]{:S(2)}, u32[]{:S(2)}) collective-permute-start(f32[2,32]{1,0:T(2,128)S(1)} %get-tuple-element.251), channel_id=1, source_target_pairs={{0,128},{128,0},{1,129},{129,1},{2,130},{130,2},{3,131},{131,3},{4... | collective-permute-start | bytes 776 | tf_op jit(solution)/shard_map/ppermute | solution.py:160
  102.9 3.6 %collective-permute-start.8 = (f32[2,32]{1,0:T(2,128)S(1)}, f32[2,32]{1,0:T(2,128)S(1)}, u32[]{:S(2)}, u32[]{:S(2)}) collective-permute-start(f32[2,32]{1,0:T(2,128)S(1)} %add.107), channel_id=1, source_target_pairs={{0,1},{1,0},{2,3},{3,2},{4,5},{5,4},{6,7},{7,6},{8,9},{9,8},{10,11... | collective-permute-start | bytes 776 | tf_op jit(solution)/shard_map/ppermute | solution.py:160
  106.5 3.6 %collective-permute-start.9 = (f32[2,32]{1,0:T(2,128)S(1)}, f32[2,32]{1,0:T(2,128)S(1)}, u32[]{:S(2)}, u32[]{:S(2)}) collective-permute-start(f32[2,32]{1,0:T(2,128)S(1)} %add.108), channel_id=1, source_target_pairs={{0,2},{1,3},{2,0},{3,1},{4,6},{5,7},{6,4},{7,5},{8,10},{9,11},{10,... | collective-permute-start | bytes 776 | tf_op jit(solution)/shard_map/ppermute | solution.py:160
  110.1 5.1 %collective-permute-start.10 = (f32[2,32]{1,0:T(2,128)S(1)}, f32[2,32]{1,0:T(2,128)S(1)}, u32[]{:S(2)}, u32[]{:S(2)}) collective-permute-start(f32[2,32]{1,0:T(2,128)S(1)} %add.109), channel_id=1, source_target_pairs={{0,4},{1,5},{2,6},{3,7},{4,0},{5,1},{6,2},{7,3},{8,12},{9,13},{10,... | collective-permute-start | bytes 776 | tf_op jit(solution)/shard_map/ppermute | solution.py:160
  118.0 8.1 %collective-permute-start.15 = (bf16[2,128,2048]{2,1,0:T(8,128)(2,1)}, bf16[2,128,2048]{2,1,0:T(8,128)(2,1)}, u32[]{:S(2)}, u32[]{:S(2)}) collective-permute-start(bf16[2,128,2048]{2,1,0:T(8,128)(2,1)} %add_convert_fusion.2), channel_id=1, source_target_pairs={{128,136},{136,144},{144,152},{152,160},{160,168},{168,176},{176,1... | collective-permute-start | bytes 3145736 | tf_op jit(solution)/shard_map/ppermute | solution.py:187
  119.6 35.4 %collective-permute-start.6 = (bf16[2,128,2048]{2,1,0:T(8,128)(2,1)}, bf16[2,128,2048]{2,1,0:T(8,128)(2,1)S(1)}, u32[]{:S(2)}, u32[]{:S(2)}) collective-permute-start(bf16[2,128,2048]{2,1,0:T(8,128)(2,1)} %get-tuple-element.250), channel_id=1, source_target_pairs={{128,0},{136,8},{144,16},{152,24},{160,32},{168,40},{176,48},{184,... | collective-permute-start | bytes 3145736 | tf_op jit(solution)/shard_map/ppermute | solution.py:187
  120.9 5.2 %collective-permute-start.14 = (f32[2,32]{1,0:T(2,128)S(1)}, f32[2,32]{1,0:T(2,128)S(1)}, u32[]{:S(2)}, u32[]{:S(2)}) collective-permute-start(f32[2,32]{1,0:T(2,128)S(1)} %add.110), channel_id=1, source_target_pairs={{0,64},{8,72},{16,80},{24,88},{32,96},{40,104},{48,112},{56,120},{... | collective-permute-start | bytes 776 | tf_op jit(solution)/shard_map/ppermute | solution.py:160
  122.5 32.5 %collective-permute-start.13 = (bf16[2,128,2048]{2,1,0:T(8,128)(2,1)S(1)}, bf16[2,128,2048]{2,1,0:T(8,128)(2,1)S(1)}, u32[]{:S(2)}, u32[]{:S(2)}) collective-permute-start(bf16[2,128,2048]{2,1,0:T(8,128)(2,1)S(1)} %add_convert_fusion.3), channel_id=1, source_target_pairs={{136,0},{144,8},{152,16},{160,24},{168,32},{176,40},{184,48},{192,... | collective-permute-start | bytes 3145736 | tf_op jit(solution)/shard_map/ppermute | solution.py:187
  126.1 7.2 %collective-permute-start.17 = (f32[1,2,32]{2,1,0:T(2,128)S(1)}, f32[1,2,32]{2,1,0:T(2,128)S(1)}, u32[]{:S(2)}, u32[]{:S(2)}) collective-permute-start(f32[1,2,32]{2,1,0:T(2,128)S(1)} %bitcast.23), channel_id=1, source_target_pairs={{0,56},{8,0},{16,8},{24,16},{32,24},{40,32},{48,40},{56,48},{64,12... | collective-permute-start | bytes 776 | tf_op jit(solution)/shard_map/ppermute | solution.py:141
  133.3 7.4 %collective-permute-start.18 = (f32[2,2,32]{2,1,0:T(2,128)S(1)}, f32[2,2,32]{2,1,0:T(2,128)S(1)}, u32[]{:S(2)}, u32[]{:S(2)}) collective-permute-start(f32[2,2,32]{2,1,0:T(2,128)S(1)} %pad_maximum_fusion.3), channel_id=1, source_target_pairs={{0,48},{8,56},{16,0},{24,8},{32,16},{40,24},{48,32},{56,40},{64,11... | collective-permute-start | bytes 1544 | tf_op jit(solution)/shard_map/ppermute | solution.py:141
  140.7 5.7 %collective-permute-start.19 = (f32[4,2,32]{2,1,0:T(2,128)S(1)}, f32[4,2,32]{2,1,0:T(2,128)S(1)}, u32[]{:S(2)}, u32[]{:S(2)}) collective-permute-start(f32[4,2,32]{2,1,0:T(2,128)S(1)} %pad_maximum_fusion.2), channel_id=1, source_target_pairs={{0,48},{8,56},{16,0},{24,8},{32,16},{40,24},{48,32},{56,40},{64,11... | collective-permute-start | bytes 3080 | tf_op jit(solution)/shard_map/ppermute | solution.py:141
  146.5 7.9 %collective-permute-start.20 = (f32[6,2,32]{2,1,0:T(2,128)S(1)}, f32[6,2,32]{2,1,0:T(2,128)S(1)}, u32[]{:S(2)}, u32[]{:S(2)}) collective-permute-start(f32[6,2,32]{2,1,0:T(2,128)S(1)} %pad_maximum_fusion.1), channel_id=1, source_target_pairs={{0,48},{8,56},{16,0},{24,8},{32,16},{40,24},{48,32},{56,40},{64,11... | collective-permute-start | bytes 4616 | tf_op jit(solution)/shard_map/ppermute | solution.py:141
  151.0 3.6 %copy-start.2 = (f32[2,32]{1,0:T(2,128)S(1)}, f32[2,32]{1,0:T(2,128)}, u32[]{:S(2)}) copy-start(f32[2,32]{1,0:T(2,128)} %param.6) | copy-start | bytes 772
  153.1 25.2 %collective-permute-start.16 = (bf16[2,128,2048]{2,1,0:T(8,128)(2,1)S(1)}, bf16[2,128,2048]{2,1,0:T(8,128)(2,1)S(1)}, u32[]{:S(2)}, u32[]{:S(2)}) collective-permute-start(bf16[2,128,2048]{2,1,0:T(8,128)(2,1)S(1)} %add_convert_fusion.1), channel_id=1, source_target_pairs={{128,8},{136,16},{144,24},{152,32},{160,40},{168,48},{176,56},{184... | collective-permute-start | bytes 3145736 | tf_op jit(solution)/shard_map/ppermute | solution.py:187

commit v6 on v5

--- a/solution.py
+++ b/solution.py
@@ -6,6 +6,7 @@
 from jax.experimental import pallas as pl
 from jax.experimental.pallas import tpu as pltpu
 from jax.sharding import PartitionSpec as P
+
 
 BLOCK = 128
 ENC_MOST = 4
@@ -167,7 +168,7 @@
     return jnp.where(inside, found, -1)
 
 
-def local(sections, head_gains, block_counts):
+def local_body(sections, head_gains, block_counts):
     phase_index = lax.axis_index("phase")
     shard_index = lax.axis_index("seq")
     count = lax.axis_size("seq")
@@ -177,9 +178,6 @@
     enc_counts = block_counts[0, 0]
     dec_counts = block_counts[0, 1]
 
-    def enc(s):
-        return s
-
     def dec(s):
         return count + s
 
@@ -188,9 +186,9 @@
 
     lower = range(count - 1)
     upper = range(1, count)
-    at_home = across(local_pair, [(enc(s), dec(s)) for s in range(count)])
-    minus_1 = across(local_pair, [(enc(s + 1), dec(s)) for s in lower])
-    plus_1 = across(local_pair, [(enc(s - 1), dec(s)) for s in upper])
+    at_home = across(local_pair, [(s, dec(s)) for s in range(count)])
+    minus_1 = across(local_pair, [(s + 1, dec(s)) for s in lower])
+    plus_1 = across(local_pair, [(s - 1, dec(s)) for s in upper])
     minus_2 = across(minus_1, [(dec(s + 1), dec(s)) for s in lower])
     plus_2 = across(plus_1, [(dec(s - 1), dec(s)) for s in upper])
     minus_3 = across(minus_2, [(dec(s + 1), dec(s)) for s in lower])
@@ -210,7 +208,7 @@
         return attention_block(jnp.reshape(start_block, (1,)), head_gains, own, pieces, allowed_keys)
 
     def encoder_rest(operands):
-        own, pieces = operands
+        own, _ = operands
         zeros = jnp.zeros_like(own)
         return (zeros, (zeros,) * WINDOW, jnp.zeros((2, head_count), jnp.float32))
 
@@ -225,14 +223,14 @@
     summed = exchange_add(terms, "phase", 1)
     back_minus = across(grads[0], [(dec(s + 1), dec(s)) for s in lower])
     back_plus = across(grads[5], [(dec(s - 1), dec(s)) for s in upper])
-    own_sum = across(grads[2], [(dec(s), enc(s)) for s in range(count)])
+    own_sum = across(grads[2], [(dec(s), s) for s in range(count)])
     summed = exchange_add(exchange_add(exchange_add(summed, "dp", 1), "dp", 2), "dp", 4)
     summed, back_minus, back_plus = lax.optimization_barrier((summed, back_minus, back_plus))
-    minus_sum = across(added(back_minus, grads[1]), [(dec(s + 1), enc(s)) for s in lower])
+    minus_sum = across(added(back_minus, grads[1]), [(dec(s + 1), s) for s in lower])
     back_plus = across(added(back_plus, grads[4]), [(dec(s - 1), dec(s)) for s in upper])
     summed = exchange_add(summed, "seq", RING)
     summed, back_plus = lax.optimization_barrier((summed, back_plus))
-    plus_sum = across(added(back_plus, grads[3]), [(dec(s - 1), enc(s)) for s in upper])
+    plus_sum = across(added(back_plus, grads[3]), [(dec(s - 1), s) for s in upper])
     summed = ring_total(summed, shard_index)
     returned = (
         own_sum.astype(jnp.float32) + minus_sum.astype(jnp.float32) + plus_sum.astype(jnp.float32)
@@ -246,7 +244,7 @@
 
 def solution(mesh):
     return jax.shard_map(
-        local,
+        local_body,
         mesh=mesh,
         in_specs=(P("phase", None, ("dp", "seq"), None), P(), P("dp", None, None)),
         out_specs=(P("phase", None, ("dp", "seq"), None), P("phase", None)),

time: 181 us -> 181 us (level)
  no operation moved by 1% of the time
where the time goes in v6:
time: 181 us; the launch traced here: 180 us
  starting transfers between devices  112 us (62%)
  waiting for transfers between devices  49.2 us (27%)
  other arithmetic  10.6 us (6%)
  local copies, waits for them, and re-layouts  7.71 us (4%)
    ppermute x5, starting transfers between devices, exchange_add(): lax.ppermute(value, axis, [(i, i ^ stride) for i in range(count)])  68.1 us
    ppermute x12, waiting for transfers between devices, across(): return lax.ppermute(value, ('phase', 'seq'), pairs)  32.7 us
    ppermute x12, starting transfers between devices, across(): return lax.ppermute(value, ('phase', 'seq'), pairs)  22.6 us
    ppermute x4, starting transfers between devices, ring_shift(): return lax.ppermute(value, 'seq', pairs)  20.9 us
    ppermute x5, waiting for transfers between devices, exchange_add(): lax.ppermute(value, axis, [(i, i ^ stride) for i in range(count)])  12.6 us
    another operation x9, local copies, waits for them, and re-layouts  7.62 us
    convert_element_type x3, other arithmetic, added(): return (a.astype(jnp.float32) + b.astype(jnp.float32)).astype(jnp.bfloat16)  6.52 us
    ppermute x4, waiting for transfers between devices, ring_shift(): return lax.ppermute(value, 'seq', pairs)  3.92 us
  transfers between devices with their start and end apart: 21, of which 10 were waited for; matrix products, arithmetic and copies ran while one was open for 4% of the time, Pallas kernels for 0%

profile of v6, /device:TPU:58, one launch (start us, length us, event | category | flops | bytes accessed | tf_op | source)
XLA Modules:
  0.0 180.0 jit_solution(4622358252121617963)
XLA Ops:
  0.6 1.5 collective-permute-start.3
  2.2 3.1 %collective-permute-start = (bf16[2,128,2048]{2,1,0:T(8,128)(2,1)}, bf16[2,128,2048]{2,1,0:T(8,128)(2,1)S(1)}, u32[]{:S(2)}, u32[]{:S(2)}) collective-permute-start(bf16[2,128,2048]{2,1,0:T(8,128)(2,1)} %bitcast.29), channel_id=1, source_target_pairs={{0,136},{8,144},{16,152},{24,160},{32,168},{40,176},{48,184},{56,1... | collective-permute-start | bytes 3145736 | tf_op jit(solution)/shard_map/ppermute | solution.py:185
  5.3 9.4 %collective-permute-done.3 = bf16[2,128,2048]{2,1,0:T(8,128)(2,1)S(1)} collective-permute-done((bf16[2,128,2048]{2,1,0:T(8,128)(2,1)}, bf16[2,128,2048]{2,1,0:T(8,128)(2,1)S(1)}, u32[]{:S(2)}, u32[]{:S(2)}) %collective-permute-start.3) | collective-permute-done | bytes 1048608 | tf_op jit(solution)/shard_map/ppermute | solution.py:185
  14.7 0.0 copy-start.3
  14.7 0.7 collective-permute-start.4
  15.4 6.2 %collective-permute-start.2 = (bf16[2,128,2048]{2,1,0:T(8,128)(2,1)}, bf16[2,128,2048]{2,1,0:T(8,128)(2,1)}, u32[]{:S(2)}, u32[]{:S(2)}) collective-permute-start(bf16[2,128,2048]{2,1,0:T(8,128)(2,1)} %bitcast.30), channel_id=1, source_target_pairs={{0,128},{8,136},{16,144},{24,152},{32,160},{40,168},{48,176},{56,1... | collective-permute-start | bytes 3145736 | tf_op jit(solution)/shard_map/ppermute | solution.py:185
  21.6 0.0 collective-permute-done
  21.6 1.6 collective-permute-start.1
  23.3 0.0 collective-permute-done.4
  23.3 1.7 collective-permute-start.5
  24.9 0.0 copy-done.3
  24.9 0.8 slice_bitcast_fusion.1
  25.7 0.2 reduce-window.8
  25.9 0.2 reduce-window_1_clone.1
  26.0 0.7 bitcast_subtract_fusion
  26.7 0.7 compare_convert_fusion.2
  27.4 0.1 compare_convert_fusion.1
  27.5 0.0 collective-permute-done.2
  27.5 0.0 collective-permute-done.1
  27.5 0.0 collective-permute-done.5
  27.5 6.9 %conditional.1 = (bf16[2,128,2048]{2,1,0:T(8,128)(2,1)S(1)}, bf16[2,128,2048]{2,1,0:T(8,128)(2,1)}, bf16[2,128,2048]{2,1,0:T(8,128)(2,1)}, bf16[2,128,2048]{2,1,...) conditional(s32[]{:T(128)} %convert_element_type.91, () %tuple.51, ...), branch_computations={%region_2.3_spmd, %region_3.6_spmd} | conditional | flops 3222798336 | bytes 32510076 | solution.py:215
  27.5 0.2 broadcast.51
  27.7 1.6 broadcast.51.clone
  29.3 1.6 broadcast.51.clone.1
  30.9 0.1 broadcast.49
  31.0 1.1 broadcast.49.clone
  32.1 1.2 broadcast.49.clone.1
  33.3 1.1 broadcast.49.clone.2
  34.4 1.6 collective-permute-start.11
  36.0 0.7 collective-permute-start.12
  36.7 65.3 %collective-permute-start.7 = (f32[2,32]{1,0:T(2,128)S(1)}, f32[2,32]{1,0:T(2,128)S(1)}, u32[]{:S(2)}, u32[]{:S(2)}) collective-permute-start(f32[2,32]{1,0:T(2,128)S(1)} %get-tuple-element.251), channel_id=1, source_target_pairs={{0,128},{128,0},{1,129},{129,1},{2,130},{130,2},{3,131},{131,3},{4... | collective-permute-start | bytes 776 | tf_op jit(solution)/shard_map/ppermute | solution.py:161
  102.1 0.8 collective-permute-done.7
  102.9 0.0 collective-permute-start.8
  102.9 3.6 %collective-permute-done.8 = f32[2,32]{1,0:T(2,128)S(1)} collective-permute-done((f32[2,32]{1,0:T(2,128)S(1)}, f32[2,32]{1,0:T(2,128)S(1)}, u32[]{:S(2)}, u32[]{:S(2)}) %collective-permute-start.8) | collective-permute-done | bytes 288 | tf_op jit(solution)/shard_map/ppermute | solution.py:161
  106.5 0.5 collective-permute-start.9
  107.0 3.0 %collective-permute-done.9 = f32[2,32]{1,0:T(2,128)S(1)} collective-permute-done((f32[2,32]{1,0:T(2,128)S(1)}, f32[2,32]{1,0:T(2,128)S(1)}, u32[]{:S(2)}, u32[]{:S(2)}) %collective-permute-start.9) | collective-permute-done | bytes 288 | tf_op jit(solution)/shard_map/ppermute | solution.py:161
  110.1 2.1 %collective-permute-start.10 = (f32[2,32]{1,0:T(2,128)S(1)}, f32[2,32]{1,0:T(2,128)S(1)}, u32[]{:S(2)}, u32[]{:S(2)}) collective-permute-start(f32[2,32]{1,0:T(2,128)S(1)} %add.109), channel_id=1, source_target_pairs={{0,4},{1,5},{2,6},{3,7},{4,0},{5,1},{6,2},{7,3},{8,12},{9,13},{10,... | collective-permute-start | bytes 776 | tf_op jit(solution)/shard_map/ppermute | solution.py:161
  112.2 3.0 %collective-permute-done.10 = f32[2,32]{1,0:T(2,128)S(1)} collective-permute-done((f32[2,32]{1,0:T(2,128)S(1)}, f32[2,32]{1,0:T(2,128)S(1)}, u32[]{:S(2)}, u32[]{:S(2)}) %collective-permute-start.10) | collective-permute-done | bytes 288 | tf_op jit(solution)/shard_map/ppermute | solution.py:161
  115.1 0.0 collective-permute-done.11
  115.1 0.0 collective-permute-done.12
  115.1 2.9 %add_convert_fusion.2 = bf16[2,128,2048]{2,1,0:T(8,128)(2,1)} fusion(f32[2,128,2048]{2,1,0:T(8,128)} %get-tuple-element.258, bf16[2,128,2048]{2,1,0:T(8,128)(2,1)S(1)} %collective-permute-done.12), kind=kLoop, calls=%fused_computation.7 | loop fusion | flops 1572864 | bytes 4194304 | tf_op jit(solution)/shard_map/convert_element_type | solution.py:220
  118.0 1.6 collective-permute-start.15
  119.6 1.3 collective-permute-start.6
  120.9 0.1 collective-permute-start.14
  121.0 1.5 add_convert_fusion.3
  122.5 1.3 collective-permute-start.13
  123.8 2.3 %collective-permute-done.14 = f32[2,32]{1,0:T(2,128)S(1)} collective-permute-done((f32[2,32]{1,0:T(2,128)S(1)}, f32[2,32]{1,0:T(2,128)S(1)}, u32[]{:S(2)}, u32[]{:S(2)}) %collective-permute-start.14) | collective-permute-done | bytes 288 | tf_op jit(solution)/shard_map/ppermute | solution.py:161
  126.1 0.0 collective-permute-done.15
  126.1 5.9 %collective-permute-start.17 = (f32[1,2,32]{2,1,0:T(2,128)S(1)}, f32[1,2,32]{2,1,0:T(2,128)S(1)}, u32[]{:S(2)}, u32[]{:S(2)}) collective-permute-start(f32[1,2,32]{2,1,0:T(2,128)S(1)} %bitcast.23), channel_id=1, source_target_pairs={{0,56},{8,0},{16,8},{24,16},{32,24},{40,32},{48,40},{56,48},{64,12... | collective-permute-start | bytes 776 | tf_op jit(solution)/shard_map/ppermute | solution.py:142
  132.0 1.3 collective-permute-done.17
  133.3 6.1 %collective-permute-start.18 = (f32[2,2,32]{2,1,0:T(2,128)S(1)}, f32[2,2,32]{2,1,0:T(2,128)S(1)}, u32[]{:S(2)}, u32[]{:S(2)}) collective-permute-start(f32[2,2,32]{2,1,0:T(2,128)S(1)} %pad_maximum_fusion.3), channel_id=1, source_target_pairs={{0,48},{8,56},{16,0},{24,8},{32,16},{40,24},{48,32},{56,40},{64,11... | collective-permute-start | bytes 1544 | tf_op jit(solution)/shard_map/ppermute | solution.py:142
  139.4 1.3 collective-permute-done.18
  140.7 4.4 %collective-permute-start.19 = (f32[4,2,32]{2,1,0:T(2,128)S(1)}, f32[4,2,32]{2,1,0:T(2,128)S(1)}, u32[]{:S(2)}, u32[]{:S(2)}) collective-permute-start(f32[4,2,32]{2,1,0:T(2,128)S(1)} %pad_maximum_fusion.2), channel_id=1, source_target_pairs={{0,48},{8,56},{16,0},{24,8},{32,16},{40,24},{48,32},{56,40},{64,11... | collective-permute-start | bytes 3080 | tf_op jit(solution)/shard_map/ppermute | solution.py:142
  145.2 1.3 collective-permute-done.19
  146.5 4.5 %collective-permute-start.20 = (f32[6,2,32]{2,1,0:T(2,128)S(1)}, f32[6,2,32]{2,1,0:T(2,128)S(1)}, u32[]{:S(2)}, u32[]{:S(2)}) collective-permute-start(f32[6,2,32]{2,1,0:T(2,128)S(1)} %pad_maximum_fusion.1), channel_id=1, source_target_pairs={{0,48},{8,56},{16,0},{24,8},{32,16},{40,24},{48,32},{56,40},{64,11... | collective-permute-start | bytes 4616 | tf_op jit(solution)/shard_map/ppermute | solution.py:142
  151.0 2.1 %add_convert_fusion.1 = bf16[2,128,2048]{2,1,0:T(8,128)(2,1)S(1)} fusion(f32[2,128,2048]{2,1,0:T(8,128)} %get-tuple-element.260, bf16[2,128,2048]{2,1,0:T(8,128)(2,1)} %collective-permute-done.15), kind=kLoop, calls=%fused_computation.6 | loop fusion | flops 1572864 | bytes 4194304 | tf_op jit(solution)/shard_map/convert_element_type | solution.py:220
  153.1 1.3 collective-permute-start.16
  154.4 0.0 collective-permute-done.20
  154.5 0.0 copy-done.2
  154.5 0.5 fusion.10
  155.1 0.0 collective-permute-done.6
  155.1 0.0 collective-permute-done.13
  155.1 23.2 %collective-permute-done.16 = bf16[2,128,2048]{2,1,0:T(8,128)(2,1)S(1)} collective-permute-done((bf16[2,128,2048]{2,1,0:T(8,128)(2,1)S(1)}, bf16[2,128,2048]{2,1,0:T(8,128)(2,1)S(1)}, u32[]{:S(2)}, u32[]{:S(2)}) %collective-permute-start.16) | collective-permute-done | bytes 1048608 | tf_op jit(solution)/shard_map/ppermute | solution.py:185
  178.3 1.7 fusion.1
  (22 shorter events, 0.1 us)
Async XLA Ops:
  0.6 14.1 %collective-permute-start.3 = (bf16[2,128,2048]{2,1,0:T(8,128)(2,1)}, bf16[2,128,2048]{2,1,0:T(8,128)(2,1)S(1)}, u32[]{:S(2)}, u32[]{:S(2)}) collective-permute-start(bf16[2,128,2048]{2,1,0:T(8,128)(2,1)} %bitcast.28), channel_id=1, source_target_pairs={{8,128},{16,136},{24,144},{32,152},{40,160},{48,168},{56,176},{64,... | collective-permute-start | bytes 3145736 | tf_op jit(solution)/shard_map/ppermute | solution.py:185
  2.2 19.5 %collective-permute-start = (bf16[2,128,2048]{2,1,0:T(8,128)(2,1)}, bf16[2,128,2048]{2,1,0:T(8,128)(2,1)S(1)}, u32[]{:S(2)}, u32[]{:S(2)}) collective-permute-start(bf16[2,128,2048]{2,1,0:T(8,128)(2,1)} %bitcast.29), channel_id=1, source_target_pairs={{0,136},{8,144},{16,152},{24,160},{32,168},{40,176},{48,184},{56,1... | collective-permute-start | bytes 3145736 | tf_op jit(solution)/shard_map/ppermute | solution.py:185
  14.7 10.2 %copy-start.3 = (bf16[2,128,2048]{2,1,0:T(8,128)(2,1)}, bf16[2,128,2048]{2,1,0:T(8,128)(2,1)S(1)}, u32[]{:S(2)}) copy-start(bf16[2,128,2048]{2,1,0:T(8,128)(2,1)S(1)} %collective-permute-done.3) | copy-start | bytes 3145732
  14.7 8.6 %collective-permute-start.4 = (bf16[2,128,2048]{2,1,0:T(8,128)(2,1)S(1)}, bf16[2,128,2048]{2,1,0:T(8,128)(2,1)S(1)}, u32[]{:S(2)}, u32[]{:S(2)}) collective-permute-start(bf16[2,128,2048]{2,1,0:T(8,128)(2,1)S(1)} %collective-permute-done.3), channel_id=1, source_target_pairs={{136,128},{144,136},{152,144},{160,152},{168,160},{176,168},{184,1... | collective-permute-start | bytes 3145736 | tf_op jit(solution)/shard_map/ppermute | solution.py:185
  15.4 12.1 %collective-permute-start.2 = (bf16[2,128,2048]{2,1,0:T(8,128)(2,1)}, bf16[2,128,2048]{2,1,0:T(8,128)(2,1)}, u32[]{:S(2)}, u32[]{:S(2)}) collective-permute-start(bf16[2,128,2048]{2,1,0:T(8,128)(2,1)} %bitcast.30), channel_id=1, source_target_pairs={{0,128},{8,136},{16,144},{24,152},{32,160},{40,168},{48,176},{56,1... | collective-permute-start | bytes 3145736 | tf_op jit(solution)/shard_map/ppermute | solution.py:185
  21.6 5.9 %collective-permute-start.1 = (bf16[2,128,2048]{2,1,0:T(8,128)(2,1)S(1)}, bf16[2,128,2048]{2,1,0:T(8,128)(2,1)}, u32[]{:S(2)}, u32[]{:S(2)}) collective-permute-start(bf16[2,128,2048]{2,1,0:T(8,128)(2,1)S(1)} %collective-permute-done), channel_id=1, source_target_pairs={{128,136},{136,144},{144,152},{152,160},{160,168},{168,176},{176,1... | collective-permute-start | bytes 3145736 | tf_op jit(solution)/shard_map/ppermute | solution.py:185
  23.3 4.2 %collective-permute-start.5 = (bf16[2,128,2048]{2,1,0:T(8,128)(2,1)S(1)}, bf16[2,128,2048]{2,1,0:T(8,128)(2,1)}, u32[]{:S(2)}, u32[]{:S(2)}) collective-permute-start(bf16[2,128,2048]{2,1,0:T(8,128)(2,1)S(1)} %collective-permute-done.4), channel_id=1, source_target_pairs={{136,128},{144,136},{152,144},{160,152},{168,160},{176,168},{184,1... | collective-permute-start | bytes 3145736 | tf_op jit(solution)/shard_map/ppermute | solution.py:185
  34.4 80.7 %collective-permute-start.11 = (bf16[2,128,2048]{2,1,0:T(8,128)(2,1)}, bf16[2,128,2048]{2,1,0:T(8,128)(2,1)}, u32[]{:S(2)}, u32[]{:S(2)}) collective-permute-start(bf16[2,128,2048]{2,1,0:T(8,128)(2,1)} %get-tuple-element.252), channel_id=1, source_target_pairs={{136,128},{144,136},{152,144},{160,152},{168,160},{176,168},{184,1... | collective-permute-start | bytes 3145736 | tf_op jit(solution)/shard_map/ppermute | solution.py:185
  36.0 79.1 %collective-permute-start.12 = (bf16[2,128,2048]{2,1,0:T(8,128)(2,1)}, bf16[2,128,2048]{2,1,0:T(8,128)(2,1)S(1)}, u32[]{:S(2)}, u32[]{:S(2)}) collective-permute-start(bf16[2,128,2048]{2,1,0:T(8,128)(2,1)} %get-tuple-element.253), channel_id=1, source_target_pairs={{128,136},{136,144},{144,152},{152,160},{160,168},{168,176},{176,1... | collective-permute-start | bytes 3145736 | tf_op jit(solution)/shard_map/ppermute | solution.py:185
  36.7 66.2 %collective-permute-start.7 = (f32[2,32]{1,0:T(2,128)S(1)}, f32[2,32]{1,0:T(2,128)S(1)}, u32[]{:S(2)}, u32[]{:S(2)}) collective-permute-start(f32[2,32]{1,0:T(2,128)S(1)} %get-tuple-element.251), channel_id=1, source_target_pairs={{0,128},{128,0},{1,129},{129,1},{2,130},{130,2},{3,131},{131,3},{4... | collective-permute-start | bytes 776 | tf_op jit(solution)/shard_map/ppermute | solution.py:161
  102.9 3.6 %collective-permute-start.8 = (f32[2,32]{1,0:T(2,128)S(1)}, f32[2,32]{1,0:T(2,128)S(1)}, u32[]{:S(2)}, u32[]{:S(2)}) collective-permute-start(f32[2,32]{1,0:T(2,128)S(1)} %add.107), channel_id=1, source_target_pairs={{0,1},{1,0},{2,3},{3,2},{4,5},{5,4},{6,7},{7,6},{8,9},{9,8},{10,11... | collective-permute-start | bytes 776 | tf_op jit(solution)/shard_map/ppermute | solution.py:161
  106.5 3.6 %collective-permute-start.9 = (f32[2,32]{1,0:T(2,128)S(1)}, f32[2,32]{1,0:T(2,128)S(1)}, u32[]{:S(2)}, u32[]{:S(2)}) collective-permute-start(f32[2,32]{1,0:T(2,128)S(1)} %add.108), channel_id=1, source_target_pairs={{0,2},{1,3},{2,0},{3,1},{4,6},{5,7},{6,4},{7,5},{8,10},{9,11},{10,... | collective-permute-start | bytes 776 | tf_op jit(solution)/shard_map/ppermute | solution.py:161
  110.1 5.1 %collective-permute-start.10 = (f32[2,32]{1,0:T(2,128)S(1)}, f32[2,32]{1,0:T(2,128)S(1)}, u32[]{:S(2)}, u32[]{:S(2)}) collective-permute-start(f32[2,32]{1,0:T(2,128)S(1)} %add.109), channel_id=1, source_target_pairs={{0,4},{1,5},{2,6},{3,7},{4,0},{5,1},{6,2},{7,3},{8,12},{9,13},{10,... | collective-permute-start | bytes 776 | tf_op jit(solution)/shard_map/ppermute | solution.py:161
  118.0 8.1 %collective-permute-start.15 = (bf16[2,128,2048]{2,1,0:T(8,128)(2,1)}, bf16[2,128,2048]{2,1,0:T(8,128)(2,1)}, u32[]{:S(2)}, u32[]{:S(2)}) collective-permute-start(bf16[2,128,2048]{2,1,0:T(8,128)(2,1)} %add_convert_fusion.2), channel_id=1, source_target_pairs={{128,136},{136,144},{144,152},{152,160},{160,168},{168,176},{176,1... | collective-permute-start | bytes 3145736 | tf_op jit(solution)/shard_map/ppermute | solution.py:185
  119.6 35.4 %collective-permute-start.6 = (bf16[2,128,2048]{2,1,0:T(8,128)(2,1)}, bf16[2,128,2048]{2,1,0:T(8,128)(2,1)S(1)}, u32[]{:S(2)}, u32[]{:S(2)}) collective-permute-start(bf16[2,128,2048]{2,1,0:T(8,128)(2,1)} %get-tuple-element.250), channel_id=1, source_target_pairs={{128,0},{136,8},{144,16},{152,24},{160,32},{168,40},{176,48},{184,... | collective-permute-start | bytes 3145736 | tf_op jit(solution)/shard_map/ppermute | solution.py:185
  120.9 5.2 %collective-permute-start.14 = (f32[2,32]{1,0:T(2,128)S(1)}, f32[2,32]{1,0:T(2,128)S(1)}, u32[]{:S(2)}, u32[]{:S(2)}) collective-permute-start(f32[2,32]{1,0:T(2,128)S(1)} %add.110), channel_id=1, source_target_pairs={{0,64},{8,72},{16,80},{24,88},{32,96},{40,104},{48,112},{56,120},{... | collective-permute-start | bytes 776 | tf_op jit(solution)/shard_map/ppermute | solution.py:161
  122.5 32.5 %collective-permute-start.13 = (bf16[2,128,2048]{2,1,0:T(8,128)(2,1)S(1)}, bf16[2,128,2048]{2,1,0:T(8,128)(2,1)S(1)}, u32[]{:S(2)}, u32[]{:S(2)}) collective-permute-start(bf16[2,128,2048]{2,1,0:T(8,128)(2,1)S(1)} %add_convert_fusion.3), channel_id=1, source_target_pairs={{136,0},{144,8},{152,16},{160,24},{168,32},{176,40},{184,48},{192,... | collective-permute-start | bytes 3145736 | tf_op jit(solution)/shard_map/ppermute | solution.py:185
  126.1 7.2 %collective-permute-start.17 = (f32[1,2,32]{2,1,0:T(2,128)S(1)}, f32[1,2,32]{2,1,0:T(2,128)S(1)}, u32[]{:S(2)}, u32[]{:S(2)}) collective-permute-start(f32[1,2,32]{2,1,0:T(2,128)S(1)} %bitcast.23), channel_id=1, source_target_pairs={{0,56},{8,0},{16,8},{24,16},{32,24},{40,32},{48,40},{56,48},{64,12... | collective-permute-start | bytes 776 | tf_op jit(solution)/shard_map/ppermute | solution.py:142
  133.3 7.4 %collective-permute-start.18 = (f32[2,2,32]{2,1,0:T(2,128)S(1)}, f32[2,2,32]{2,1,0:T(2,128)S(1)}, u32[]{:S(2)}, u32[]{:S(2)}) collective-permute-start(f32[2,2,32]{2,1,0:T(2,128)S(1)} %pad_maximum_fusion.3), channel_id=1, source_target_pairs={{0,48},{8,56},{16,0},{24,8},{32,16},{40,24},{48,32},{56,40},{64,11... | collective-permute-start | bytes 1544 | tf_op jit(solution)/shard_map/ppermute | solution.py:142
  140.7 5.7 %collective-permute-start.19 = (f32[4,2,32]{2,1,0:T(2,128)S(1)}, f32[4,2,32]{2,1,0:T(2,128)S(1)}, u32[]{:S(2)}, u32[]{:S(2)}) collective-permute-start(f32[4,2,32]{2,1,0:T(2,128)S(1)} %pad_maximum_fusion.2), channel_id=1, source_target_pairs={{0,48},{8,56},{16,0},{24,8},{32,16},{40,24},{48,32},{56,40},{64,11... | collective-permute-start | bytes 3080 | tf_op jit(solution)/shard_map/ppermute | solution.py:142
  146.5 7.9 %collective-permute-start.20 = (f32[6,2,32]{2,1,0:T(2,128)S(1)}, f32[6,2,32]{2,1,0:T(2,128)S(1)}, u32[]{:S(2)}, u32[]{:S(2)}) collective-permute-start(f32[6,2,32]{2,1,0:T(2,128)S(1)} %pad_maximum_fusion.1), channel_id=1, source_target_pairs={{0,48},{8,56},{16,0},{24,8},{32,16},{40,24},{48,32},{56,40},{64,11... | collective-permute-start | bytes 4616 | tf_op jit(solution)/shard_map/ppermute | solution.py:142
  151.0 3.6 %copy-start.2 = (f32[2,32]{1,0:T(2,128)S(1)}, f32[2,32]{1,0:T(2,128)}, u32[]{:S(2)}) copy-start(f32[2,32]{1,0:T(2,128)} %param.6) | copy-start | bytes 772
  153.1 25.2 %collective-permute-start.16 = (bf16[2,128,2048]{2,1,0:T(8,128)(2,1)S(1)}, bf16[2,128,2048]{2,1,0:T(8,128)(2,1)S(1)}, u32[]{:S(2)}, u32[]{:S(2)}) collective-permute-start(bf16[2,128,2048]{2,1,0:T(8,128)(2,1)S(1)} %add_convert_fusion.1), channel_id=1, source_target_pairs={{128,8},{136,16},{144,24},{152,32},{160,40},{168,48},{176,56},{184... | collective-permute-start | bytes 3145736 | tf_op jit(solution)/shard_map/ppermute | solution.py:185

commit v7 on v6

--- a/solution.py
+++ b/solution.py
@@ -53,11 +53,11 @@
         g_value = gains_ref[1, head]
         mine = first if j == 0 else jnp.logical_not(first)
         q_h = jnp.where(mine, q, jnp.zeros_like(q))
-        raw = lax.dot_general(q_h, k, (((1,), (1,)), ((), ())), preferred_element_type=jnp.float32) * inv_root
-        logits = jnp.where(allowed, g_logit * raw, masked_score)
+        raw = lax.dot_general(q_h, k, (((1,), (1,)), ((), ())), preferred_element_type=jnp.float32)
+        logits = jnp.where(allowed, (g_logit * inv_root) * raw, masked_score)
         top = jnp.max(logits, axis=1, keepdims=True)
         lifted = jnp.exp(logits - top)
-        chances = lifted / jnp.sum(lifted, axis=1, keepdims=True)
+        chances = lifted * (1.0 / jnp.sum(lifted, axis=1, keepdims=True))
         p_low = chances.astype(jnp.bfloat16)
         att_parts.append(jnp.dot(p_low, v, preferred_element_type=jnp.float32) * g_value)
         heads.append((g_logit, g_value, mine, raw, chances, p_low))
@@ -75,7 +75,7 @@
         dq_parts.append(jnp.dot(score_low, k, preferred_element_type=jnp.float32) * factor)
         dk_parts.append(lax.dot_general(score_low, q, (((0,), (0,)), ((), ())), preferred_element_type=jnp.float32) * factor)
         dv_parts.append(lax.dot_general(p_low, do, (((0,), (0,)), ((), ())), preferred_element_type=jnp.float32) * g_value)
-        logit_terms.append(jnp.sum(score_grad * raw))
+        logit_terms.append(jnp.sum(score_grad * raw) * inv_root)
     out_ref[1] = jnp.where(first, dq_parts[0], dq_parts[1]).astype(jnp.bfloat16)
     key_grad = jnp.where(first, dk_parts[0], dk_parts[1]).astype(jnp.bfloat16)
     value_grad = jnp.where(first, dv_parts[0], dv_parts[1]).astype(jnp.bfloat16)
@@ -217,7 +217,7 @@
     )
 
     def added(a, b):
-        return (a.astype(jnp.float32) + b.astype(jnp.float32)).astype(jnp.bfloat16)
+        return a + b
 
     token_total = tok_dev * count * lax.axis_size("dp")
     summed = exchange_add(terms, "phase", 1)

time: 181 us -> 175 us (0.967)
  the two profiles are of different devices: /device:TPU:58 before, /device:TPU:8 now
where the time goes in v7:
time: 175 us; the launch traced here: 172 us
  starting transfers between devices  121 us (69%)
  waiting for transfers between devices  37.7 us (22%)
  other arithmetic  7.43 us (4%)
  local copies, waits for them, and re-layouts  5.75 us (3%)
    ppermute x5, starting transfers between devices, exchange_add(): lax.ppermute(value, axis, [(i, i ^ stride) for i in range(count)])  75.9 us
    ppermute x12, starting transfers between devices, across(): return lax.ppermute(value, ('phase', 'seq'), pairs)  29.9 us
    ppermute x12, waiting for transfers between devices, across(): return lax.ppermute(value, ('phase', 'seq'), pairs)  22.5 us
    ppermute x4, starting transfers between devices, ring_shift(): return lax.ppermute(value, 'seq', pairs)  14.8 us
    ppermute x5, waiting for transfers between devices, exchange_add(): lax.ppermute(value, axis, [(i, i ^ stride) for i in range(count)])  9.62 us
    another operation x9, local copies, waits for them, and re-layouts  5.66 us
    ppermute x4, waiting for transfers between devices, ring_shift(): return lax.ppermute(value, 'seq', pairs)  5.63 us
  transfers between devices with their start and end apart: 21, of which 10 were waited for; matrix products, arithmetic and copies ran while one was open for 3% of the time, Pallas kernels for 0%

profile of v7, /device:TPU:8, one launch (start us, length us, event | category | flops | bytes accessed | tf_op | source)
XLA Modules:
  0.0 172.4 jit_solution(10292241894185870654)
XLA Ops:
  0.6 0.7 collective-permute-start.3
  1.4 3.9 %collective-permute-start = (bf16[2,128,2048]{2,1,0:T(8,128)(2,1)}, bf16[2,128,2048]{2,1,0:T(8,128)(2,1)S(1)}, u32[]{:S(2)}, u32[]{:S(2)}) collective-permute-start(bf16[2,128,2048]{2,1,0:T(8,128)(2,1)} %bitcast.29), channel_id=1, source_target_pairs={{0,136},{8,144},{16,152},{24,160},{32,168},{40,176},{48,184},{56,1... | collective-permute-start | bytes 3145736 | tf_op jit(solution)/shard_map/ppermute | solution.py:185
  5.3 0.0 collective-permute-done.3
  5.3 0.0 copy-start.1
  5.3 0.7 collective-permute-start.4
  6.0 15.0 %collective-permute-start.2 = (bf16[2,128,2048]{2,1,0:T(8,128)(2,1)}, bf16[2,128,2048]{2,1,0:T(8,128)(2,1)}, u32[]{:S(2)}, u32[]{:S(2)}) collective-permute-start(bf16[2,128,2048]{2,1,0:T(8,128)(2,1)} %bitcast.30), channel_id=1, source_target_pairs={{0,128},{8,136},{16,144},{24,152},{32,160},{40,168},{48,176},{56,1... | collective-permute-start | bytes 3145736 | tf_op jit(solution)/shard_map/ppermute | solution.py:185
  21.0 0.0 collective-permute-done
  21.0 1.6 collective-permute-start.1
  22.6 0.0 collective-permute-done.4
  22.6 1.6 collective-permute-start.5
  24.3 0.0 copy-done.1
  24.3 0.8 slice_bitcast_fusion.1
  25.0 0.2 reduce-window.8
  25.2 0.2 reduce-window_1_clone.1
  25.4 0.7 bitcast_subtract_fusion
  26.1 0.7 compare_convert_fusion.2
  26.8 0.1 compare_convert_fusion.1
  26.8 0.0 collective-permute-done.2
  26.8 0.0 collective-permute-done.1
  26.8 0.0 collective-permute-done.5
  26.8 4.9 %conditional.1 = (bf16[2,128,2048]{2,1,0:T(8,128)(2,1)}, bf16[2,128,2048]{2,1,0:T(8,128)(2,1)}, bf16[2,128,2048]{2,1,0:T(8,128)(2,1)S(1)}, bf16[2,128,2048]{2,1,...) conditional(s32[]{:T(128)} %convert_element_type.45, () %tuple.45, ...), branch_computations={%region_2.3_spmd, %region_3.6_spmd} | conditional | flops 3221225472 | bytes 23072892 | solution.py:215
  26.9 1.1 broadcast.46
  28.0 1.1 broadcast.46.clone
  29.1 0.1 broadcast.46.clone.1
  29.2 1.1 broadcast.46.clone.2
  30.4 0.1 broadcast.46.clone.3
  30.5 0.1 broadcast.46.clone.4
  30.6 1.2 broadcast.46.clone.5
  31.8 1.6 collective-permute-start.11
  33.4 0.7 collective-permute-start.12
  34.1 54.7 %collective-permute-start.7 = (f32[2,32]{1,0:T(2,128)S(1)}, f32[2,32]{1,0:T(2,128)S(1)}, u32[]{:S(2)}, u32[]{:S(2)}) collective-permute-start(f32[2,32]{1,0:T(2,128)S(1)} %get-tuple-element.248), channel_id=1, source_target_pairs={{0,128},{128,0},{1,129},{129,1},{2,130},{130,2},{3,131},{131,3},{4... | collective-permute-start | bytes 776 | tf_op jit(solution)/shard_map/ppermute | solution.py:161
  88.9 0.8 collective-permute-done.7
  89.7 0.5 collective-permute-start.8
  90.1 3.1 %collective-permute-done.8 = f32[2,32]{1,0:T(2,128)S(1)} collective-permute-done((f32[2,32]{1,0:T(2,128)S(1)}, f32[2,32]{1,0:T(2,128)S(1)}, u32[]{:S(2)}, u32[]{:S(2)}) %collective-permute-start.8) | collective-permute-done | bytes 288 | tf_op jit(solution)/shard_map/ppermute | solution.py:161
  93.3 1.5 collective-permute-start.9
  94.8 2.1 %collective-permute-done.9 = f32[2,32]{1,0:T(2,128)S(1)} collective-permute-done((f32[2,32]{1,0:T(2,128)S(1)}, f32[2,32]{1,0:T(2,128)S(1)}, u32[]{:S(2)}, u32[]{:S(2)}) %collective-permute-start.9) | collective-permute-done | bytes 288 | tf_op jit(solution)/shard_map/ppermute | solution.py:161
  96.8 3.0 %collective-permute-start.10 = (f32[2,32]{1,0:T(2,128)S(1)}, f32[2,32]{1,0:T(2,128)S(1)}, u32[]{:S(2)}, u32[]{:S(2)}) collective-permute-start(f32[2,32]{1,0:T(2,128)S(1)} %add.109), channel_id=1, source_target_pairs={{0,4},{1,5},{2,6},{3,7},{4,0},{5,1},{6,2},{7,3},{8,12},{9,13},{10,... | collective-permute-start | bytes 776 | tf_op jit(solution)/shard_map/ppermute | solution.py:161
  99.9 2.0 %collective-permute-done.10 = f32[2,32]{1,0:T(2,128)S(1)} collective-permute-done((f32[2,32]{1,0:T(2,128)S(1)}, f32[2,32]{1,0:T(2,128)S(1)}, u32[]{:S(2)}, u32[]{:S(2)}) %collective-permute-start.10) | collective-permute-done | bytes 288 | tf_op jit(solution)/shard_map/ppermute | solution.py:161
  101.9 0.0 collective-permute-done.11
  101.9 0.0 collective-permute-done.12
  101.9 1.4 add.114
  103.3 0.7 collective-permute-start.15
  104.0 16.2 %collective-permute-start.14 = (f32[2,32]{1,0:T(2,128)S(1)}, f32[2,32]{1,0:T(2,128)S(1)}, u32[]{:S(2)}, u32[]{:S(2)}) collective-permute-start(f32[2,32]{1,0:T(2,128)S(1)} %add.110), channel_id=1, source_target_pairs={{0,64},{8,72},{16,80},{24,88},{32,96},{40,104},{48,112},{56,120},{... | collective-permute-start | bytes 776 | tf_op jit(solution)/shard_map/ppermute | solution.py:161
  120.2 1.6 collective-permute-done.14
  121.8 0.0 collective-permute-done.15
  121.8 5.9 %collective-permute-start.17 = (f32[1,2,32]{2,1,0:T(2,128)S(1)}, f32[1,2,32]{2,1,0:T(2,128)S(1)}, u32[]{:S(2)}, u32[]{:S(2)}) collective-permute-start(f32[1,2,32]{2,1,0:T(2,128)S(1)} %bitcast.23), channel_id=1, source_target_pairs={{0,56},{8,0},{16,8},{24,16},{32,24},{40,32},{48,40},{56,48},{64,12... | collective-permute-start | bytes 776 | tf_op jit(solution)/shard_map/ppermute | solution.py:142
  127.7 1.3 collective-permute-done.17
  129.0 1.7 collective-permute-start.18
  130.7 2.8 %collective-permute-done.18 = f32[2,2,32]{2,1,0:T(2,128)S(1)} collective-permute-done((f32[2,2,32]{2,1,0:T(2,128)S(1)}, f32[2,2,32]{2,1,0:T(2,128)S(1)}, u32[]{:S(2)}, u32[]{:S(2)}) %collective-permute-start.18) | collective-permute-done | bytes 544 | tf_op jit(solution)/shard_map/ppermute | solution.py:142
  133.5 2.9 %collective-permute-start.19 = (f32[4,2,32]{2,1,0:T(2,128)S(1)}, f32[4,2,32]{2,1,0:T(2,128)S(1)}, u32[]{:S(2)}, u32[]{:S(2)}) collective-permute-start(f32[4,2,32]{2,1,0:T(2,128)S(1)} %pad_maximum_fusion.2), channel_id=1, source_target_pairs={{0,48},{8,56},{16,0},{24,8},{32,16},{40,24},{48,32},{56,40},{64,11... | collective-permute-start | bytes 3080 | tf_op jit(solution)/shard_map/ppermute | solution.py:142
  136.4 1.6 collective-permute-done.19
  138.0 4.2 %collective-permute-start.20 = (f32[6,2,32]{2,1,0:T(2,128)S(1)}, f32[6,2,32]{2,1,0:T(2,128)S(1)}, u32[]{:S(2)}, u32[]{:S(2)}) collective-permute-start(f32[6,2,32]{2,1,0:T(2,128)S(1)} %pad_maximum_fusion.1), channel_id=1, source_target_pairs={{0,48},{8,56},{16,0},{24,8},{32,16},{40,24},{48,32},{56,40},{64,11... | collective-permute-start | bytes 4616 | tf_op jit(solution)/shard_map/ppermute | solution.py:142
  142.2 1.3 collective-permute-start.6
  143.5 1.6 add.111
  145.1 1.3 collective-permute-start.13
  146.4 0.0 copy-start
  146.5 0.4 add.115
  146.8 0.7 collective-permute-start.16
  147.6 0.0 collective-permute-done.20
  147.7 0.5 fusion.10
  148.2 6.6 %collective-permute-done.6 = bf16[2,128,2048]{2,1,0:T(8,128)(2,1)S(1)} collective-permute-done((bf16[2,128,2048]{2,1,0:T(8,128)(2,1)}, bf16[2,128,2048]{2,1,0:T(8,128)(2,1)S(1)}, u32[]{:S(2)}, u32[]{:S(2)}) %collective-permute-start.6) | collective-permute-done | bytes 1048608 | tf_op jit(solution)/shard_map/ppermute | solution.py:185
  154.8 15.9 %collective-permute-done.13 = bf16[2,128,2048]{2,1,0:T(8,128)(2,1)S(1)} collective-permute-done((bf16[2,128,2048]{2,1,0:T(8,128)(2,1)S(1)}, bf16[2,128,2048]{2,1,0:T(8,128)(2,1)S(1)}, u32[]{:S(2)}, u32[]{:S(2)}) %collective-permute-start.13) | collective-permute-done | bytes 1048608 | tf_op jit(solution)/shard_map/ppermute | solution.py:185
  170.7 0.0 collective-permute-done.16
  170.7 1.7 fusion.1
  (22 shorter events, 0.1 us)
Async XLA Ops:
  0.6 4.6 %collective-permute-start.3 = (bf16[2,128,2048]{2,1,0:T(8,128)(2,1)}, bf16[2,128,2048]{2,1,0:T(8,128)(2,1)S(1)}, u32[]{:S(2)}, u32[]{:S(2)}) collective-permute-start(bf16[2,128,2048]{2,1,0:T(8,128)(2,1)} %bitcast.28), channel_id=1, source_target_pairs={{8,128},{16,136},{24,144},{32,152},{40,160},{48,168},{56,176},{64,... | collective-permute-start | bytes 3145736 | tf_op jit(solution)/shard_map/ppermute | solution.py:185
  1.4 19.6 %collective-permute-start = (bf16[2,128,2048]{2,1,0:T(8,128)(2,1)}, bf16[2,128,2048]{2,1,0:T(8,128)(2,1)S(1)}, u32[]{:S(2)}, u32[]{:S(2)}) collective-permute-start(bf16[2,128,2048]{2,1,0:T(8,128)(2,1)} %bitcast.29), channel_id=1, source_target_pairs={{0,136},{8,144},{16,152},{24,160},{32,168},{40,176},{48,184},{56,1... | collective-permute-start | bytes 3145736 | tf_op jit(solution)/shard_map/ppermute | solution.py:185
  5.3 19.0 %copy-start.1 = (bf16[2,128,2048]{2,1,0:T(8,128)(2,1)}, bf16[2,128,2048]{2,1,0:T(8,128)(2,1)S(1)}, u32[]{:S(2)}) copy-start(bf16[2,128,2048]{2,1,0:T(8,128)(2,1)S(1)} %collective-permute-done.3) | copy-start | bytes 3145732
  5.3 17.4 %collective-permute-start.4 = (bf16[2,128,2048]{2,1,0:T(8,128)(2,1)S(1)}, bf16[2,128,2048]{2,1,0:T(8,128)(2,1)S(1)}, u32[]{:S(2)}, u32[]{:S(2)}) collective-permute-start(bf16[2,128,2048]{2,1,0:T(8,128)(2,1)S(1)} %collective-permute-done.3), channel_id=1, source_target_pairs={{136,128},{144,136},{152,144},{160,152},{168,160},{176,168},{184,1... | collective-permute-start | bytes 3145736 | tf_op jit(solution)/shard_map/ppermute | solution.py:185
  6.0 20.8 %collective-permute-start.2 = (bf16[2,128,2048]{2,1,0:T(8,128)(2,1)}, bf16[2,128,2048]{2,1,0:T(8,128)(2,1)}, u32[]{:S(2)}, u32[]{:S(2)}) collective-permute-start(bf16[2,128,2048]{2,1,0:T(8,128)(2,1)} %bitcast.30), channel_id=1, source_target_pairs={{0,128},{8,136},{16,144},{24,152},{32,160},{40,168},{48,176},{56,1... | collective-permute-start | bytes 3145736 | tf_op jit(solution)/shard_map/ppermute | solution.py:185
  21.0 5.8 %collective-permute-start.1 = (bf16[2,128,2048]{2,1,0:T(8,128)(2,1)S(1)}, bf16[2,128,2048]{2,1,0:T(8,128)(2,1)}, u32[]{:S(2)}, u32[]{:S(2)}) collective-permute-start(bf16[2,128,2048]{2,1,0:T(8,128)(2,1)S(1)} %collective-permute-done), channel_id=1, source_target_pairs={{128,136},{136,144},{144,152},{152,160},{160,168},{168,176},{176,1... | collective-permute-start | bytes 3145736 | tf_op jit(solution)/shard_map/ppermute | solution.py:185
  22.6 4.2 %collective-permute-start.5 = (bf16[2,128,2048]{2,1,0:T(8,128)(2,1)S(1)}, bf16[2,128,2048]{2,1,0:T(8,128)(2,1)}, u32[]{:S(2)}, u32[]{:S(2)}) collective-permute-start(bf16[2,128,2048]{2,1,0:T(8,128)(2,1)S(1)} %collective-permute-done.4), channel_id=1, source_target_pairs={{136,128},{144,136},{152,144},{160,152},{168,160},{176,168},{184,1... | collective-permute-start | bytes 3145736 | tf_op jit(solution)/shard_map/ppermute | solution.py:185
  31.8 70.1 %collective-permute-start.11 = (bf16[2,128,2048]{2,1,0:T(8,128)(2,1)}, bf16[2,128,2048]{2,1,0:T(8,128)(2,1)}, u32[]{:S(2)}, u32[]{:S(2)}) collective-permute-start(bf16[2,128,2048]{2,1,0:T(8,128)(2,1)} %get-tuple-element.249), channel_id=1, source_target_pairs={{136,128},{144,136},{152,144},{160,152},{168,160},{176,168},{184,1... | collective-permute-start | bytes 3145736 | tf_op jit(solution)/shard_map/ppermute | solution.py:185
  33.4 68.5 %collective-permute-start.12 = (bf16[2,128,2048]{2,1,0:T(8,128)(2,1)}, bf16[2,128,2048]{2,1,0:T(8,128)(2,1)S(1)}, u32[]{:S(2)}, u32[]{:S(2)}) collective-permute-start(bf16[2,128,2048]{2,1,0:T(8,128)(2,1)} %get-tuple-element.250), channel_id=1, source_target_pairs={{128,136},{136,144},{144,152},{152,160},{160,168},{168,176},{176,1... | collective-permute-start | bytes 3145736 | tf_op jit(solution)/shard_map/ppermute | solution.py:185
  34.1 55.5 %collective-permute-start.7 = (f32[2,32]{1,0:T(2,128)S(1)}, f32[2,32]{1,0:T(2,128)S(1)}, u32[]{:S(2)}, u32[]{:S(2)}) collective-permute-start(f32[2,32]{1,0:T(2,128)S(1)} %get-tuple-element.248), channel_id=1, source_target_pairs={{0,128},{128,0},{1,129},{129,1},{2,130},{130,2},{3,131},{131,3},{4... | collective-permute-start | bytes 776 | tf_op jit(solution)/shard_map/ppermute | solution.py:161
  89.7 3.6 %collective-permute-start.8 = (f32[2,32]{1,0:T(2,128)S(1)}, f32[2,32]{1,0:T(2,128)S(1)}, u32[]{:S(2)}, u32[]{:S(2)}) collective-permute-start(f32[2,32]{1,0:T(2,128)S(1)} %add.107), channel_id=1, source_target_pairs={{0,1},{1,0},{2,3},{3,2},{4,5},{5,4},{6,7},{7,6},{8,9},{9,8},{10,11... | collective-permute-start | bytes 776 | tf_op jit(solution)/shard_map/ppermute | solution.py:161
  93.3 3.6 %collective-permute-start.9 = (f32[2,32]{1,0:T(2,128)S(1)}, f32[2,32]{1,0:T(2,128)S(1)}, u32[]{:S(2)}, u32[]{:S(2)}) collective-permute-start(f32[2,32]{1,0:T(2,128)S(1)} %add.108), channel_id=1, source_target_pairs={{0,2},{1,3},{2,0},{3,1},{4,6},{5,7},{6,4},{7,5},{8,10},{9,11},{10,... | collective-permute-start | bytes 776 | tf_op jit(solution)/shard_map/ppermute | solution.py:161
  96.8 5.1 %collective-permute-start.10 = (f32[2,32]{1,0:T(2,128)S(1)}, f32[2,32]{1,0:T(2,128)S(1)}, u32[]{:S(2)}, u32[]{:S(2)}) collective-permute-start(f32[2,32]{1,0:T(2,128)S(1)} %add.109), channel_id=1, source_target_pairs={{0,4},{1,5},{2,6},{3,7},{4,0},{5,1},{6,2},{7,3},{8,12},{9,13},{10,... | collective-permute-start | bytes 776 | tf_op jit(solution)/shard_map/ppermute | solution.py:161
  103.3 18.5 %collective-permute-start.15 = (bf16[2,128,2048]{2,1,0:T(8,128)(2,1)}, bf16[2,128,2048]{2,1,0:T(8,128)(2,1)S(1)}, u32[]{:S(2)}, u32[]{:S(2)}) collective-permute-start(bf16[2,128,2048]{2,1,0:T(8,128)(2,1)} %add.114), channel_id=1, source_target_pairs={{128,136},{136,144},{144,152},{152,160},{160,168},{168,176},{176,1... | collective-permute-start | bytes 3145736 | tf_op jit(solution)/shard_map/ppermute | solution.py:185
  104.0 17.7 %collective-permute-start.14 = (f32[2,32]{1,0:T(2,128)S(1)}, f32[2,32]{1,0:T(2,128)S(1)}, u32[]{:S(2)}, u32[]{:S(2)}) collective-permute-start(f32[2,32]{1,0:T(2,128)S(1)} %add.110), channel_id=1, source_target_pairs={{0,64},{8,72},{16,80},{24,88},{32,96},{40,104},{48,112},{56,120},{... | collective-permute-start | bytes 776 | tf_op jit(solution)/shard_map/ppermute | solution.py:161
  121.8 7.2 %collective-permute-start.17 = (f32[1,2,32]{2,1,0:T(2,128)S(1)}, f32[1,2,32]{2,1,0:T(2,128)S(1)}, u32[]{:S(2)}, u32[]{:S(2)}) collective-permute-start(f32[1,2,32]{2,1,0:T(2,128)S(1)} %bitcast.23), channel_id=1, source_target_pairs={{0,56},{8,0},{16,8},{24,16},{32,24},{40,32},{48,40},{56,48},{64,12... | collective-permute-start | bytes 776 | tf_op jit(solution)/shard_map/ppermute | solution.py:142
  129.0 4.5 %collective-permute-start.18 = (f32[2,2,32]{2,1,0:T(2,128)S(1)}, f32[2,2,32]{2,1,0:T(2,128)S(1)}, u32[]{:S(2)}, u32[]{:S(2)}) collective-permute-start(f32[2,2,32]{2,1,0:T(2,128)S(1)} %pad_maximum_fusion.3), channel_id=1, source_target_pairs={{0,48},{8,56},{16,0},{24,8},{32,16},{40,24},{48,32},{56,40},{64,11... | collective-permute-start | bytes 1544 | tf_op jit(solution)/shard_map/ppermute | solution.py:142
  133.5 4.5 %collective-permute-start.19 = (f32[4,2,32]{2,1,0:T(2,128)S(1)}, f32[4,2,32]{2,1,0:T(2,128)S(1)}, u32[]{:S(2)}, u32[]{:S(2)}) collective-permute-start(f32[4,2,32]{2,1,0:T(2,128)S(1)} %pad_maximum_fusion.2), channel_id=1, source_target_pairs={{0,48},{8,56},{16,0},{24,8},{32,16},{40,24},{48,32},{56,40},{64,11... | collective-permute-start | bytes 3080 | tf_op jit(solution)/shard_map/ppermute | solution.py:142
  138.0 9.6 %collective-permute-start.20 = (f32[6,2,32]{2,1,0:T(2,128)S(1)}, f32[6,2,32]{2,1,0:T(2,128)S(1)}, u32[]{:S(2)}, u32[]{:S(2)}) collective-permute-start(f32[6,2,32]{2,1,0:T(2,128)S(1)} %pad_maximum_fusion.1), channel_id=1, source_target_pairs={{0,48},{8,56},{16,0},{24,8},{32,16},{40,24},{48,32},{56,40},{64,11... | collective-permute-start | bytes 4616 | tf_op jit(solution)/shard_map/ppermute | solution.py:142
  142.2 12.6 %collective-permute-start.6 = (bf16[2,128,2048]{2,1,0:T(8,128)(2,1)}, bf16[2,128,2048]{2,1,0:T(8,128)(2,1)S(1)}, u32[]{:S(2)}, u32[]{:S(2)}) collective-permute-start(bf16[2,128,2048]{2,1,0:T(8,128)(2,1)} %get-tuple-element.247), channel_id=1, source_target_pairs={{128,0},{136,8},{144,16},{152,24},{160,32},{168,40},{176,48},{184,... | collective-permute-start | bytes 3145736 | tf_op jit(solution)/shard_map/ppermute | solution.py:185
  145.1 25.5 %collective-permute-start.13 = (bf16[2,128,2048]{2,1,0:T(8,128)(2,1)S(1)}, bf16[2,128,2048]{2,1,0:T(8,128)(2,1)S(1)}, u32[]{:S(2)}, u32[]{:S(2)}) collective-permute-start(bf16[2,128,2048]{2,1,0:T(8,128)(2,1)S(1)} %add.111), channel_id=1, source_target_pairs={{136,0},{144,8},{152,16},{160,24},{168,32},{176,40},{184,48},{192,... | collective-permute-start | bytes 3145736 | tf_op jit(solution)/shard_map/ppermute | solution.py:185
  146.4 1.3 copy-start
  146.8 23.8 %collective-permute-start.16 = (bf16[2,128,2048]{2,1,0:T(8,128)(2,1)S(1)}, bf16[2,128,2048]{2,1,0:T(8,128)(2,1)S(1)}, u32[]{:S(2)}, u32[]{:S(2)}) collective-permute-start(bf16[2,128,2048]{2,1,0:T(8,128)(2,1)S(1)} %add.115), channel_id=1, source_target_pairs={{128,8},{136,16},{144,24},{152,32},{160,40},{168,48},{176,56},{184... | collective-permute-start | bytes 3145736 | tf_op jit(solution)/shard_map/ppermute | solution.py:185

commit v8 on v7

--- a/solution.py
+++ b/solution.py
@@ -14,6 +14,7 @@
 REACH_HIGH = 3
 WINDOW = REACH_LOW + REACH_HIGH + 1
 RING = 8
+CHUNKS = 2
 
 masked_score = -1e30
 
@@ -174,6 +175,7 @@
     count = lax.axis_size("seq")
     local_pair = sections[0]
     tok_dev = local_pair.shape[1]
+    inner = local_pair.shape[2]
     head_count = head_gains.shape[1]
     enc_counts = block_counts[0, 0]
     dec_counts = block_counts[0, 1]
@@ -186,13 +188,15 @@
 
     lower = range(count - 1)
     upper = range(1, count)
-    at_home = across(local_pair, [(s, dec(s)) for s in range(count)])
-    minus_1 = across(local_pair, [(s + 1, dec(s)) for s in lower])
-    plus_1 = across(local_pair, [(s - 1, dec(s)) for s in upper])
-    minus_2 = across(minus_1, [(dec(s + 1), dec(s)) for s in lower])
-    plus_2 = across(plus_1, [(dec(s - 1), dec(s)) for s in upper])
-    minus_3 = across(minus_2, [(dec(s + 1), dec(s)) for s in lower])
-    window = [plus_2, plus_1, at_home, minus_1, minus_2, minus_3]
+
+    def forward(pair):
+        at_home = across(pair, [(s, dec(s)) for s in range(count)])
+        minus_1 = across(pair, [(s + 1, dec(s)) for s in lower])
+        plus_1 = across(pair, [(s - 1, dec(s)) for s in upper])
+        minus_2 = across(minus_1, [(dec(s + 1), dec(s)) for s in lower])
+        plus_2 = across(plus_1, [(dec(s - 1), dec(s)) for s in upper])
+        minus_3 = across(minus_2, [(dec(s + 1), dec(s)) for s in lower])
+        return [plus_2, plus_1, at_home, minus_1, minus_2, minus_3]
 
     first_block = shard_index - REACH_LOW
     window_blocks = first_block + jnp.arange(WINDOW, dtype=jnp.int32)
@@ -202,23 +206,35 @@
     start_block = jnp.clip(enc_starts[segment] - first_block, 0, WINDOW - ENC_MOST).astype(jnp.int32)
     slice_segs = lax.dynamic_slice_in_dim(enc_segs, start_block, ENC_MOST)
     allowed_keys = jnp.repeat(slice_segs == segment, BLOCK)
-
-    def decoder_work(operands):
-        own, pieces = operands
-        return attention_block(jnp.reshape(start_block, (1,)), head_gains, own, pieces, allowed_keys)
-
-    def encoder_rest(operands):
-        own, _ = operands
-        zeros = jnp.zeros_like(own)
-        return (zeros, (zeros,) * WINDOW, jnp.zeros((2, head_count), jnp.float32))
-
-    produced, grads, terms = lax.cond(
-        phase_index == 1, decoder_work, encoder_rest, (local_pair, window)
-    )
-
-    def added(a, b):
-        return a + b
-
+    start = jnp.reshape(start_block, (1,))
+
+    width = inner // CHUNKS
+    heads = head_count // CHUNKS
+    pairs = [local_pair[:, :, c * width : (c + 1) * width] for c in range(CHUNKS)]
+    gains = [head_gains[:, c * heads : (c + 1) * heads] for c in range(CHUNKS)]
+    windows = []
+    for c in range(CHUNKS):
+        windows.append(forward(pairs[c]))
+    outs = []
+    for c in range(CHUNKS):
+        outs.append(attention_block(start, gains[c], pairs[c], windows[c], allowed_keys))
+
+    def backward(grads):
+        back_minus = across(grads[0], [(dec(s + 1), dec(s)) for s in lower])
+        back_plus = across(grads[5], [(dec(s - 1), dec(s)) for s in upper])
+        own_sum = across(grads[2], [(dec(s), s) for s in range(count)])
+        minus_sum = across(back_minus + grads[1], [(dec(s + 1), s) for s in lower])
+        back_plus = across(back_plus + grads[4], [(dec(s - 1), dec(s)) for s in upper])
+        plus_sum = across(back_plus + grads[3], [(dec(s - 1), s) for s in upper])
+        return own_sum, minus_sum, plus_sum
+
+    terms = jnp.concatenate([out[2] for out in outs], axis=1)
+    terms = jnp.where(phase_index == 1, terms, 0.0)
+    returned_parts = []
+    for c in range(CHUNKS - 1):
+        returned_parts.append(backward(outs[c][1]))
+
+    grads = outs[CHUNKS - 1][1]
     token_total = tok_dev * count * lax.axis_size("dp")
     summed = exchange_add(terms, "phase", 1)
     back_minus = across(grads[0], [(dec(s + 1), dec(s)) for s in lower])
@@ -226,15 +242,22 @@
     own_sum = across(grads[2], [(dec(s), s) for s in range(count)])
     summed = exchange_add(exchange_add(exchange_add(summed, "dp", 1), "dp", 2), "dp", 4)
     summed, back_minus, back_plus = lax.optimization_barrier((summed, back_minus, back_plus))
-    minus_sum = across(added(back_minus, grads[1]), [(dec(s + 1), s) for s in lower])
-    back_plus = across(added(back_plus, grads[4]), [(dec(s - 1), dec(s)) for s in upper])
+    minus_sum = across(back_minus + grads[1], [(dec(s + 1), s) for s in lower])
+    back_plus = across(back_plus + grads[4], [(dec(s - 1), dec(s)) for s in upper])
     summed = exchange_add(summed, "seq", RING)
     summed, back_plus = lax.optimization_barrier((summed, back_plus))
-    plus_sum = across(added(back_plus, grads[3]), [(dec(s - 1), s) for s in upper])
+    plus_sum = across(back_plus + grads[3], [(dec(s - 1), s) for s in upper])
     summed = ring_total(summed, shard_index)
-    returned = (
-        own_sum.astype(jnp.float32) + minus_sum.astype(jnp.float32) + plus_sum.astype(jnp.float32)
-    ).astype(jnp.bfloat16)
+    returned_parts.append((own_sum, minus_sum, plus_sum))
+
+    returned = jnp.concatenate(
+        [
+            (a.astype(jnp.float32) + b.astype(jnp.float32) + d.astype(jnp.float32)).astype(jnp.bfloat16)
+            for a, b, d in returned_parts
+        ],
+        axis=2,
+    )
+    produced = jnp.concatenate([out[0] for out in outs], axis=2)
     chosen = lax.dynamic_index_in_dim(summed, phase_index, 0, keepdims=False)
     scale = jnp.where(phase_index == 0, head_gains[1], 1.0) * math.sqrt(token_total)
     gain_total = chosen / scale

time: 175 us -> 160 us (0.914)
  the two profiles are of different devices: /device:TPU:8 before, /device:TPU:28 now
where the time goes in v8:
time: 160 us; the launch traced here: 159 us
  starting transfers between devices  73.8 us (46%)
  waiting for transfers between devices  38.5 us (24%)
  Pallas kernels  31 us (19%)
  other arithmetic  8.01 us (5%)
  local copies, waits for them, and re-layouts  5.43 us (3%)
  between operations  2.49 us (2%)
    ppermute x24, starting transfers between devices, across(): return lax.ppermute(value, ('phase', 'seq'), pairs)  51.4 us
    pallas_call x2, Pallas kernels, attention_block(): pl.pallas_call(attention_kernel, grid_spec=grid_spec, out_shape=[jax.Shap...  31 us
    ppermute x24, waiting for transfers between devices, across(): return lax.ppermute(value, ('phase', 'seq'), pairs)  19.7 us
    ppermute x5, waiting for transfers between devices, exchange_add(): lax.ppermute(value, axis, [(i, i ^ stride) for i in range(count)])  13.2 us
    ppermute x4, starting transfers between devices, ring_shift(): return lax.ppermute(value, 'seq', pairs)  12 us
    ppermute x5, starting transfers between devices, exchange_add(): lax.ppermute(value, axis, [(i, i ^ stride) for i in range(count)])  10.4 us
    ppermute x4, waiting for transfers between devices, ring_shift(): return lax.ppermute(value, 'seq', pairs)  5.59 us
  transfers between devices with their start and end apart: 33, of which 13 were waited for; matrix products, arithmetic and copies ran while one was open for 6% of the time, Pallas kernels for 10%

profile of v8, /device:TPU:28, one launch (start us, length us, event | category | flops | bytes accessed | tf_op | source)
XLA Modules:
  0.0 159.3 jit_solution(3610707880826230090)
XLA Ops:
  0.6 1.3 fusion.13
  2.0 7.9 %collective-permute-start.3 = (bf16[2,128,1024]{2,1,0:T(8,128)(2,1)S(1)}, bf16[2,128,1024]{2,1,0:T(8,128)(2,1)S(1)}, u32[]{:S(2)}, u32[]{:S(2)}) collective-permute-start(bf16[2,128,1024]{2,1,0:T(8,128)(2,1)S(1)} %get-tuple-element.48.own_ref), channel_id=1, source_target_pairs={{8,128},{16,136},{24,144},{32,152},{40,160},{48,168},{56,176},{64,... | collective-permute-start | bytes 1572872 | tf_op jit(solution)/shard_map/ppermute | solution.py:187
  9.9 1.3 collective-permute-start.15
  11.2 2.1 %collective-permute-start.2 = (bf16[2,128,1024]{2,1,0:T(8,128)(2,1)S(1)}, bf16[2,128,1024]{2,1,0:T(8,128)(2,1)}, u32[]{:S(2)}, u32[]{:S(2)}) collective-permute-start(bf16[2,128,1024]{2,1,0:T(8,128)(2,1)S(1)} %get-tuple-element.48.own_ref), channel_id=1, source_target_pairs={{0,128},{8,136},{16,144},{24,152},{32,160},{40,168},{48,176},{56,1... | collective-permute-start | bytes 1572872 | tf_op jit(solution)/shard_map/ppermute | solution.py:187
  13.3 2.1 %collective-permute-start = (bf16[2,128,1024]{2,1,0:T(8,128)(2,1)S(1)}, bf16[2,128,1024]{2,1,0:T(8,128)(2,1)}, u32[]{:S(2)}, u32[]{:S(2)}) collective-permute-start(bf16[2,128,1024]{2,1,0:T(8,128)(2,1)S(1)} %get-tuple-element.48.own_ref), channel_id=1, source_target_pairs={{0,136},{8,144},{16,152},{24,160},{32,168},{40,176},{48,184},{56,1... | collective-permute-start | bytes 1572872 | tf_op jit(solution)/shard_map/ppermute | solution.py:187
  15.5 1.3 collective-permute-start.12
  16.8 0.2 reduce-window_1_clone.1
  17.2 1.5 collective-permute-start.4
  18.6 3.5 %collective-permute-done.15.refs_3_ = bf16[2,128,1024]{2,1,0:T(8,128)(2,1)S(1)} collective-permute-done((bf16[2,128,1024]{2,1,0:T(8,128)(2,1)S(1)}, bf16[2,128,1024]{2,1,0:T(8,128)(2,1)S(1)}, u32[]{:S(2)}, u32[]{:S(2)}) %collective-permute-start.15) | collective-permute-done | bytes 524320 | tf_op jit(solution)/shard_map/ppermute | solution.py:187
  22.1 1.4 collective-permute-start.16
  23.6 0.6 fusion.11
  24.9 0.6 dynamic_slice.14
  26.1 0.2 convert_reduce_fusion
  26.3 1.5 collective-permute-start.1
  27.8 1.5 collective-permute-start.5
  29.3 14.8 %collective-permute-start.14 = (bf16[2,128,1024]{2,1,0:T(8,128)(2,1)S(1)}, bf16[2,128,1024]{2,1,0:T(8,128)(2,1)}, u32[]{:S(2)}, u32[]{:S(2)}) collective-permute-start(bf16[2,128,1024]{2,1,0:T(8,128)(2,1)S(1)} %get-tuple-element.49.own_ref), channel_id=1, source_target_pairs={{0,128},{8,136},{16,144},{24,152},{32,160},{40,168},{48,176},{56,1... | collective-permute-start | bytes 1572872 | tf_op jit(solution)/shard_map/ppermute | solution.py:187
  44.1 1.5 collective-permute-start.13
  45.6 1.5 collective-permute-start.17
  47.1 0.6 fusion.15
  47.7 0.7 broadcast_in_dim.16
  48.4 15.4 %shard_map.50 = (bf16[2,128,1024]{2,1,0:T(8,128)(2,1)}, bf16[2,128,1024]{2,1,0:T(8,128)(2,1)}, bf16[2,128,1024]{2,1,0:T(8,128)(2,1)}, bf16[2,128,1024]{2,1,0:T(8...) custom-call(s32[1]{0:T(128)} %bitcast.5.start_ref, ...), custom_call_target="tpu_custom_call" | custom-call | flops 1610612736 | bytes 7340032 | tf_op jit(solution)/shard_map/pallas_call | solution.py:123
  63.8 0.9 slice_reduce_fusion.3
  64.9 15.6 %shard_map.51 = (bf16[2,128,1024]{2,1,0:T(8,128)(2,1)}, bf16[2,128,1024]{2,1,0:T(8,128)(2,1)}, bf16[2,128,1024]{2,1,0:T(8,128)(2,1)}, bf16[2,128,1024]{2,1,0:T(8...) custom-call(s32[1]{0:T(128)} %bitcast.5.start_ref, ...), custom_call_target="tpu_custom_call" | custom-call | flops 1610612736 | bytes 7340032 | tf_op jit(solution)/shard_map/pallas_call | solution.py:123
  80.6 0.9 slice_reduce_fusion.1
  81.6 0.7 collective-permute-start.23
  82.3 0.7 collective-permute-start.24
  83.1 8.5 %collective-permute-start.19 = (f32[2,32]{1,0:T(2,128)S(1)}, f32[2,32]{1,0:T(2,128)S(1)}, u32[]{:S(2)}, u32[]{:S(2)}) collective-permute-start(f32[2,32]{1,0:T(2,128)S(1)} %maximum_select_fusion.1), channel_id=1, source_target_pairs={{0,128},{128,0},{1,129},{129,1},{2,130},{130,2},{3,131},{131,3},{4... | collective-permute-start | bytes 776 | tf_op jit(solution)/shard_map/ppermute | solution.py:162
  91.6 0.8 collective-permute-done.19
  92.6 3.6 %collective-permute-done.20 = f32[2,32]{1,0:T(2,128)S(1)} collective-permute-done((f32[2,32]{1,0:T(2,128)S(1)}, f32[2,32]{1,0:T(2,128)S(1)}, u32[]{:S(2)}, u32[]{:S(2)}) %collective-permute-start.20) | collective-permute-done | bytes 288 | tf_op jit(solution)/shard_map/ppermute | solution.py:162
  96.2 1.2 collective-permute-start.21
  97.4 2.4 %collective-permute-done.21 = f32[2,32]{1,0:T(2,128)S(1)} collective-permute-done((f32[2,32]{1,0:T(2,128)S(1)}, f32[2,32]{1,0:T(2,128)S(1)}, u32[]{:S(2)}, u32[]{:S(2)}) %collective-permute-start.21) | collective-permute-done | bytes 288 | tf_op jit(solution)/shard_map/ppermute | solution.py:162
  99.8 0.5 collective-permute-start.22
  100.3 0.7 collective-permute-start.9
  101.0 3.9 %collective-permute-done.22 = f32[2,32]{1,0:T(2,128)S(1)} collective-permute-done((f32[2,32]{1,0:T(2,128)S(1)}, f32[2,32]{1,0:T(2,128)S(1)}, u32[]{:S(2)}, u32[]{:S(2)}) %collective-permute-start.22) | collective-permute-done | bytes 288 | tf_op jit(solution)/shard_map/ppermute | solution.py:162
  104.9 2.0 %add.123 = bf16[2,128,1024]{2,1,0:T(8,128)(2,1)} add(bf16[2,128,1024]{2,1,0:T(8,128)(2,1)S(1)} %collective-permute-done.24, bf16[2,128,1024]{2,1,0:T(8,128)(2,1)} %get-tuple-element.38) | non-fusion elementwise | flops 262144 | bytes 1572864 | tf_op jit(solution)/shard_map/add | solution.py:246
  106.9 0.8 collective-permute-start.27
  107.9 1.5 collective-permute-start.7
  109.4 0.2 add.113
  109.6 0.8 collective-permute-start.10
  110.4 2.5 %collective-permute-done.26 = f32[2,32]{1,0:T(2,128)S(1)} collective-permute-done((f32[2,32]{1,0:T(2,128)S(1)}, f32[2,32]{1,0:T(2,128)S(1)}, u32[]{:S(2)}, u32[]{:S(2)}) %collective-permute-start.26) | collective-permute-done | bytes 288 | tf_op jit(solution)/shard_map/ppermute | solution.py:162
  113.0 3.1 %collective-permute-start.29 = (f32[1,2,32]{2,1,0:T(2,128)S(1)}, f32[1,2,32]{2,1,0:T(2,128)S(1)}, u32[]{:S(2)}, u32[]{:S(2)}) collective-permute-start(f32[1,2,32]{2,1,0:T(2,128)S(1)} %bitcast.30), channel_id=1, source_target_pairs={{0,56},{8,0},{16,8},{24,16},{32,24},{40,32},{48,40},{56,48},{64,12... | collective-permute-start | bytes 776 | tf_op jit(solution)/shard_map/ppermute | solution.py:143
  116.1 1.3 collective-permute-done.29
  117.4 1.7 %collective-permute-start.30 = (f32[2,2,32]{2,1,0:T(2,128)S(1)}, f32[2,2,32]{2,1,0:T(2,128)S(1)}, u32[]{:S(2)}, u32[]{:S(2)}) collective-permute-start(f32[2,2,32]{2,1,0:T(2,128)S(1)} %pad_maximum_fusion.2), channel_id=1, source_target_pairs={{0,48},{8,56},{16,0},{24,8},{32,16},{40,24},{48,32},{56,40},{64,11... | collective-permute-start | bytes 1544 | tf_op jit(solution)/shard_map/ppermute | solution.py:143
  119.1 2.8 %collective-permute-done.30 = f32[2,2,32]{2,1,0:T(2,128)S(1)} collective-permute-done((f32[2,2,32]{2,1,0:T(2,128)S(1)}, f32[2,2,32]{2,1,0:T(2,128)S(1)}, u32[]{:S(2)}, u32[]{:S(2)}) %collective-permute-start.30) | collective-permute-done | bytes 544 | tf_op jit(solution)/shard_map/ppermute | solution.py:143
  121.9 3.0 %collective-permute-start.31 = (f32[4,2,32]{2,1,0:T(2,128)S(1)}, f32[4,2,32]{2,1,0:T(2,128)S(1)}, u32[]{:S(2)}, u32[]{:S(2)}) collective-permute-start(f32[4,2,32]{2,1,0:T(2,128)S(1)} %pad_maximum_fusion.1), channel_id=1, source_target_pairs={{0,48},{8,56},{16,0},{24,8},{32,16},{40,24},{48,32},{56,40},{64,11... | collective-permute-start | bytes 3080 | tf_op jit(solution)/shard_map/ppermute | solution.py:143
  124.8 1.5 collective-permute-done.31
  126.4 4.2 %collective-permute-start.32 = (f32[6,2,32]{2,1,0:T(2,128)S(1)}, f32[6,2,32]{2,1,0:T(2,128)S(1)}, u32[]{:S(2)}, u32[]{:S(2)}) collective-permute-start(f32[6,2,32]{2,1,0:T(2,128)S(1)} %pad_maximum_fusion), channel_id=1, source_target_pairs={{0,48},{8,56},{16,0},{24,8},{32,16},{40,24},{48,32},{56,40},{64,11... | collective-permute-start | bytes 4616 | tf_op jit(solution)/shard_map/ppermute | solution.py:143
  130.6 1.3 collective-permute-start.6
  131.9 1.3 collective-permute-start.18
  133.2 1.2 add.111
  134.5 1.4 collective-permute-start.8
  135.9 0.2 add.120
  136.1 0.2 add.124
  136.4 1.3 collective-permute-start.25
  137.7 0.2 add.114
  137.9 1.3 collective-permute-start.11
  139.3 1.3 collective-permute-start.28
  140.6 0.5 fusion.10
  141.1 5.6 %collective-permute-done.8 = bf16[2,128,1024]{2,1,0:T(8,128)(2,1)S(1)} collective-permute-done((bf16[2,128,1024]{2,1,0:T(8,128)(2,1)S(1)}, bf16[2,128,1024]{2,1,0:T(8,128)(2,1)S(1)}, u32[]{:S(2)}, u32[]{:S(2)}) %collective-permute-start.8) | collective-permute-done | bytes 524320 | tf_op jit(solution)/shard_map/ppermute | solution.py:187
  146.8 5.2 %collective-permute-done.11 = bf16[2,128,1024]{2,1,0:T(8,128)(2,1)S(1)} collective-permute-done((bf16[2,128,1024]{2,1,0:T(8,128)(2,1)S(1)}, bf16[2,128,1024]{2,1,0:T(8,128)(2,1)S(1)}, u32[]{:S(2)}, u32[]{:S(2)}) %collective-permute-start.11) | collective-permute-done | bytes 524320 | tf_op jit(solution)/shard_map/ppermute | solution.py:187
  152.0 0.3 fusion
  152.4 5.2 %collective-permute-done.28 = bf16[2,128,1024]{2,1,0:T(8,128)(2,1)S(1)} collective-permute-done((bf16[2,128,1024]{2,1,0:T(8,128)(2,1)S(1)}, bf16[2,128,1024]{2,1,0:T(8,128)(2,1)S(1)}, u32[]{:S(2)}, u32[]{:S(2)}) %collective-permute-start.28) | collective-permute-done | bytes 524320 | tf_op jit(solution)/shard_map/ppermute | solution.py:187
  157.6 0.3 fusion.1
  157.9 1.4 maximum_select_fusion
  (83 shorter events, 1.3 us)
Async XLA Ops:
  0.6 16.2 %copy-start.10 = (s32[1,2,8]{2,1,0:T(2,128)S(1)}, s32[1,2,8]{2,1,0:T(2,128)}, u32[]{:S(2)}) copy-start(s32[1,2,8]{2,1,0:T(2,128)} %param.5) | copy-start | bytes 196
  0.6 46.5 %copy-start.9 = (f32[2,32]{1,0:T(2,128)S(1)}, f32[2,32]{1,0:T(2,128)}, u32[]{:S(2)}) copy-start(f32[2,32]{1,0:T(2,128)} %param.4) | copy-start | bytes 772
  1.9 46.4 %copy-start.8 = (bf16[2,128,1024]{2,1,0:T(8,128)(2,1)}, bf16[2,128,1024]{2,1,0:T(8,128)(2,1)S(1)}, u32[]{:S(2)}) copy-start(bf16[2,128,1024]{2,1,0:T(8,128)(2,1)S(1)} %get-tuple-element.48.own_ref) | copy-start | bytes 1572868
  1.9 61.8 %copy-start.7 = (bf16[2,128,1024]{2,1,0:T(8,128)(2,1)}, bf16[2,128,1024]{2,1,0:T(8,128)(2,1)S(1)}, u32[]{:S(2)}) copy-start(bf16[2,128,1024]{2,1,0:T(8,128)(2,1)S(1)} %get-tuple-element.49.own_ref) | copy-start | bytes 1572868
  2.0 15.2 %collective-permute-start.3 = (bf16[2,128,1024]{2,1,0:T(8,128)(2,1)S(1)}, bf16[2,128,1024]{2,1,0:T(8,128)(2,1)S(1)}, u32[]{:S(2)}, u32[]{:S(2)}) collective-permute-start(bf16[2,128,1024]{2,1,0:T(8,128)(2,1)S(1)} %get-tuple-element.48.own_ref), channel_id=1, source_target_pairs={{8,128},{16,136},{24,144},{32,152},{40,160},{48,168},{56,176},{64,... | collective-permute-start | bytes 1572872 | tf_op jit(solution)/shard_map/ppermute | solution.py:187
  9.9 12.3 %collective-permute-start.15 = (bf16[2,128,1024]{2,1,0:T(8,128)(2,1)S(1)}, bf16[2,128,1024]{2,1,0:T(8,128)(2,1)S(1)}, u32[]{:S(2)}, u32[]{:S(2)}) collective-permute-start(bf16[2,128,1024]{2,1,0:T(8,128)(2,1)S(1)} %get-tuple-element.49.own_ref), channel_id=1, source_target_pairs={{8,128},{16,136},{24,144},{32,152},{40,160},{48,168},{56,176},{64,... | collective-permute-start | bytes 1572872 | tf_op jit(solution)/shard_map/ppermute | solution.py:187
  11.2 18.1 %collective-permute-start.2 = (bf16[2,128,1024]{2,1,0:T(8,128)(2,1)S(1)}, bf16[2,128,1024]{2,1,0:T(8,128)(2,1)}, u32[]{:S(2)}, u32[]{:S(2)}) collective-permute-start(bf16[2,128,1024]{2,1,0:T(8,128)(2,1)S(1)} %get-tuple-element.48.own_ref), channel_id=1, source_target_pairs={{0,128},{8,136},{16,144},{24,152},{32,160},{40,168},{48,176},{56,1... | collective-permute-start | bytes 1572872 | tf_op jit(solution)/shard_map/ppermute | solution.py:187
  13.3 13.0 %collective-permute-start = (bf16[2,128,1024]{2,1,0:T(8,128)(2,1)S(1)}, bf16[2,128,1024]{2,1,0:T(8,128)(2,1)}, u32[]{:S(2)}, u32[]{:S(2)}) collective-permute-start(bf16[2,128,1024]{2,1,0:T(8,128)(2,1)S(1)} %get-tuple-element.48.own_ref), channel_id=1, source_target_pairs={{0,136},{8,144},{16,152},{24,160},{32,168},{40,176},{48,184},{56,1... | collective-permute-start | bytes 1572872 | tf_op jit(solution)/shard_map/ppermute | solution.py:187
  15.5 28.6 %collective-permute-start.12 = (bf16[2,128,1024]{2,1,0:T(8,128)(2,1)S(1)}, bf16[2,128,1024]{2,1,0:T(8,128)(2,1)S(1)}, u32[]{:S(2)}, u32[]{:S(2)}) collective-permute-start(bf16[2,128,1024]{2,1,0:T(8,128)(2,1)S(1)} %get-tuple-element.49.own_ref), channel_id=1, source_target_pairs={{0,136},{8,144},{16,152},{24,160},{32,168},{40,176},{48,184},{56,1... | collective-permute-start | bytes 1572872 | tf_op jit(solution)/shard_map/ppermute | solution.py:187
  17.2 31.2 %copy-start.14 = (bf16[2,128,1024]{2,1,0:T(8,128)(2,1)}, bf16[2,128,1024]{2,1,0:T(8,128)(2,1)S(1)}, u32[]{:S(2)}) copy-start(bf16[2,128,1024]{2,1,0:T(8,128)(2,1)S(1)} %collective-permute-done.3.refs_3_) | copy-start | bytes 1572868
  17.2 10.6 %collective-permute-start.4 = (bf16[2,128,1024]{2,1,0:T(8,128)(2,1)S(1)}, bf16[2,128,1024]{2,1,0:T(8,128)(2,1)}, u32[]{:S(2)}, u32[]{:S(2)}) collective-permute-start(bf16[2,128,1024]{2,1,0:T(8,128)(2,1)S(1)} %collective-permute-done.3.refs_3_), channel_id=1, source_target_pairs={{136,128},{144,136},{152,144},{160,152},{168,160},{176,168},{184,1... | collective-permute-start | bytes 1572872 | tf_op jit(solution)/shard_map/ppermute | solution.py:187
  22.1 41.7 %copy-start.12 = (bf16[2,128,1024]{2,1,0:T(8,128)(2,1)}, bf16[2,128,1024]{2,1,0:T(8,128)(2,1)S(1)}, u32[]{:S(2)}) copy-start(bf16[2,128,1024]{2,1,0:T(8,128)(2,1)S(1)} %collective-permute-done.15.refs_3_) | copy-start | bytes 1572868
  22.1 23.4 %collective-permute-start.16 = (bf16[2,128,1024]{2,1,0:T(8,128)(2,1)S(1)}, bf16[2,128,1024]{2,1,0:T(8,128)(2,1)}, u32[]{:S(2)}, u32[]{:S(2)}) collective-permute-start(bf16[2,128,1024]{2,1,0:T(8,128)(2,1)S(1)} %collective-permute-done.15.refs_3_), channel_id=1, source_target_pairs={{136,128},{144,136},{152,144},{160,152},{168,160},{176,168},{184,1... | collective-permute-start | bytes 1572872 | tf_op jit(solution)/shard_map/ppermute | solution.py:187
  26.3 21.4 %collective-permute-start.1 = (bf16[2,128,1024]{2,1,0:T(8,128)(2,1)}, bf16[2,128,1024]{2,1,0:T(8,128)(2,1)}, u32[]{:S(2)}, u32[]{:S(2)}) collective-permute-start(bf16[2,128,1024]{2,1,0:T(8,128)(2,1)} %collective-permute-done.refs_1_), channel_id=1, source_target_pairs={{128,136},{136,144},{144,152},{152,160},{160,168},{168,176},{176,1... | collective-permute-start | bytes 1572872 | tf_op jit(solution)/shard_map/ppermute | solution.py:187
  27.8 19.9 %collective-permute-start.5 = (bf16[2,128,1024]{2,1,0:T(8,128)(2,1)}, bf16[2,128,1024]{2,1,0:T(8,128)(2,1)}, u32[]{:S(2)}, u32[]{:S(2)}) collective-permute-start(bf16[2,128,1024]{2,1,0:T(8,128)(2,1)} %collective-permute-done.4.refs_4_), channel_id=1, source_target_pairs={{136,128},{144,136},{152,144},{160,152},{168,160},{176,168},{184,1... | collective-permute-start | bytes 1572872 | tf_op jit(solution)/shard_map/ppermute | solution.py:187
  29.3 35.6 %collective-permute-start.14 = (bf16[2,128,1024]{2,1,0:T(8,128)(2,1)S(1)}, bf16[2,128,1024]{2,1,0:T(8,128)(2,1)}, u32[]{:S(2)}, u32[]{:S(2)}) collective-permute-start(bf16[2,128,1024]{2,1,0:T(8,128)(2,1)S(1)} %get-tuple-element.49.own_ref), channel_id=1, source_target_pairs={{0,128},{8,136},{16,144},{24,152},{32,160},{40,168},{48,176},{56,1... | collective-permute-start | bytes 1572872 | tf_op jit(solution)/shard_map/ppermute | solution.py:187
  44.1 19.7 %copy-start.13 = (bf16[2,128,1024]{2,1,0:T(8,128)(2,1)}, bf16[2,128,1024]{2,1,0:T(8,128)(2,1)S(1)}, u32[]{:S(2)}) copy-start(bf16[2,128,1024]{2,1,0:T(8,128)(2,1)S(1)} %collective-permute-done.12.refs_1_) | copy-start | bytes 1572868
  44.1 20.8 %collective-permute-start.13 = (bf16[2,128,1024]{2,1,0:T(8,128)(2,1)S(1)}, bf16[2,128,1024]{2,1,0:T(8,128)(2,1)}, u32[]{:S(2)}, u32[]{:S(2)}) collective-permute-start(bf16[2,128,1024]{2,1,0:T(8,128)(2,1)S(1)} %collective-permute-done.12.refs_1_), channel_id=1, source_target_pairs={{128,136},{136,144},{144,152},{152,160},{160,168},{168,176},{176,1... | collective-permute-start | bytes 1572872 | tf_op jit(solution)/shard_map/ppermute | solution.py:187
  45.6 19.4 %collective-permute-start.17 = (bf16[2,128,1024]{2,1,0:T(8,128)(2,1)}, bf16[2,128,1024]{2,1,0:T(8,128)(2,1)}, u32[]{:S(2)}, u32[]{:S(2)}) collective-permute-start(bf16[2,128,1024]{2,1,0:T(8,128)(2,1)} %collective-permute-done.16.refs_4_), channel_id=1, source_target_pairs={{136,128},{144,136},{152,144},{160,152},{168,160},{176,168},{184,1... | collective-permute-start | bytes 1572872 | tf_op jit(solution)/shard_map/ppermute | solution.py:187
  64.9 35.4 %copy-start.11 = (bf16[2,128,1024]{2,1,0:T(8,128)(2,1)S(1)}, bf16[2,128,1024]{2,1,0:T(8,128)(2,1)}, u32[]{:S(2)}) copy-start(bf16[2,128,1024]{2,1,0:T(8,128)(2,1)} %get-tuple-element.26) | copy-start | bytes 1572868
  80.5 28.8 %copy-start.4 = (bf16[2,128,1024]{2,1,0:T(8,128)(2,1)S(1)}, bf16[2,128,1024]{2,1,0:T(8,128)(2,1)}, u32[]{:S(2)}) copy-start(bf16[2,128,1024]{2,1,0:T(8,128)(2,1)} %get-tuple-element.27) | copy-start | bytes 1572868
  81.6 23.3 %collective-permute-start.23 = (bf16[2,128,1024]{2,1,0:T(8,128)(2,1)}, bf16[2,128,1024]{2,1,0:T(8,128)(2,1)S(1)}, u32[]{:S(2)}, u32[]{:S(2)}) collective-permute-start(bf16[2,128,1024]{2,1,0:T(8,128)(2,1)} %get-tuple-element.32), channel_id=1, source_target_pairs={{136,128},{144,136},{152,144},{160,152},{168,160},{176,168},{184,1... | collective-permute-start | bytes 1572872 | tf_op jit(solution)/shard_map/ppermute | solution.py:187
  82.3 22.6 %collective-permute-start.24 = (bf16[2,128,1024]{2,1,0:T(8,128)(2,1)}, bf16[2,128,1024]{2,1,0:T(8,128)(2,1)S(1)}, u32[]{:S(2)}, u32[]{:S(2)}) collective-permute-start(bf16[2,128,1024]{2,1,0:T(8,128)(2,1)} %get-tuple-element.33), channel_id=1, source_target_pairs={{128,136},{136,144},{144,152},{152,160},{160,168},{168,176},{176,1... | collective-permute-start | bytes 1572872 | tf_op jit(solution)/shard_map/ppermute | solution.py:187
  83.1 9.3 %collective-permute-start.19 = (f32[2,32]{1,0:T(2,128)S(1)}, f32[2,32]{1,0:T(2,128)S(1)}, u32[]{:S(2)}, u32[]{:S(2)}) collective-permute-start(f32[2,32]{1,0:T(2,128)S(1)} %maximum_select_fusion.1), channel_id=1, source_target_pairs={{0,128},{128,0},{1,129},{129,1},{2,130},{130,2},{3,131},{131,3},{4... | collective-permute-start | bytes 776 | tf_op jit(solution)/shard_map/ppermute | solution.py:162
  92.5 3.6 %collective-permute-start.20 = (f32[2,32]{1,0:T(2,128)S(1)}, f32[2,32]{1,0:T(2,128)S(1)}, u32[]{:S(2)}, u32[]{:S(2)}) collective-permute-start(f32[2,32]{1,0:T(2,128)S(1)} %fusion.16), channel_id=1, source_target_pairs={{0,1},{1,0},{2,3},{3,2},{4,5},{5,4},{6,7},{7,6},{8,9},{9,8},{10,11... | collective-permute-start | bytes 776 | tf_op jit(solution)/shard_map/ppermute | solution.py:162
  96.2 3.6 %collective-permute-start.21 = (f32[2,32]{1,0:T(2,128)S(1)}, f32[2,32]{1,0:T(2,128)S(1)}, u32[]{:S(2)}, u32[]{:S(2)}) collective-permute-start(f32[2,32]{1,0:T(2,128)S(1)} %fusion.17), channel_id=1, source_target_pairs={{0,2},{1,3},{2,0},{3,1},{4,6},{5,7},{6,4},{7,5},{8,10},{9,11},{10,... | collective-permute-start | bytes 776 | tf_op jit(solution)/shard_map/ppermute | solution.py:162
  99.8 5.1 %collective-permute-start.22 = (f32[2,32]{1,0:T(2,128)S(1)}, f32[2,32]{1,0:T(2,128)S(1)}, u32[]{:S(2)}, u32[]{:S(2)}) collective-permute-start(f32[2,32]{1,0:T(2,128)S(1)} %add.118), channel_id=1, source_target_pairs={{0,4},{1,5},{2,6},{3,7},{4,0},{5,1},{6,2},{7,3},{8,12},{9,13},{10,... | collective-permute-start | bytes 776 | tf_op jit(solution)/shard_map/ppermute | solution.py:162
  100.3 9.1 %collective-permute-start.9 = (bf16[2,128,1024]{2,1,0:T(8,128)(2,1)S(1)}, bf16[2,128,1024]{2,1,0:T(8,128)(2,1)S(1)}, u32[]{:S(2)}, u32[]{:S(2)}) collective-permute-start(bf16[2,128,1024]{2,1,0:T(8,128)(2,1)S(1)} %copy-done.11), channel_id=1, source_target_pairs={{128,136},{136,144},{144,152},{152,160},{160,168},{168,176},{176,1... | collective-permute-start | bytes 1572872 | tf_op jit(solution)/shard_map/ppermute | solution.py:187
  106.9 26.3 %copy-start.1 = (bf16[2,128,1024]{2,1,0:T(8,128)(2,1)S(1)}, bf16[2,128,1024]{2,1,0:T(8,128)(2,1)}, u32[]{:S(2)}) copy-start(bf16[2,128,1024]{2,1,0:T(8,128)(2,1)} %get-tuple-element.25) | copy-start | bytes 1572868
  106.9 6.0 %collective-permute-start.27 = (bf16[2,128,1024]{2,1,0:T(8,128)(2,1)}, bf16[2,128,1024]{2,1,0:T(8,128)(2,1)S(1)}, u32[]{:S(2)}, u32[]{:S(2)}) collective-permute-start(bf16[2,128,1024]{2,1,0:T(8,128)(2,1)} %add.123), channel_id=1, source_target_pairs={{128,136},{136,144},{144,152},{152,160},{160,168},{168,176},{176,1... | collective-permute-start | bytes 1572872 | tf_op jit(solution)/shard_map/ppermute | solution.py:187
  107.8 5.2 %collective-permute-start.26 = (f32[2,32]{1,0:T(2,128)S(1)}, f32[2,32]{1,0:T(2,128)S(1)}, u32[]{:S(2)}, u32[]{:S(2)}) collective-permute-start(f32[2,32]{1,0:T(2,128)S(1)} %add.119), channel_id=1, source_target_pairs={{0,64},{8,72},{16,80},{24,88},{32,96},{40,104},{48,112},{56,120},{... | collective-permute-start | bytes 776 | tf_op jit(solution)/shard_map/ppermute | solution.py:162
  107.9 25.3 %collective-permute-start.7 = (bf16[2,128,1024]{2,1,0:T(8,128)(2,1)}, bf16[2,128,1024]{2,1,0:T(8,128)(2,1)}, u32[]{:S(2)}, u32[]{:S(2)}) collective-permute-start(bf16[2,128,1024]{2,1,0:T(8,128)(2,1)} %get-tuple-element.24), channel_id=1, source_target_pairs={{136,128},{144,136},{152,144},{160,152},{168,160},{176,168},{184,1... | collective-permute-start | bytes 1572872 | tf_op jit(solution)/shard_map/ppermute | solution.py:187
  109.6 26.3 %copy-start.3 = (bf16[2,128,1024]{2,1,0:T(8,128)(2,1)S(1)}, bf16[2,128,1024]{2,1,0:T(8,128)(2,1)}, u32[]{:S(2)}) copy-start(bf16[2,128,1024]{2,1,0:T(8,128)(2,1)} %get-tuple-element.35) | copy-start | bytes 1572868
  109.6 26.8 %collective-permute-start.10 = (bf16[2,128,1024]{2,1,0:T(8,128)(2,1)S(1)}, bf16[2,128,1024]{2,1,0:T(8,128)(2,1)S(1)}, u32[]{:S(2)}, u32[]{:S(2)}) collective-permute-start(bf16[2,128,1024]{2,1,0:T(8,128)(2,1)S(1)} %add.113), channel_id=1, source_target_pairs={{128,136},{136,144},{144,152},{152,160},{160,168},{168,176},{176,1... | collective-permute-start | bytes 1572872 | tf_op jit(solution)/shard_map/ppermute | solution.py:187
  113.0 4.4 %collective-permute-start.29 = (f32[1,2,32]{2,1,0:T(2,128)S(1)}, f32[1,2,32]{2,1,0:T(2,128)S(1)}, u32[]{:S(2)}, u32[]{:S(2)}) collective-permute-start(f32[1,2,32]{2,1,0:T(2,128)S(1)} %bitcast.30), channel_id=1, source_target_pairs={{0,56},{8,0},{16,8},{24,16},{32,24},{40,32},{48,40},{56,48},{64,12... | collective-permute-start | bytes 776 | tf_op jit(solution)/shard_map/ppermute | solution.py:143
  117.4 4.5 %collective-permute-start.30 = (f32[2,2,32]{2,1,0:T(2,128)S(1)}, f32[2,2,32]{2,1,0:T(2,128)S(1)}, u32[]{:S(2)}, u32[]{:S(2)}) collective-permute-start(f32[2,2,32]{2,1,0:T(2,128)S(1)} %pad_maximum_fusion.2), channel_id=1, source_target_pairs={{0,48},{8,56},{16,0},{24,8},{32,16},{40,24},{48,32},{56,40},{64,11... | collective-permute-start | bytes 1544 | tf_op jit(solution)/shard_map/ppermute | solution.py:143
  121.9 4.5 %collective-permute-start.31 = (f32[4,2,32]{2,1,0:T(2,128)S(1)}, f32[4,2,32]{2,1,0:T(2,128)S(1)}, u32[]{:S(2)}, u32[]{:S(2)}) collective-permute-start(f32[4,2,32]{2,1,0:T(2,128)S(1)} %pad_maximum_fusion.1), channel_id=1, source_target_pairs={{0,48},{8,56},{16,0},{24,8},{32,16},{40,24},{48,32},{56,40},{64,11... | collective-permute-start | bytes 3080 | tf_op jit(solution)/shard_map/ppermute | solution.py:143
  126.4 11.5 %collective-permute-start.32 = (f32[6,2,32]{2,1,0:T(2,128)S(1)}, f32[6,2,32]{2,1,0:T(2,128)S(1)}, u32[]{:S(2)}, u32[]{:S(2)}) collective-permute-start(f32[6,2,32]{2,1,0:T(2,128)S(1)} %pad_maximum_fusion), channel_id=1, source_target_pairs={{0,48},{8,56},{16,0},{24,8},{32,16},{40,24},{48,32},{56,40},{64,11... | collective-permute-start | bytes 4616 | tf_op jit(solution)/shard_map/ppermute | solution.py:143
  130.6 8.6 %collective-permute-start.6 = (bf16[2,128,1024]{2,1,0:T(8,128)(2,1)}, bf16[2,128,1024]{2,1,0:T(8,128)(2,1)S(1)}, u32[]{:S(2)}, u32[]{:S(2)}) collective-permute-start(bf16[2,128,1024]{2,1,0:T(8,128)(2,1)} %get-tuple-element.23), channel_id=1, source_target_pairs={{128,0},{136,8},{144,16},{152,24},{160,32},{168,40},{176,48},{184,... | collective-permute-start | bytes 1572872 | tf_op jit(solution)/shard_map/ppermute | solution.py:187
  131.9 20.4 %collective-permute-start.18 = (bf16[2,128,1024]{2,1,0:T(8,128)(2,1)}, bf16[2,128,1024]{2,1,0:T(8,128)(2,1)S(1)}, u32[]{:S(2)}, u32[]{:S(2)}) collective-permute-start(bf16[2,128,1024]{2,1,0:T(8,128)(2,1)} %get-tuple-element.29), channel_id=1, source_target_pairs={{128,0},{136,8},{144,16},{152,24},{160,32},{168,40},{176,48},{184,... | collective-permute-start | bytes 1572872 | tf_op jit(solution)/shard_map/ppermute | solution.py:187
  134.5 1.7 %copy-start.2 = (bf16[2,128,1024]{2,1,0:T(8,128)(2,1)S(1)}, bf16[2,128,1024]{2,1,0:T(8,128)(2,1)}, u32[]{:S(2)}) copy-start(bf16[2,128,1024]{2,1,0:T(8,128)(2,1)} %get-tuple-element.40) | copy-start | bytes 1572868
  134.5 12.3 %collective-permute-start.8 = (bf16[2,128,1024]{2,1,0:T(8,128)(2,1)S(1)}, bf16[2,128,1024]{2,1,0:T(8,128)(2,1)S(1)}, u32[]{:S(2)}, u32[]{:S(2)}) collective-permute-start(bf16[2,128,1024]{2,1,0:T(8,128)(2,1)S(1)} %add.111), channel_id=1, source_target_pairs={{136,0},{144,8},{152,16},{160,24},{168,32},{176,40},{184,48},{192,... | collective-permute-start | bytes 1572872 | tf_op jit(solution)/shard_map/ppermute | solution.py:187
  136.1 1.5 copy-start
  136.4 16.0 %collective-permute-start.25 = (bf16[2,128,1024]{2,1,0:T(8,128)(2,1)S(1)}, bf16[2,128,1024]{2,1,0:T(8,128)(2,1)S(1)}, u32[]{:S(2)}, u32[]{:S(2)}) collective-permute-start(bf16[2,128,1024]{2,1,0:T(8,128)(2,1)S(1)} %add.120), channel_id=1, source_target_pairs={{136,0},{144,8},{152,16},{160,24},{168,32},{176,40},{184,48},{192,... | collective-permute-start | bytes 1572872 | tf_op jit(solution)/shard_map/ppermute | solution.py:187
  137.9 14.1 %collective-permute-start.11 = (bf16[2,128,1024]{2,1,0:T(8,128)(2,1)S(1)}, bf16[2,128,1024]{2,1,0:T(8,128)(2,1)S(1)}, u32[]{:S(2)}, u32[]{:S(2)}) collective-permute-start(bf16[2,128,1024]{2,1,0:T(8,128)(2,1)S(1)} %add.114), channel_id=1, source_target_pairs={{128,8},{136,16},{144,24},{152,32},{160,40},{168,48},{176,56},{184... | collective-permute-start | bytes 1572872 | tf_op jit(solution)/shard_map/ppermute | solution.py:187
  139.3 18.3 %collective-permute-start.28 = (bf16[2,128,1024]{2,1,0:T(8,128)(2,1)S(1)}, bf16[2,128,1024]{2,1,0:T(8,128)(2,1)S(1)}, u32[]{:S(2)}, u32[]{:S(2)}) collective-permute-start(bf16[2,128,1024]{2,1,0:T(8,128)(2,1)S(1)} %add.124), channel_id=1, source_target_pairs={{128,8},{136,16},{144,24},{152,32},{160,40},{168,48},{176,56},{184... | collective-permute-start | bytes 1572872 | tf_op jit(solution)/shard_map/ppermute | solution.py:187
  152.3 5.6 %copy-start.5 = (bf16[2,128,1024]{2,1,0:T(8,128)(2,1)S(1)}, bf16[2,128,1024]{2,1,0:T(8,128)(2,1)}, u32[]{:S(2)}) copy-start(bf16[2,128,1024]{2,1,0:T(8,128)(2,1)} %get-tuple-element.41) | copy-start | bytes 1572868
  152.3 5.6 %copy-start.6 = (bf16[2,128,1024]{2,1,0:T(8,128)(2,1)S(1)}, bf16[2,128,1024]{2,1,0:T(8,128)(2,1)}, u32[]{:S(2)}) copy-start(bf16[2,128,1024]{2,1,0:T(8,128)(2,1)} %get-tuple-element.42) | copy-start | bytes 1572868

commit v9 on v7

--- a/solution.py
+++ b/solution.py
@@ -139,7 +139,7 @@
     for source in range(count):
         base = source - source % RING
         pairs.append((source, base + (source - steps) % RING))
-    return lax.ppermute(value, "seq", pairs)
+    return lax.ppermute(value, ("phase", "seq"), pairs)
 
 
 def ring_total(value, shard_index):
@@ -158,7 +158,7 @@
 
 def exchange_add(value, axis, stride):
     count = lax.axis_size(axis)
-    return value + lax.ppermute(value, axis, [(i, i ^ stride) for i in range(count)])
+    return value + lax.ppermute(value, ("phase", axis), [(i, i ^ stride) for i in range(count)])
 
 
 def segment_of(block_ids, block_sizes, block_total):
@@ -220,7 +220,7 @@
         return a + b
 
     token_total = tok_dev * count * lax.axis_size("dp")
-    summed = exchange_add(terms, "phase", 1)
+    summed = lax.ppermute(terms, "phase", [(1, 0)])
     back_minus = across(grads[0], [(dec(s + 1), dec(s)) for s in lower])
     back_plus = across(grads[5], [(dec(s - 1), dec(s)) for s in upper])
     own_sum = across(grads[2], [(dec(s), s) for s in range(count)])
@@ -235,7 +235,8 @@
     returned = (
         own_sum.astype(jnp.float32) + minus_sum.astype(jnp.float32) + plus_sum.astype(jnp.float32)
     ).astype(jnp.bfloat16)
-    chosen = lax.dynamic_index_in_dim(summed, phase_index, 0, keepdims=False)
+    shared = lax.ppermute(summed, "phase", [(0, 1)])
+    chosen = jnp.where(phase_index == 0, summed[0], shared[1])
     scale = jnp.where(phase_index == 0, head_gains[1], 1.0) * math.sqrt(token_total)
     gain_total = chosen / scale
     result = jnp.where(phase_index == 0, returned, produced)[None]

time: 175 us -> 184 us (1.051)
  the two profiles are of different devices: /device:TPU:8 before, /device:TPU:1 now
where the time goes in v9:
time: 184 us
  starting transfers between devices  75 us (41%)
  waiting for transfers between devices  64.4 us (35%)
  Pallas kernels  29 us (16%)
  other arithmetic  9.65 us (5%)
  local copies, waits for them, and re-layouts  3.29 us (2%)
    ppermute x12, starting transfers between devices, across(): return lax.ppermute(value, ('phase', 'seq'), pairs)  67.1 us
    ppermute x12, waiting for transfers between devices, across(): return lax.ppermute(value, ('phase', 'seq'), pairs)  61.9 us
    pallas_call x1, Pallas kernels, attention_block(): pl.pallas_call(attention_kernel, grid_spec=grid_spec, out_shape=[jax.Shap...  29 us
  transfers between devices with their start and end apart: 22, of which 9 were waited for; matrix products, arithmetic and copies ran while one was open for 3% of the time, Pallas kernels for 0%

profile of v9, /device:TPU:1, one launch (start us, length us, event | category | flops | bytes accessed | tf_op | source)
XLA Modules:
  0.0 183.7 jit_solution(723677270456825531)
XLA Ops:
  0.6 1.3 collective-permute-start.3
  1.9 0.7 collective-permute-start
  2.7 15.0 %collective-permute-done.3 = bf16[2,128,2048]{2,1,0:T(8,128)(2,1)S(1)} collective-permute-done((bf16[2,128,2048]{2,1,0:T(8,128)(2,1)}, bf16[2,128,2048]{2,1,0:T(8,128)(2,1)S(1)}, u32[]{:S(2)}, u32[]{:S(2)}) %collective-permute-start.3) | collective-permute-done | bytes 1048608 | tf_op jit(solution)/shard_map/ppermute | solution.py:185
  17.6 1.3 collective-permute-start.4
  18.9 1.3 collective-permute-start.2
  20.2 0.0 collective-permute-done
  20.2 5.3 %collective-permute-start.1 = (bf16[2,128,2048]{2,1,0:T(8,128)(2,1)S(1)}, bf16[2,128,2048]{2,1,0:T(8,128)(2,1)}, u32[]{:S(2)}, u32[]{:S(2)}) collective-permute-start(bf16[2,128,2048]{2,1,0:T(8,128)(2,1)S(1)} %collective-permute-done), channel_id=1, source_target_pairs={{128,136},{136,144},{144,152},{152,160},{160,168},{168,176},{176,1... | collective-permute-start | bytes 3145736 | tf_op jit(solution)/shard_map/ppermute | solution.py:185
  25.5 8.0 %collective-permute-done.4 = bf16[2,128,2048]{2,1,0:T(8,128)(2,1)S(1)} collective-permute-done((bf16[2,128,2048]{2,1,0:T(8,128)(2,1)S(1)}, bf16[2,128,2048]{2,1,0:T(8,128)(2,1)S(1)}, u32[]{:S(2)}, u32[]{:S(2)}) %collective-permute-start.4) | collective-permute-done | bytes 1048608 | tf_op jit(solution)/shard_map/ppermute | solution.py:185
  33.5 1.3 collective-permute-start.5
  34.8 0.8 slice_bitcast_fusion.1
  35.6 0.2 reduce-window.8
  35.7 0.2 reduce-window_1_clone.1
  35.9 0.7 bitcast_subtract_fusion
  36.6 0.7 compare_convert_fusion.2
  37.3 0.1 compare_convert_fusion.1
  37.4 0.0 collective-permute-done.2
  37.4 0.0 collective-permute-done.1
  37.4 11.9 %collective-permute-done.5 = bf16[2,128,2048]{2,1,0:T(8,128)(2,1)} collective-permute-done((bf16[2,128,2048]{2,1,0:T(8,128)(2,1)S(1)}, bf16[2,128,2048]{2,1,0:T(8,128)(2,1)}, u32[]{:S(2)}, u32[]{:S(2)}) %collective-permute-start.5) | collective-permute-done | bytes 1048608 | tf_op jit(solution)/shard_map/ppermute | solution.py:185
  49.3 33.7 %conditional.1 = (bf16[2,128,2048]{2,1,0:T(8,128)(2,1)}, bf16[2,128,2048]{2,1,0:T(8,128)(2,1)}, bf16[2,128,2048]{2,1,0:T(8,128)(2,1)S(1)}, bf16[2,128,2048]{2,1,...) conditional(s32[]{:T(128)} %convert_element_type.45, () %tuple.54, ...), branch_computations={%region_2.3_spmd, %region_3.6_spmd} | conditional | flops 3221225472 | bytes 23072892 | solution.py:215
  49.3 0.8 reduce_sum.21
  50.7 0.6 dynamic_slice.16
  52.0 0.1 reduce_sum.22
  52.1 0.1 compare_convert_fusion
  52.2 0.6 broadcast_in_dim.23
  52.8 29.0 %branch_1_fun.5 = (bf16[2,128,2048]{2,1,0:T(8,128)(2,1)}, bf16[2,128,2048]{2,1,0:T(8,128)(2,1)}, bf16[2,128,2048]{2,1,0:T(8,128)(2,1)S(1)}, bf16[2,128,2048]{2,1...) custom-call(s32[1]{0:T(128)} %bitcast.1.start_ref, ...), custom_call_target="tpu_custom_call" | custom-call | flops 3221225472 | bytes 14680064 | tf_op jit(solution)/shard_map/cond/branch_1_fun/pallas_call | solution.py:122
  81.8 1.0 slice_reduce_fusion.1
  82.8 0.1 squeeze.42
  82.9 0.1 squeeze.43
  83.0 1.3 collective-permute-start.11
  84.3 5.4 %collective-permute-start.12 = (bf16[2,128,2048]{2,1,0:T(8,128)(2,1)}, bf16[2,128,2048]{2,1,0:T(8,128)(2,1)S(1)}, u32[]{:S(2)}, u32[]{:S(2)}) collective-permute-start(bf16[2,128,2048]{2,1,0:T(8,128)(2,1)} %get-tuple-element.244), channel_id=1, source_target_pairs={{128,136},{136,144},{144,152},{152,160},{160,168},{168,176},{176,1... | collective-permute-start | bytes 3145736 | tf_op jit(solution)/shard_map/ppermute | solution.py:185
  89.8 1.3 collective-permute-start.7
  91.1 0.8 collective-permute-done.7
  91.9 0.6 collective-permute-start.8
  92.5 0.0 collective-permute-done.8
  92.6 0.7 collective-permute-start.9
  93.2 0.0 collective-permute-done.9
  93.3 0.7 collective-permute-start.10
  93.9 0.0 collective-permute-done.10
  93.9 6.3 %collective-permute-done.11 = bf16[2,128,2048]{2,1,0:T(8,128)(2,1)} collective-permute-done((bf16[2,128,2048]{2,1,0:T(8,128)(2,1)}, bf16[2,128,2048]{2,1,0:T(8,128)(2,1)}, u32[]{:S(2)}, u32[]{:S(2)}) %collective-permute-start.11) | collective-permute-done | bytes 1048608 | tf_op jit(solution)/shard_map/ppermute | solution.py:185
  100.3 1.5 collective-permute-done.12
  101.8 1.4 add.106
  103.1 4.6 %collective-permute-start.15 = (bf16[2,128,2048]{2,1,0:T(8,128)(2,1)}, bf16[2,128,2048]{2,1,0:T(8,128)(2,1)S(1)}, u32[]{:S(2)}, u32[]{:S(2)}) collective-permute-start(bf16[2,128,2048]{2,1,0:T(8,128)(2,1)} %add.106), channel_id=1, source_target_pairs={{128,136},{136,144},{144,152},{152,160},{160,168},{168,176},{176,1... | collective-permute-start | bytes 3145736 | tf_op jit(solution)/shard_map/ppermute | solution.py:185
  107.8 0.7 collective-permute-start.14
  108.5 0.0 collective-permute-done.14
  108.5 11.3 %collective-permute-done.15 = bf16[2,128,2048]{2,1,0:T(8,128)(2,1)S(1)} collective-permute-done((bf16[2,128,2048]{2,1,0:T(8,128)(2,1)}, bf16[2,128,2048]{2,1,0:T(8,128)(2,1)S(1)}, u32[]{:S(2)}, u32[]{:S(2)}) %collective-permute-start.15) | collective-permute-done | bytes 1048608 | tf_op jit(solution)/shard_map/ppermute | solution.py:185
  119.7 0.6 collective-permute-start.17
  120.4 0.0 collective-permute-done.17
  120.4 0.7 collective-permute-start.18
  121.1 0.0 collective-permute-done.18
  121.1 0.7 collective-permute-start.19
  121.8 0.7 collective-permute-start.20
  122.5 39.2 %collective-permute-start.6 = (bf16[2,128,2048]{2,1,0:T(8,128)(2,1)}, bf16[2,128,2048]{2,1,0:T(8,128)(2,1)S(1)}, u32[]{:S(2)}, u32[]{:S(2)}) collective-permute-start(bf16[2,128,2048]{2,1,0:T(8,128)(2,1)} %get-tuple-element.241), channel_id=1, source_target_pairs={{128,0},{136,8},{144,16},{152,24},{160,32},{168,40},{176,48},{184,... | collective-permute-start | bytes 3145736 | tf_op jit(solution)/shard_map/ppermute | solution.py:185
  161.7 1.6 add.103
  163.3 0.7 collective-permute-start.13
  164.1 0.0 copy-start
  164.1 0.4 add.107
  164.5 4.7 %collective-permute-start.16 = (bf16[2,128,2048]{2,1,0:T(8,128)(2,1)S(1)}, bf16[2,128,2048]{2,1,0:T(8,128)(2,1)S(1)}, u32[]{:S(2)}, u32[]{:S(2)}) collective-permute-start(bf16[2,128,2048]{2,1,0:T(8,128)(2,1)S(1)} %add.107), channel_id=1, source_target_pairs={{128,8},{136,16},{144,24},{152,32},{160,40},{168,48},{176,56},{184... | collective-permute-start | bytes 3145736 | tf_op jit(solution)/shard_map/ppermute | solution.py:185
  169.2 0.0 collective-permute-done.20
  169.3 1.3 collective-permute-start.21
  170.6 1.7 collective-permute-done.21
  172.3 0.5 fusion.9
  172.9 0.0 collective-permute-done.13
  172.9 8.0 %collective-permute-done.16 = bf16[2,128,2048]{2,1,0:T(8,128)(2,1)S(1)} collective-permute-done((bf16[2,128,2048]{2,1,0:T(8,128)(2,1)S(1)}, bf16[2,128,2048]{2,1,0:T(8,128)(2,1)S(1)}, u32[]{:S(2)}, u32[]{:S(2)}) %collective-permute-start.16) | collective-permute-done | bytes 1048608 | tf_op jit(solution)/shard_map/ppermute | solution.py:185
  180.8 2.9 %fusion.1 = bf16[1,2,128,2048]{3,2,1,0:T(8,128)(2,1)} fusion(bf16[2,128,2048]{2,1,0:T(8,128)(2,1)} %get-tuple-element.252, bf16[2,128,2048]{2,1,0:T(8,128)(2,1)S(1)} %collective-permute-done.16, bf16[2,128,2048]{2,1,0:T(8,128)(2,1)S(1)} %collective-permute-done.13, bf16[2,128,2048]{2,1,0:T(8,128)(2,1)S(1)} %collective-permute-done.6, pred[]{:T(512)S(6)} %eq.29), kind=kLoop, calls=%fused_computation.7 | loop fusion | flops 3670016 | bytes 5242881 | tf_op jit(solution)/shard_map/broadcast_in_dim | solution.py:242
  (31 shorter events, 0.2 us)
Async XLA Ops:
  0.6 17.0 %collective-permute-start.3 = (bf16[2,128,2048]{2,1,0:T(8,128)(2,1)}, bf16[2,128,2048]{2,1,0:T(8,128)(2,1)S(1)}, u32[]{:S(2)}, u32[]{:S(2)}) collective-permute-start(bf16[2,128,2048]{2,1,0:T(8,128)(2,1)} %bitcast.28), channel_id=1, source_target_pairs={{8,128},{16,136},{24,144},{32,152},{40,160},{48,168},{56,176},{64,... | collective-permute-start | bytes 3145736 | tf_op jit(solution)/shard_map/ppermute | solution.py:185
  1.9 18.3 %collective-permute-start = (bf16[2,128,2048]{2,1,0:T(8,128)(2,1)}, bf16[2,128,2048]{2,1,0:T(8,128)(2,1)S(1)}, u32[]{:S(2)}, u32[]{:S(2)}) collective-permute-start(bf16[2,128,2048]{2,1,0:T(8,128)(2,1)} %bitcast.29), channel_id=1, source_target_pairs={{0,136},{8,144},{16,152},{24,160},{32,168},{40,176},{48,184},{56,1... | collective-permute-start | bytes 3145736 | tf_op jit(solution)/shard_map/ppermute | solution.py:185
  17.6 17.2 %copy-start.1 = (bf16[2,128,2048]{2,1,0:T(8,128)(2,1)}, bf16[2,128,2048]{2,1,0:T(8,128)(2,1)S(1)}, u32[]{:S(2)}) copy-start(bf16[2,128,2048]{2,1,0:T(8,128)(2,1)S(1)} %collective-permute-done.3) | copy-start | bytes 3145732
  17.6 15.9 %collective-permute-start.4 = (bf16[2,128,2048]{2,1,0:T(8,128)(2,1)S(1)}, bf16[2,128,2048]{2,1,0:T(8,128)(2,1)S(1)}, u32[]{:S(2)}, u32[]{:S(2)}) collective-permute-start(bf16[2,128,2048]{2,1,0:T(8,128)(2,1)S(1)} %collective-permute-done.3), channel_id=1, source_target_pairs={{136,128},{144,136},{152,144},{160,152},{168,160},{176,168},{184,1... | collective-permute-start | bytes 3145736 | tf_op jit(solution)/shard_map/ppermute | solution.py:185
  18.9 18.5 %collective-permute-start.2 = (bf16[2,128,2048]{2,1,0:T(8,128)(2,1)}, bf16[2,128,2048]{2,1,0:T(8,128)(2,1)}, u32[]{:S(2)}, u32[]{:S(2)}) collective-permute-start(bf16[2,128,2048]{2,1,0:T(8,128)(2,1)} %bitcast.30), channel_id=1, source_target_pairs={{0,128},{8,136},{16,144},{24,152},{32,160},{40,168},{48,176},{56,1... | collective-permute-start | bytes 3145736 | tf_op jit(solution)/shard_map/ppermute | solution.py:185
  20.2 17.2 %collective-permute-start.1 = (bf16[2,128,2048]{2,1,0:T(8,128)(2,1)S(1)}, bf16[2,128,2048]{2,1,0:T(8,128)(2,1)}, u32[]{:S(2)}, u32[]{:S(2)}) collective-permute-start(bf16[2,128,2048]{2,1,0:T(8,128)(2,1)S(1)} %collective-permute-done), channel_id=1, source_target_pairs={{128,136},{136,144},{144,152},{152,160},{160,168},{168,176},{176,1... | collective-permute-start | bytes 3145736 | tf_op jit(solution)/shard_map/ppermute | solution.py:185
  33.5 15.8 %collective-permute-start.5 = (bf16[2,128,2048]{2,1,0:T(8,128)(2,1)S(1)}, bf16[2,128,2048]{2,1,0:T(8,128)(2,1)}, u32[]{:S(2)}, u32[]{:S(2)}) collective-permute-start(bf16[2,128,2048]{2,1,0:T(8,128)(2,1)S(1)} %collective-permute-done.4), channel_id=1, source_target_pairs={{136,128},{144,136},{152,144},{160,152},{168,160},{176,168},{184,1... | collective-permute-start | bytes 3145736 | tf_op jit(solution)/shard_map/ppermute | solution.py:185
  49.3 3.5 %copy-start.2 = (bf16[2,128,2048]{2,1,0:T(8,128)(2,1)}, bf16[2,128,2048]{2,1,0:T(8,128)(2,1)S(1)}, u32[]{:S(2)}) copy-start(bf16[2,128,2048]{2,1,0:T(8,128)(2,1)S(1)} %get-tuple-element.211.refs_1_) | copy-start | bytes 3145732 | tf_op jit(solution)/shard_map/cond
  49.3 3.5 %copy-start.3 = (bf16[2,128,2048]{2,1,0:T(8,128)(2,1)}, bf16[2,128,2048]{2,1,0:T(8,128)(2,1)S(1)}, u32[]{:S(2)}) copy-start(bf16[2,128,2048]{2,1,0:T(8,128)(2,1)S(1)} %get-tuple-element.214.refs_4_) | copy-start | bytes 3145732 | tf_op jit(solution)/shard_map/cond
  83.0 17.2 %collective-permute-start.11 = (bf16[2,128,2048]{2,1,0:T(8,128)(2,1)}, bf16[2,128,2048]{2,1,0:T(8,128)(2,1)}, u32[]{:S(2)}, u32[]{:S(2)}) collective-permute-start(bf16[2,128,2048]{2,1,0:T(8,128)(2,1)} %get-tuple-element.243), channel_id=1, source_target_pairs={{136,128},{144,136},{152,144},{160,152},{168,160},{176,168},{184,1... | collective-permute-start | bytes 3145736 | tf_op jit(solution)/shard_map/ppermute | solution.py:185
  84.3 17.4 %collective-permute-start.12 = (bf16[2,128,2048]{2,1,0:T(8,128)(2,1)}, bf16[2,128,2048]{2,1,0:T(8,128)(2,1)S(1)}, u32[]{:S(2)}, u32[]{:S(2)}) collective-permute-start(bf16[2,128,2048]{2,1,0:T(8,128)(2,1)} %get-tuple-element.244), channel_id=1, source_target_pairs={{128,136},{136,144},{144,152},{152,160},{160,168},{168,176},{176,1... | collective-permute-start | bytes 3145736 | tf_op jit(solution)/shard_map/ppermute | solution.py:185
  89.8 2.1 %collective-permute-start.7 = (f32[2,32]{1,0:T(2,128)S(1)}, f32[2,32]{1,0:T(2,128)S(1)}, u32[]{:S(2)}, u32[]{:S(2)}) collective-permute-start(f32[2,32]{1,0:T(2,128)S(1)} %get-tuple-element.242), channel_id=1, source_target_pairs={{128,0},{129,1},{130,2},{131,3},{132,4},{133,5},{134,6},{135,7},{1... | collective-permute-start | bytes 776 | tf_op jit(solution)/shard_map/ppermute | solution.py:223
  91.9 0.7 collective-permute-start.8
  92.6 0.7 collective-permute-start.9
  93.3 0.7 collective-permute-start.10
  103.1 16.6 %collective-permute-start.15 = (bf16[2,128,2048]{2,1,0:T(8,128)(2,1)}, bf16[2,128,2048]{2,1,0:T(8,128)(2,1)S(1)}, u32[]{:S(2)}, u32[]{:S(2)}) collective-permute-start(bf16[2,128,2048]{2,1,0:T(8,128)(2,1)} %add.106), channel_id=1, source_target_pairs={{128,136},{136,144},{144,152},{152,160},{160,168},{168,176},{176,1... | collective-permute-start | bytes 3145736 | tf_op jit(solution)/shard_map/ppermute | solution.py:185
  107.8 0.7 collective-permute-start.14
  119.7 0.7 collective-permute-start.17
  120.4 0.7 collective-permute-start.18
  121.1 0.7 collective-permute-start.19
  121.8 47.3 %collective-permute-start.20 = (f32[6,2,32]{2,1,0:T(2,128)S(1)}, f32[6,2,32]{2,1,0:T(2,128)S(1)}, u32[]{:S(2)}, u32[]{:S(2)}) collective-permute-start(f32[6,2,32]{2,1,0:T(2,128)S(1)} %pad_maximum_fusion.1), channel_id=1, source_target_pairs={{0,48},{8,56},{16,0},{24,8},{32,16},{40,24},{48,32},{56,40},{64,11... | collective-permute-start | bytes 4616 | tf_op jit(solution)/shard_map/ppermute | solution.py:142
  122.5 50.3 %collective-permute-start.6 = (bf16[2,128,2048]{2,1,0:T(8,128)(2,1)}, bf16[2,128,2048]{2,1,0:T(8,128)(2,1)S(1)}, u32[]{:S(2)}, u32[]{:S(2)}) collective-permute-start(bf16[2,128,2048]{2,1,0:T(8,128)(2,1)} %get-tuple-element.241), channel_id=1, source_target_pairs={{128,0},{136,8},{144,16},{152,24},{160,32},{168,40},{176,48},{184,... | collective-permute-start | bytes 3145736 | tf_op jit(solution)/shard_map/ppermute | solution.py:185
  163.3 9.5 %collective-permute-start.13 = (bf16[2,128,2048]{2,1,0:T(8,128)(2,1)S(1)}, bf16[2,128,2048]{2,1,0:T(8,128)(2,1)S(1)}, u32[]{:S(2)}, u32[]{:S(2)}) collective-permute-start(bf16[2,128,2048]{2,1,0:T(8,128)(2,1)S(1)} %add.103), channel_id=1, source_target_pairs={{136,0},{144,8},{152,16},{160,24},{168,32},{176,40},{184,48},{192,... | collective-permute-start | bytes 3145736 | tf_op jit(solution)/shard_map/ppermute | solution.py:185
  164.1 8.3 %copy-start = (f32[2,32]{1,0:T(2,128)S(1)}, f32[2,32]{1,0:T(2,128)}, u32[]{:S(2)}) copy-start(f32[2,32]{1,0:T(2,128)} %param.6) | copy-start | bytes 772
  164.5 16.4 %collective-permute-start.16 = (bf16[2,128,2048]{2,1,0:T(8,128)(2,1)S(1)}, bf16[2,128,2048]{2,1,0:T(8,128)(2,1)S(1)}, u32[]{:S(2)}, u32[]{:S(2)}) collective-permute-start(bf16[2,128,2048]{2,1,0:T(8,128)(2,1)S(1)} %add.107), channel_id=1, source_target_pairs={{128,8},{136,16},{144,24},{152,32},{160,40},{168,48},{176,56},{184... | collective-permute-start | bytes 3145736 | tf_op jit(solution)/shard_map/ppermute | solution.py:185
  169.3 3.1 %collective-permute-start.21 = (f32[2,32]{1,0:T(2,128)S(1)}, f32[2,32]{1,0:T(2,128)S(1)}, u32[]{:S(2)}, u32[]{:S(2)}) collective-permute-start(f32[2,32]{1,0:T(2,128)S(1)} %fusion.12), channel_id=1, source_target_pairs={{0,128},{1,129},{2,130},{3,131},{4,132},{5,133},{6,134},{7,135},{8... | collective-permute-start | bytes 776 | tf_op jit(solution)/shard_map/ppermute | solution.py:238

commit v10 on v9

--- a/solution.py
+++ b/solution.py
@@ -13,7 +13,6 @@
 REACH_LOW = 2
 REACH_HIGH = 3
 WINDOW = REACH_LOW + REACH_HIGH + 1
-RING = 8
 
 masked_score = -1e30
 
@@ -133,32 +132,21 @@
     return produced, grads, terms
 
 
-def ring_shift(value, steps):
-    count = lax.axis_size("seq")
-    pairs = []
-    for source in range(count):
-        base = source - source % RING
-        pairs.append((source, base + (source - steps) % RING))
-    return lax.ppermute(value, ("phase", "seq"), pairs)
-
-
-def ring_total(value, shard_index):
-    gathered = value[None]
-    gathered = jnp.concatenate([gathered, ring_shift(gathered, 1)], axis=0)
-    gathered = jnp.concatenate([gathered, ring_shift(gathered, 2)], axis=0)
-    while gathered.shape[0] < RING:
-        have = gathered.shape[0]
-        gathered = jnp.concatenate([gathered, ring_shift(gathered, 2)[have - 2 : have]], axis=0)
-    ordered = jnp.roll(gathered, shard_index % RING, axis=0)
+def group_total(value, axis, size, stride, index):
+    count = lax.axis_size(axis)
+    gathered = [value]
+    for shift in range(1, size):
+        pairs = []
+        for source in range(count):
+            position = (source // stride) % size
+            base = source - position * stride
+            pairs.append((source, base + ((position - shift) % size) * stride))
+        gathered.append(lax.ppermute(value, ("phase", axis), pairs))
+    ordered = jnp.roll(jnp.stack(gathered), (index // stride) % size, axis=0)
     total = ordered[0]
-    for index in range(1, RING):
-        total = total + ordered[index]
+    for position in range(1, size):
+        total = total + ordered[position]
     return total
-
-
-def exchange_add(value, axis, stride):
-    count = lax.axis_size(axis)
-    return value + lax.ppermute(value, ("phase", axis), [(i, i ^ stride) for i in range(count)])
 
 
 def segment_of(block_ids, block_sizes, block_total):
@@ -220,18 +208,20 @@
         return a + b
 
     token_total = tok_dev * count * lax.axis_size("dp")
+    dp_index = lax.axis_index("dp")
     summed = lax.ppermute(terms, "phase", [(1, 0)])
     back_minus = across(grads[0], [(dec(s + 1), dec(s)) for s in lower])
     back_plus = across(grads[5], [(dec(s - 1), dec(s)) for s in upper])
     own_sum = across(grads[2], [(dec(s), s) for s in range(count)])
-    summed = exchange_add(exchange_add(exchange_add(summed, "dp", 1), "dp", 2), "dp", 4)
+    summed = group_total(summed, "dp", 4, 1, dp_index)
+    summed = group_total(summed, "dp", 2, 4, dp_index)
     summed, back_minus, back_plus = lax.optimization_barrier((summed, back_minus, back_plus))
     minus_sum = across(added(back_minus, grads[1]), [(dec(s + 1), s) for s in lower])
     back_plus = across(added(back_plus, grads[4]), [(dec(s - 1), dec(s)) for s in upper])
-    summed = exchange_add(summed, "seq", RING)
+    summed = group_total(summed, "seq", 4, 1, shard_index)
     summed, back_plus = lax.optimization_barrier((summed, back_plus))
     plus_sum = across(added(back_plus, grads[3]), [(dec(s - 1), s) for s in upper])
-    summed = ring_total(summed, shard_index)
+    summed = group_total(summed, "seq", 4, 4, shard_index)
     returned = (
         own_sum.astype(jnp.float32) + minus_sum.astype(jnp.float32) + plus_sum.astype(jnp.float32)
     ).astype(jnp.bfloat16)

time: 184 us -> 179 us (0.973)
  starting transfers between devices: 75 us -> 59.6 us
  waiting for transfers between devices: 64.4 us -> 71.7 us
  other arithmetic: 9.65 us -> 12.9 us
    ppermute x1, waiting for transfers between devices: 1.72 us -> 29.9 us  [local_body(): shared = lax.ppermute(summed, 'phase', [(0, 1)])]
    ppermute x12, waiting for transfers between devices: 61.9 us -> 41 us  [across(): return lax.ppermute(value, ('phase', 'seq'), pairs)]
    ppermute x12, starting transfers between devices: 67.1 us -> 50.4 us  [across(): return lax.ppermute(value, ('phase', 'seq'), pairs)]
    add x3, other arithmetic: 3.36 us -> 5.82 us  [added(): return a + b]
    ppermute x8 -> x10, starting transfers between devices: 5.27 us -> 6.59 us  [group_total(): gathered.append(lax.ppermute(value, ('phase', axis), pairs))]
  transfers between devices with their start and end apart: 22 -> 24, of which waited for: 9 -> 7; matrix products, arithmetic and copies ran while one was open for 3% -> 4% of each run, Pallas kernels for 0% -> 0%
where the time goes in v10:
time: 179 us
  waiting for transfers between devices  71.7 us (40%)
  starting transfers between devices  59.6 us (33%)
  Pallas kernels  29 us (16%)
  other arithmetic  12.9 us (7%)
  local copies, waits for them, and re-layouts  3.18 us (2%)
    ppermute x12, starting transfers between devices, across(): return lax.ppermute(value, ('phase', 'seq'), pairs)  50.4 us
    ppermute x12, waiting for transfers between devices, across(): return lax.ppermute(value, ('phase', 'seq'), pairs)  41 us
    ppermute x1, waiting for transfers between devices, local_body(): shared = lax.ppermute(summed, 'phase', [(0, 1)])  29.9 us
    pallas_call x1, Pallas kernels, attention_block(): pl.pallas_call(attention_kernel, grid_spec=grid_spec, out_shape=[jax.Shap...  29 us
    ppermute x10, starting transfers between devices, group_total(): gathered.append(lax.ppermute(value, ('phase', axis), pairs))  6.59 us
    add x3, other arithmetic, added(): return a + b  5.82 us
    broadcast_in_dim x1, other arithmetic, local_body(): result = jnp.where(phase_index == 0, returned, produced)[None]  3.61 us
  transfers between devices with their start and end apart: 24, of which 7 were waited for; matrix products, arithmetic and copies ran while one was open for 4% of the time, Pallas kernels for 0%

profile of v10, /device:TPU:1, one launch (start us, length us, event | category | flops | bytes accessed | tf_op | source)
XLA Modules:
  0.0 178.5 jit_solution(17557111908523493142)
XLA Ops:
  0.6 1.3 collective-permute-start.3
  1.9 0.7 collective-permute-start
  2.7 15.0 %collective-permute-done.3 = bf16[2,128,2048]{2,1,0:T(8,128)(2,1)S(1)} collective-permute-done((bf16[2,128,2048]{2,1,0:T(8,128)(2,1)}, bf16[2,128,2048]{2,1,0:T(8,128)(2,1)S(1)}, u32[]{:S(2)}, u32[]{:S(2)}) %collective-permute-start.3) | collective-permute-done | bytes 1048608 | tf_op jit(solution)/shard_map/ppermute | solution.py:173
  17.6 1.3 collective-permute-start.4
  18.9 1.3 collective-permute-start.2
  20.2 0.0 collective-permute-done
  20.2 5.3 %collective-permute-start.1 = (bf16[2,128,2048]{2,1,0:T(8,128)(2,1)S(1)}, bf16[2,128,2048]{2,1,0:T(8,128)(2,1)}, u32[]{:S(2)}, u32[]{:S(2)}) collective-permute-start(bf16[2,128,2048]{2,1,0:T(8,128)(2,1)S(1)} %collective-permute-done), channel_id=1, source_target_pairs={{128,136},{136,144},{144,152},{152,160},{160,168},{168,176},{176,1... | collective-permute-start | bytes 3145736 | tf_op jit(solution)/shard_map/ppermute | solution.py:173
  25.5 8.0 %collective-permute-done.4 = bf16[2,128,2048]{2,1,0:T(8,128)(2,1)S(1)} collective-permute-done((bf16[2,128,2048]{2,1,0:T(8,128)(2,1)S(1)}, bf16[2,128,2048]{2,1,0:T(8,128)(2,1)S(1)}, u32[]{:S(2)}, u32[]{:S(2)}) %collective-permute-start.4) | collective-permute-done | bytes 1048608 | tf_op jit(solution)/shard_map/ppermute | solution.py:173
  33.5 1.3 collective-permute-start.5
  34.8 0.8 slice_bitcast_fusion.1
  35.6 0.2 reduce-window_1_clone.1
  35.7 0.2 reduce-window.8
  35.9 0.7 compare_convert_fusion.2
  36.6 0.7 bitcast_subtract_fusion
  37.3 0.1 compare_convert_fusion.1
  37.4 0.0 collective-permute-done.2
  37.4 0.0 collective-permute-done.1
  37.4 11.9 %collective-permute-done.5 = bf16[2,128,2048]{2,1,0:T(8,128)(2,1)} collective-permute-done((bf16[2,128,2048]{2,1,0:T(8,128)(2,1)S(1)}, bf16[2,128,2048]{2,1,0:T(8,128)(2,1)}, u32[]{:S(2)}, u32[]{:S(2)}) %collective-permute-start.5) | collective-permute-done | bytes 1048608 | tf_op jit(solution)/shard_map/ppermute | solution.py:173
  49.3 33.5 %conditional.1 = (bf16[2,128,2048]{2,1,0:T(8,128)(2,1)}, bf16[2,128,2048]{2,1,0:T(8,128)(2,1)}, bf16[2,128,2048]{2,1,0:T(8,128)(2,1)S(1)}, bf16[2,128,2048]{2,1,...) conditional(s32[]{:T(128)} %convert_element_type.45, () %tuple.39, ...), branch_computations={%region_2.3_spmd, %region_3.6_spmd} | conditional | flops 3221225472 | bytes 23072892 | solution.py:203
  49.3 0.8 reduce_sum.21
  50.6 0.6 dynamic_slice.18
  51.8 0.1 reduce_sum.22
  51.9 0.1 compare_convert_fusion
  52.0 0.7 broadcast_in_dim.21
  52.6 29.0 %branch_1_fun.5 = (bf16[2,128,2048]{2,1,0:T(8,128)(2,1)}, bf16[2,128,2048]{2,1,0:T(8,128)(2,1)}, bf16[2,128,2048]{2,1,0:T(8,128)(2,1)S(1)}, bf16[2,128,2048]{2,1...) custom-call(s32[1]{0:T(128)} %bitcast.1.start_ref, ...), custom_call_target="tpu_custom_call" | custom-call | flops 3221225472 | bytes 14680064 | tf_op jit(solution)/shard_map/cond/branch_1_fun/pallas_call | solution.py:121
  81.6 1.0 slice_reduce_fusion.1
  82.6 0.1 squeeze.24
  82.7 0.1 squeeze.23
  82.8 1.3 collective-permute-start.12
  84.1 6.4 %collective-permute-start.13 = (bf16[2,128,2048]{2,1,0:T(8,128)(2,1)}, bf16[2,128,2048]{2,1,0:T(8,128)(2,1)}, u32[]{:S(2)}, u32[]{:S(2)}) collective-permute-start(bf16[2,128,2048]{2,1,0:T(8,128)(2,1)} %get-tuple-element.251), channel_id=1, source_target_pairs={{128,136},{136,144},{144,152},{152,160},{160,168},{168,176},{176,1... | collective-permute-start | bytes 3145736 | tf_op jit(solution)/shard_map/ppermute | solution.py:173
  90.5 1.3 collective-permute-start.7
  91.8 0.8 collective-permute-done.7
  92.6 0.6 collective-permute-start.8
  93.2 0.7 collective-permute-start.9
  93.9 0.7 collective-permute-start.10
  94.6 0.0 collective-permute-done.8
  94.6 0.0 collective-permute-done.9
  94.6 0.0 collective-permute-done.10
  94.7 0.7 collective-permute-start.11
  95.4 0.0 collective-permute-done.11
  95.4 4.6 %collective-permute-done.12 = bf16[2,128,2048]{2,1,0:T(8,128)(2,1)} collective-permute-done((bf16[2,128,2048]{2,1,0:T(8,128)(2,1)}, bf16[2,128,2048]{2,1,0:T(8,128)(2,1)}, u32[]{:S(2)}, u32[]{:S(2)}) %collective-permute-start.12) | collective-permute-done | bytes 1048608 | tf_op jit(solution)/shard_map/ppermute | solution.py:173
  100.1 1.5 collective-permute-done.13
  101.5 2.6 %add.149 = bf16[2,128,2048]{2,1,0:T(8,128)(2,1)} add(bf16[2,128,2048]{2,1,0:T(8,128)(2,1)} %collective-permute-done.13, bf16[2,128,2048]{2,1,0:T(8,128)(2,1)S(1)} %get-tuple-element.256) | non-fusion elementwise | flops 524288 | bytes 3145728 | tf_op jit(solution)/shard_map/add | solution.py:208
  104.1 5.6 %collective-permute-start.18 = (bf16[2,128,2048]{2,1,0:T(8,128)(2,1)}, bf16[2,128,2048]{2,1,0:T(8,128)(2,1)}, u32[]{:S(2)}, u32[]{:S(2)}) collective-permute-start(bf16[2,128,2048]{2,1,0:T(8,128)(2,1)} %add.149), channel_id=1, source_target_pairs={{128,136},{136,144},{144,152},{152,160},{160,168},{168,176},{176,1... | collective-permute-start | bytes 3145736 | tf_op jit(solution)/shard_map/ppermute | solution.py:173
  109.7 10.7 %collective-permute-start.6 = (bf16[2,128,2048]{2,1,0:T(8,128)(2,1)}, bf16[2,128,2048]{2,1,0:T(8,128)(2,1)}, u32[]{:S(2)}, u32[]{:S(2)}) collective-permute-start(bf16[2,128,2048]{2,1,0:T(8,128)(2,1)} %get-tuple-element.248), channel_id=1, source_target_pairs={{128,0},{136,8},{144,16},{152,24},{160,32},{168,40},{176,48},{184,... | collective-permute-start | bytes 3145736 | tf_op jit(solution)/shard_map/ppermute | solution.py:173
  120.4 0.6 collective-permute-start.15
  121.0 0.7 collective-permute-start.16
  121.7 0.7 collective-permute-start.17
  122.4 1.6 add.142
  124.0 1.6 collective-permute-start.14
  125.7 0.0 collective-permute-done.18
  125.7 0.0 copy-start
  125.7 1.6 add.150
  127.3 13.7 %collective-permute-start.19 = (bf16[2,128,2048]{2,1,0:T(8,128)(2,1)S(1)}, bf16[2,128,2048]{2,1,0:T(8,128)(2,1)S(1)}, u32[]{:S(2)}, u32[]{:S(2)}) collective-permute-start(bf16[2,128,2048]{2,1,0:T(8,128)(2,1)S(1)} %add.150), channel_id=1, source_target_pairs={{128,8},{136,16},{144,24},{152,32},{160,40},{168,48},{176,56},{184... | collective-permute-start | bytes 3145736 | tf_op jit(solution)/shard_map/ppermute | solution.py:173
  141.1 0.7 collective-permute-start.20
  141.8 0.7 collective-permute-start.21
  142.4 0.0 collective-permute-done.20
  142.4 0.7 collective-permute-start.22
  143.1 0.0 collective-permute-done.21
  143.1 0.0 collective-permute-done.22
  143.2 1.3 collective-permute-start.23
  144.5 29.9 %collective-permute-done.23 = f32[2,32]{1,0:T(2,128)S(1)} collective-permute-done((f32[2,32]{1,0:T(2,128)S(1)}, f32[2,32]{1,0:T(2,128)S(1)}, u32[]{:S(2)}, u32[]{:S(2)}) %collective-permute-start.23) | collective-permute-done | bytes 288 | tf_op jit(solution)/shard_map/ppermute | solution.py:228
  174.4 0.5 fusion.28
  174.9 3.6 %fusion.1 = bf16[1,2,128,2048]{3,2,1,0:T(8,128)(2,1)} fusion(bf16[2,128,2048]{2,1,0:T(8,128)(2,1)} %get-tuple-element.259, bf16[2,128,2048]{2,1,0:T(8,128)(2,1)S(1)} %collective-permute-done.19, bf16[2,128,2048]{2,1,0:T(8,128)(2,1)} %collective-permute-done.14, bf16[2,128,2048]{2,1,0:T(8,128)(2,1)} %collective-permute-done.6, pred[]{:T(512)S(6)} %eq.33), kind=kLoop, calls=%fused_computation.7 | loop fusion | flops 3670016 | bytes 5242881 | tf_op jit(solution)/shard_map/broadcast_in_dim | solution.py:232
  (26 shorter events, 0.2 us)
Async XLA Ops:
  0.6 17.0 %collective-permute-start.3 = (bf16[2,128,2048]{2,1,0:T(8,128)(2,1)}, bf16[2,128,2048]{2,1,0:T(8,128)(2,1)S(1)}, u32[]{:S(2)}, u32[]{:S(2)}) collective-permute-start(bf16[2,128,2048]{2,1,0:T(8,128)(2,1)} %bitcast.53), channel_id=1, source_target_pairs={{8,128},{16,136},{24,144},{32,152},{40,160},{48,168},{56,176},{64,... | collective-permute-start | bytes 3145736 | tf_op jit(solution)/shard_map/ppermute | solution.py:173
  1.9 18.3 %collective-permute-start = (bf16[2,128,2048]{2,1,0:T(8,128)(2,1)}, bf16[2,128,2048]{2,1,0:T(8,128)(2,1)S(1)}, u32[]{:S(2)}, u32[]{:S(2)}) collective-permute-start(bf16[2,128,2048]{2,1,0:T(8,128)(2,1)} %bitcast.54), channel_id=1, source_target_pairs={{0,136},{8,144},{16,152},{24,160},{32,168},{40,176},{48,184},{56,1... | collective-permute-start | bytes 3145736 | tf_op jit(solution)/shard_map/ppermute | solution.py:173
  17.6 17.2 %copy-start.1 = (bf16[2,128,2048]{2,1,0:T(8,128)(2,1)}, bf16[2,128,2048]{2,1,0:T(8,128)(2,1)S(1)}, u32[]{:S(2)}) copy-start(bf16[2,128,2048]{2,1,0:T(8,128)(2,1)S(1)} %collective-permute-done.3) | copy-start | bytes 3145732
  17.6 15.9 %collective-permute-start.4 = (bf16[2,128,2048]{2,1,0:T(8,128)(2,1)S(1)}, bf16[2,128,2048]{2,1,0:T(8,128)(2,1)S(1)}, u32[]{:S(2)}, u32[]{:S(2)}) collective-permute-start(bf16[2,128,2048]{2,1,0:T(8,128)(2,1)S(1)} %collective-permute-done.3), channel_id=1, source_target_pairs={{136,128},{144,136},{152,144},{160,152},{168,160},{176,168},{184,1... | collective-permute-start | bytes 3145736 | tf_op jit(solution)/shard_map/ppermute | solution.py:173
  18.9 18.5 %collective-permute-start.2 = (bf16[2,128,2048]{2,1,0:T(8,128)(2,1)}, bf16[2,128,2048]{2,1,0:T(8,128)(2,1)}, u32[]{:S(2)}, u32[]{:S(2)}) collective-permute-start(bf16[2,128,2048]{2,1,0:T(8,128)(2,1)} %bitcast.55), channel_id=1, source_target_pairs={{0,128},{8,136},{16,144},{24,152},{32,160},{40,168},{48,176},{56,1... | collective-permute-start | bytes 3145736 | tf_op jit(solution)/shard_map/ppermute | solution.py:173
  20.2 17.2 %collective-permute-start.1 = (bf16[2,128,2048]{2,1,0:T(8,128)(2,1)S(1)}, bf16[2,128,2048]{2,1,0:T(8,128)(2,1)}, u32[]{:S(2)}, u32[]{:S(2)}) collective-permute-start(bf16[2,128,2048]{2,1,0:T(8,128)(2,1)S(1)} %collective-permute-done), channel_id=1, source_target_pairs={{128,136},{136,144},{144,152},{152,160},{160,168},{168,176},{176,1... | collective-permute-start | bytes 3145736 | tf_op jit(solution)/shard_map/ppermute | solution.py:173
  33.5 15.8 %collective-permute-start.5 = (bf16[2,128,2048]{2,1,0:T(8,128)(2,1)S(1)}, bf16[2,128,2048]{2,1,0:T(8,128)(2,1)}, u32[]{:S(2)}, u32[]{:S(2)}) collective-permute-start(bf16[2,128,2048]{2,1,0:T(8,128)(2,1)S(1)} %collective-permute-done.4), channel_id=1, source_target_pairs={{136,128},{144,136},{152,144},{160,152},{168,160},{176,168},{184,1... | collective-permute-start | bytes 3145736 | tf_op jit(solution)/shard_map/ppermute | solution.py:173
  49.3 3.3 %copy-start.2 = (bf16[2,128,2048]{2,1,0:T(8,128)(2,1)}, bf16[2,128,2048]{2,1,0:T(8,128)(2,1)S(1)}, u32[]{:S(2)}) copy-start(bf16[2,128,2048]{2,1,0:T(8,128)(2,1)S(1)} %get-tuple-element.218.refs_1_) | copy-start | bytes 3145732 | tf_op jit(solution)/shard_map/cond
  49.3 3.3 %copy-start.3 = (bf16[2,128,2048]{2,1,0:T(8,128)(2,1)}, bf16[2,128,2048]{2,1,0:T(8,128)(2,1)S(1)}, u32[]{:S(2)}) copy-start(bf16[2,128,2048]{2,1,0:T(8,128)(2,1)S(1)} %get-tuple-element.221.refs_4_) | copy-start | bytes 3145732 | tf_op jit(solution)/shard_map/cond
  82.8 17.3 %collective-permute-start.12 = (bf16[2,128,2048]{2,1,0:T(8,128)(2,1)}, bf16[2,128,2048]{2,1,0:T(8,128)(2,1)}, u32[]{:S(2)}, u32[]{:S(2)}) collective-permute-start(bf16[2,128,2048]{2,1,0:T(8,128)(2,1)} %get-tuple-element.250), channel_id=1, source_target_pairs={{136,128},{144,136},{152,144},{160,152},{168,160},{176,168},{184,1... | collective-permute-start | bytes 3145736 | tf_op jit(solution)/shard_map/ppermute | solution.py:173
  84.1 17.4 %collective-permute-start.13 = (bf16[2,128,2048]{2,1,0:T(8,128)(2,1)}, bf16[2,128,2048]{2,1,0:T(8,128)(2,1)}, u32[]{:S(2)}, u32[]{:S(2)}) collective-permute-start(bf16[2,128,2048]{2,1,0:T(8,128)(2,1)} %get-tuple-element.251), channel_id=1, source_target_pairs={{128,136},{136,144},{144,152},{152,160},{160,168},{168,176},{176,1... | collective-permute-start | bytes 3145736 | tf_op jit(solution)/shard_map/ppermute | solution.py:173
  90.5 2.1 %collective-permute-start.7 = (f32[2,32]{1,0:T(2,128)S(1)}, f32[2,32]{1,0:T(2,128)S(1)}, u32[]{:S(2)}, u32[]{:S(2)}) collective-permute-start(f32[2,32]{1,0:T(2,128)S(1)} %get-tuple-element.249), channel_id=1, source_target_pairs={{128,0},{129,1},{130,2},{131,3},{132,4},{133,5},{134,6},{135,7},{1... | collective-permute-start | bytes 776 | tf_op jit(solution)/shard_map/ppermute | solution.py:212
  92.6 2.0 %collective-permute-start.8 = (f32[2,32]{1,0:T(2,128)S(1)}, f32[2,32]{1,0:T(2,128)S(1)}, u32[]{:S(2)}, u32[]{:S(2)}) collective-permute-start(f32[2,32]{1,0:T(2,128)S(1)} %collective-permute-done.7), channel_id=1, source_target_pairs={{0,3},{1,0},{2,1},{3,2},{4,7},{5,4},{6,5},{7,6},{8,11},{9,8},{10,9... | collective-permute-start | bytes 776 | tf_op jit(solution)/shard_map/ppermute | solution.py:144
  93.2 1.4 collective-permute-start.9
  93.9 0.7 collective-permute-start.10
  94.7 0.7 collective-permute-start.11
  104.1 21.6 %collective-permute-start.18 = (bf16[2,128,2048]{2,1,0:T(8,128)(2,1)}, bf16[2,128,2048]{2,1,0:T(8,128)(2,1)}, u32[]{:S(2)}, u32[]{:S(2)}) collective-permute-start(bf16[2,128,2048]{2,1,0:T(8,128)(2,1)} %add.149), channel_id=1, source_target_pairs={{128,136},{136,144},{144,152},{152,160},{160,168},{168,176},{176,1... | collective-permute-start | bytes 3145736 | tf_op jit(solution)/shard_map/ppermute | solution.py:173
  109.7 65.2 %collective-permute-start.6 = (bf16[2,128,2048]{2,1,0:T(8,128)(2,1)}, bf16[2,128,2048]{2,1,0:T(8,128)(2,1)}, u32[]{:S(2)}, u32[]{:S(2)}) collective-permute-start(bf16[2,128,2048]{2,1,0:T(8,128)(2,1)} %get-tuple-element.248), channel_id=1, source_target_pairs={{128,0},{136,8},{144,16},{152,24},{160,32},{168,40},{176,48},{184,... | collective-permute-start | bytes 3145736 | tf_op jit(solution)/shard_map/ppermute | solution.py:173
  120.4 3.6 %collective-permute-start.15 = (f32[2,32]{1,0:T(2,128)S(1)}, f32[2,32]{1,0:T(2,128)S(1)}, u32[]{:S(2)}, u32[]{:S(2)}) collective-permute-start(f32[2,32]{1,0:T(2,128)S(1)} %fusion.27), channel_id=1, source_target_pairs={{0,24},{8,0},{16,8},{24,16},{32,56},{40,32},{48,40},{56,48},{64,88... | collective-permute-start | bytes 776 | tf_op jit(solution)/shard_map/ppermute | solution.py:144
  121.0 4.6 %collective-permute-start.16 = (f32[2,32]{1,0:T(2,128)S(1)}, f32[2,32]{1,0:T(2,128)S(1)}, u32[]{:S(2)}, u32[]{:S(2)}) collective-permute-start(f32[2,32]{1,0:T(2,128)S(1)} %fusion.27), channel_id=1, source_target_pairs={{0,16},{8,24},{16,0},{24,8},{32,48},{40,56},{48,32},{56,40},{64,80... | collective-permute-start | bytes 776 | tf_op jit(solution)/shard_map/ppermute | solution.py:144
  121.7 4.0 %collective-permute-start.17 = (f32[2,32]{1,0:T(2,128)S(1)}, f32[2,32]{1,0:T(2,128)S(1)}, u32[]{:S(2)}, u32[]{:S(2)}) collective-permute-start(f32[2,32]{1,0:T(2,128)S(1)} %fusion.27), channel_id=1, source_target_pairs={{0,8},{8,16},{16,24},{24,0},{32,40},{40,48},{48,56},{56,32},{64,72... | collective-permute-start | bytes 776 | tf_op jit(solution)/shard_map/ppermute | solution.py:144
  124.0 50.9 %collective-permute-start.14 = (bf16[2,128,2048]{2,1,0:T(8,128)(2,1)S(1)}, bf16[2,128,2048]{2,1,0:T(8,128)(2,1)}, u32[]{:S(2)}, u32[]{:S(2)}) collective-permute-start(bf16[2,128,2048]{2,1,0:T(8,128)(2,1)S(1)} %add.142), channel_id=1, source_target_pairs={{136,0},{144,8},{152,16},{160,24},{168,32},{176,40},{184,48},{192,... | collective-permute-start | bytes 3145736 | tf_op jit(solution)/shard_map/ppermute | solution.py:173
  125.7 48.7 %copy-start = (f32[2,32]{1,0:T(2,128)S(1)}, f32[2,32]{1,0:T(2,128)}, u32[]{:S(2)}) copy-start(f32[2,32]{1,0:T(2,128)} %param.8) | copy-start | bytes 772
  127.3 47.6 %collective-permute-start.19 = (bf16[2,128,2048]{2,1,0:T(8,128)(2,1)S(1)}, bf16[2,128,2048]{2,1,0:T(8,128)(2,1)S(1)}, u32[]{:S(2)}, u32[]{:S(2)}) collective-permute-start(bf16[2,128,2048]{2,1,0:T(8,128)(2,1)S(1)} %add.150), channel_id=1, source_target_pairs={{128,8},{136,16},{144,24},{152,32},{160,40},{168,48},{176,56},{184... | collective-permute-start | bytes 3145736 | tf_op jit(solution)/shard_map/ppermute | solution.py:173
  141.1 1.3 collective-permute-start.20
  141.8 1.4 collective-permute-start.21
  142.4 0.7 collective-permute-start.22
  143.2 31.2 %collective-permute-start.23 = (f32[2,32]{1,0:T(2,128)S(1)}, f32[2,32]{1,0:T(2,128)S(1)}, u32[]{:S(2)}, u32[]{:S(2)}) collective-permute-start(f32[2,32]{1,0:T(2,128)S(1)} %fusion.30), channel_id=1, source_target_pairs={{0,128},{1,129},{2,130},{3,131},{4,132},{5,133},{6,134},{7,135},{8... | collective-permute-start | bytes 776 | tf_op jit(solution)/shard_map/ppermute | solution.py:228

commit v11 on v10

--- a/solution.py
+++ b/solution.py
@@ -13,6 +13,7 @@
 REACH_LOW = 2
 REACH_HIGH = 3
 WINDOW = REACH_LOW + REACH_HIGH + 1
+RING = 8
 
 masked_score = -1e30
 
@@ -141,12 +142,17 @@
             position = (source // stride) % size
             base = source - position * stride
             pairs.append((source, base + ((position - shift) % size) * stride))
-        gathered.append(lax.ppermute(value, ("phase", axis), pairs))
+        gathered.append(lax.ppermute(value, axis, pairs))
     ordered = jnp.roll(jnp.stack(gathered), (index // stride) % size, axis=0)
     total = ordered[0]
     for position in range(1, size):
         total = total + ordered[position]
     return total
+
+
+def exchange_add(value, axis, stride):
+    count = lax.axis_size(axis)
+    return value + lax.ppermute(value, axis, [(i, i ^ stride) for i in range(count)])
 
 
 def segment_of(block_ids, block_sizes, block_total):
@@ -208,25 +214,22 @@
         return a + b
 
     token_total = tok_dev * count * lax.axis_size("dp")
-    dp_index = lax.axis_index("dp")
-    summed = lax.ppermute(terms, "phase", [(1, 0)])
+    summed = exchange_add(terms, "phase", 1)
     back_minus = across(grads[0], [(dec(s + 1), dec(s)) for s in lower])
     back_plus = across(grads[5], [(dec(s - 1), dec(s)) for s in upper])
     own_sum = across(grads[2], [(dec(s), s) for s in range(count)])
-    summed = group_total(summed, "dp", 4, 1, dp_index)
-    summed = group_total(summed, "dp", 2, 4, dp_index)
+    summed = group_total(summed, "dp", lax.axis_size("dp"), 1, lax.axis_index("dp"))
     summed, back_minus, back_plus = lax.optimization_barrier((summed, back_minus, back_plus))
     minus_sum = across(added(back_minus, grads[1]), [(dec(s + 1), s) for s in lower])
     back_plus = across(added(back_plus, grads[4]), [(dec(s - 1), dec(s)) for s in upper])
-    summed = group_total(summed, "seq", 4, 1, shard_index)
+    summed = exchange_add(summed, "seq", RING)
     summed, back_plus = lax.optimization_barrier((summed, back_plus))
     plus_sum = across(added(back_plus, grads[3]), [(dec(s - 1), s) for s in upper])
-    summed = group_total(summed, "seq", 4, 4, shard_index)
+    summed = group_total(summed, "seq", RING, 1, shard_index)
     returned = (
         own_sum.astype(jnp.float32) + minus_sum.astype(jnp.float32) + plus_sum.astype(jnp.float32)
     ).astype(jnp.bfloat16)
-    shared = lax.ppermute(summed, "phase", [(0, 1)])
-    chosen = jnp.where(phase_index == 0, summed[0], shared[1])
+    chosen = lax.dynamic_index_in_dim(summed, phase_index, 0, keepdims=False)
     scale = jnp.where(phase_index == 0, head_gains[1], 1.0) * math.sqrt(token_total)
     gain_total = chosen / scale
     result = jnp.where(phase_index == 0, returned, produced)[None]

time: 179 us -> 173 us (0.966)
  waiting for transfers between devices: 71.7 us -> 56.6 us
  starting transfers between devices: 59.6 us -> 72 us
  other arithmetic: 12.9 us -> 9.66 us
    ppermute x12 -> x16, starting transfers between devices: 9.16 us -> 46 us  [the longest x14 27.2 us: group_total(): gathered.append(lax.ppermute(value, axis, pairs))]
    ppermute x12, starting transfers between devices: 50.4 us -> 26 us  [across(): return lax.ppermute(value, ('phase', 'seq'), pairs)]
    ppermute x12 -> x16, waiting for transfers between devices: 30.7 us -> 8.28 us  [the longest x14 7.14 us: group_total(): gathered.append(lax.ppermute(value, axis, pairs))]
    ppermute x12, waiting for transfers between devices: 41 us -> 48.3 us  [across(): return lax.ppermute(value, ('phase', 'seq'), pairs)]
    add x3, other arithmetic: 5.82 us -> 3.36 us  [added(): return a + b]
  transfers between devices with their start and end apart: 24 -> 28, of which waited for: 7 -> 12; matrix products, arithmetic and copies ran while one was open for 4% -> 3% of each run, Pallas kernels for 0% -> 0%
where the time goes in v11:
time: 173 us
  starting transfers between devices  72 us (42%)
  waiting for transfers between devices  56.6 us (33%)
  Pallas kernels  29 us (17%)
  other arithmetic  9.66 us (6%)
  local copies, waits for them, and re-layouts  3.27 us (2%)
    ppermute x12, waiting for transfers between devices, across(): return lax.ppermute(value, ('phase', 'seq'), pairs)  48.3 us
    pallas_call x1, Pallas kernels, attention_block(): pl.pallas_call(attention_kernel, grid_spec=grid_spec, out_shape=[jax.Shap...  29 us
    ppermute x14, starting transfers between devices, group_total(): gathered.append(lax.ppermute(value, axis, pairs))  27.2 us
    ppermute x12, starting transfers between devices, across(): return lax.ppermute(value, ('phase', 'seq'), pairs)  26 us
    ppermute x2, starting transfers between devices, exchange_add(): lax.ppermute(value, axis, [(i, i ^ stride) for i in range(count)])  18.8 us
    ppermute x14, waiting for transfers between devices, group_total(): gathered.append(lax.ppermute(value, axis, pairs))  7.14 us
  transfers between devices with their start and end apart: 28, of which 12 were waited for; matrix products, arithmetic and copies ran while one was open for 3% of the time, Pallas kernels for 0%

profile of v11, /device:TPU:1, one launch (start us, length us, event | category | flops | bytes accessed | tf_op | source)
XLA Modules:
  0.0 172.6 jit_solution(26625256787309930)
XLA Ops:
  0.6 1.3 collective-permute-start.3
  1.9 0.7 collective-permute-start
  2.7 15.0 %collective-permute-done.3 = bf16[2,128,2048]{2,1,0:T(8,128)(2,1)S(1)} collective-permute-done((bf16[2,128,2048]{2,1,0:T(8,128)(2,1)}, bf16[2,128,2048]{2,1,0:T(8,128)(2,1)S(1)}, u32[]{:S(2)}, u32[]{:S(2)}) %collective-permute-start.3) | collective-permute-done | bytes 1048608 | tf_op jit(solution)/shard_map/ppermute | solution.py:179
  17.6 1.3 collective-permute-start.4
  18.9 1.3 collective-permute-start.2
  20.2 5.3 %collective-permute-start.1 = (bf16[2,128,2048]{2,1,0:T(8,128)(2,1)S(1)}, bf16[2,128,2048]{2,1,0:T(8,128)(2,1)}, u32[]{:S(2)}, u32[]{:S(2)}) collective-permute-start(bf16[2,128,2048]{2,1,0:T(8,128)(2,1)S(1)} %collective-permute-done), channel_id=1, source_target_pairs={{128,136},{136,144},{144,152},{152,160},{160,168},{168,176},{176,1... | collective-permute-start | bytes 3145736 | tf_op jit(solution)/shard_map/ppermute | solution.py:179
  25.6 7.9 %collective-permute-done.4 = bf16[2,128,2048]{2,1,0:T(8,128)(2,1)S(1)} collective-permute-done((bf16[2,128,2048]{2,1,0:T(8,128)(2,1)S(1)}, bf16[2,128,2048]{2,1,0:T(8,128)(2,1)S(1)}, u32[]{:S(2)}, u32[]{:S(2)}) %collective-permute-start.4) | collective-permute-done | bytes 1048608 | tf_op jit(solution)/shard_map/ppermute | solution.py:179
  33.5 1.3 collective-permute-start.5
  34.8 0.8 slice_bitcast_fusion.1
  35.6 0.2 reduce-window.8
  35.8 0.2 reduce-window_1_clone.1
  35.9 0.7 bitcast_subtract_fusion
  36.6 0.7 compare_convert_fusion.2
  37.3 0.1 compare_convert_fusion.1
  37.4 0.0 collective-permute-done.2
  37.4 0.0 collective-permute-done.1
  37.4 11.9 %collective-permute-done.5 = bf16[2,128,2048]{2,1,0:T(8,128)(2,1)} collective-permute-done((bf16[2,128,2048]{2,1,0:T(8,128)(2,1)S(1)}, bf16[2,128,2048]{2,1,0:T(8,128)(2,1)}, u32[]{:S(2)}, u32[]{:S(2)}) %collective-permute-start.5) | collective-permute-done | bytes 1048608 | tf_op jit(solution)/shard_map/ppermute | solution.py:179
  49.3 33.5 %conditional.1 = (bf16[2,128,2048]{2,1,0:T(8,128)(2,1)}, bf16[2,128,2048]{2,1,0:T(8,128)(2,1)}, bf16[2,128,2048]{2,1,0:T(8,128)(2,1)S(1)}, bf16[2,128,2048]{2,1,...) conditional(s32[]{:T(128)} %convert_element_type.45, () %tuple.46, ...), branch_computations={%region_2.3_spmd, %region_3.6_spmd} | conditional | flops 3221225472 | bytes 23072892 | solution.py:209
  49.3 0.8 reduce_sum.21
  50.7 0.6 dynamic_slice.18
  51.8 0.1 reduce_sum.22
  51.9 0.1 compare_convert_fusion
  52.0 0.6 broadcast_in_dim.21
  52.6 29.0 %branch_1_fun.5 = (bf16[2,128,2048]{2,1,0:T(8,128)(2,1)}, bf16[2,128,2048]{2,1,0:T(8,128)(2,1)}, bf16[2,128,2048]{2,1,0:T(8,128)(2,1)S(1)}, bf16[2,128,2048]{2,1...) custom-call(s32[1]{0:T(128)} %bitcast.1.start_ref, ...), custom_call_target="tpu_custom_call" | custom-call | flops 3221225472 | bytes 14680064 | tf_op jit(solution)/shard_map/cond/branch_1_fun/pallas_call | solution.py:122
  81.6 1.0 slice_reduce_fusion.1
  82.6 0.1 squeeze.53
  82.7 0.1 squeeze.54
  82.8 0.1 collective-permute-start.7
  82.9 1.1 collective-permute-done.7
  84.1 3.5 %collective-permute-start.8 = (f32[2,32]{1,0:T(2,128)S(1)}, f32[2,32]{1,0:T(2,128)S(1)}, u32[]{:S(2)}, u32[]{:S(2)}) collective-permute-start(f32[2,32]{1,0:T(2,128)S(1)} %get-tuple-element.264), channel_id=1, source_target_pairs={{0,7},{1,0},{2,1},{3,2},{4,3},{5,4},{6,5},{7,6},{8,15},{9,8},{10,9... | collective-permute-start | bytes 776 | tf_op jit(solution)/shard_map/ppermute | solution.py:145
  87.6 1.3 collective-permute-start.15
  88.9 5.4 %collective-permute-start.16 = (bf16[2,128,2048]{2,1,0:T(8,128)(2,1)}, bf16[2,128,2048]{2,1,0:T(8,128)(2,1)S(1)}, u32[]{:S(2)}, u32[]{:S(2)}) collective-permute-start(bf16[2,128,2048]{2,1,0:T(8,128)(2,1)} %get-tuple-element.251), channel_id=1, source_target_pairs={{128,136},{136,144},{144,152},{152,160},{160,168},{168,176},{176,1... | collective-permute-start | bytes 3145736 | tf_op jit(solution)/shard_map/ppermute | solution.py:179
  94.3 0.6 collective-permute-start.9
  94.9 0.1 collective-permute-start.10
  95.1 0.0 collective-permute-done.8
  95.1 2.5 %collective-permute-start.11 = (f32[2,32]{1,0:T(2,128)S(1)}, f32[2,32]{1,0:T(2,128)S(1)}, u32[]{:S(2)}, u32[]{:S(2)}) collective-permute-start(f32[2,32]{1,0:T(2,128)S(1)} %get-tuple-element.264), channel_id=1, source_target_pairs={{0,4},{1,5},{2,6},{3,7},{4,0},{5,1},{6,2},{7,3},{8,12},{9,13},{10,... | collective-permute-start | bytes 776 | tf_op jit(solution)/shard_map/ppermute | solution.py:145
  97.5 0.0 collective-permute-done.9
  97.6 0.7 collective-permute-done.10
  98.3 0.9 collective-permute-start.13
  99.2 1.2 collective-permute-start.14
  100.4 2.0 %collective-permute-done.12 = f32[2,32]{1,0:T(2,128)S(1)} collective-permute-done((f32[2,32]{1,0:T(2,128)S(1)}, f32[2,32]{1,0:T(2,128)S(1)}, u32[]{:S(2)}, u32[]{:S(2)}) %collective-permute-start.12) | collective-permute-done | bytes 288 | tf_op jit(solution)/shard_map/ppermute | solution.py:145
  102.4 1.3 collective-permute-done.14
  103.8 1.0 collective-permute-done.15
  104.8 1.5 collective-permute-done.16
  106.3 1.4 add.141
  107.7 4.6 %collective-permute-start.19 = (bf16[2,128,2048]{2,1,0:T(8,128)(2,1)}, bf16[2,128,2048]{2,1,0:T(8,128)(2,1)S(1)}, u32[]{:S(2)}, u32[]{:S(2)}) collective-permute-start(bf16[2,128,2048]{2,1,0:T(8,128)(2,1)} %add.141), channel_id=1, source_target_pairs={{128,136},{136,144},{144,152},{152,160},{160,168},{168,176},{176,1... | collective-permute-start | bytes 3145736 | tf_op jit(solution)/shard_map/ppermute | solution.py:179
  112.3 18.7 %collective-permute-start.18 = (f32[2,32]{1,0:T(2,128)S(1)}, f32[2,32]{1,0:T(2,128)S(1)}, u32[]{:S(2)}, u32[]{:S(2)}) collective-permute-start(f32[2,32]{1,0:T(2,128)S(1)} %fusion.4), channel_id=1, source_target_pairs={{0,64},{8,72},{16,80},{24,88},{32,96},{40,104},{48,112},{56,120},{... | collective-permute-start | bytes 776 | tf_op jit(solution)/shard_map/ppermute | solution.py:155
  131.0 1.3 collective-permute-start.6
  132.3 1.6 add.138
  134.0 0.7 collective-permute-start.17
  134.7 10.6 %collective-permute-start.21 = (f32[2,32]{1,0:T(2,128)S(1)}, f32[2,32]{1,0:T(2,128)S(1)}, u32[]{:S(2)}, u32[]{:S(2)}) collective-permute-start(f32[2,32]{1,0:T(2,128)S(1)} %add.140), channel_id=1, source_target_pairs={{0,56},{8,0},{16,8},{24,16},{32,24},{40,32},{48,40},{56,48},{64,12... | collective-permute-start | bytes 776 | tf_op jit(solution)/shard_map/ppermute | solution.py:145
  145.4 0.0 collective-permute-start.22
  145.4 0.0 copy-start
  145.4 0.4 add.142
  145.8 0.3 collective-permute-done.21
  146.1 5.1 %collective-permute-start.24 = (f32[2,32]{1,0:T(2,128)S(1)}, f32[2,32]{1,0:T(2,128)S(1)}, u32[]{:S(2)}, u32[]{:S(2)}) collective-permute-start(f32[2,32]{1,0:T(2,128)S(1)} %add.140), channel_id=1, source_target_pairs={{0,32},{8,40},{16,48},{24,56},{32,0},{40,8},{48,16},{56,24},{64,96... | collective-permute-start | bytes 776 | tf_op jit(solution)/shard_map/ppermute | solution.py:145
  151.2 1.2 collective-permute-start.25
  152.5 1.1 collective-permute-start.26
  153.6 0.4 collective-permute-start.27
  153.9 2.8 %collective-permute-done.25 = f32[2,32]{1,0:T(2,128)S(1)} collective-permute-done((f32[2,32]{1,0:T(2,128)S(1)}, f32[2,32]{1,0:T(2,128)S(1)}, u32[]{:S(2)}, u32[]{:S(2)}) %collective-permute-start.25) | collective-permute-done | bytes 288 | tf_op jit(solution)/shard_map/ppermute | solution.py:145
  156.7 1.3 collective-permute-start.20
  158.2 0.5 fusion.6
  158.7 11.0 %collective-permute-done.20 = bf16[2,128,2048]{2,1,0:T(8,128)(2,1)S(1)} collective-permute-done((bf16[2,128,2048]{2,1,0:T(8,128)(2,1)S(1)}, bf16[2,128,2048]{2,1,0:T(8,128)(2,1)S(1)}, u32[]{:S(2)}, u32[]{:S(2)}) %collective-permute-start.20) | collective-permute-done | bytes 1048608 | tf_op jit(solution)/shard_map/ppermute | solution.py:179
  169.7 2.9 %fusion.1 = bf16[1,2,128,2048]{3,2,1,0:T(8,128)(2,1)} fusion(bf16[2,128,2048]{2,1,0:T(8,128)(2,1)} %get-tuple-element.259, bf16[2,128,2048]{2,1,0:T(8,128)(2,1)S(1)} %collective-permute-done.20, bf16[2,128,2048]{2,1,0:T(8,128)(2,1)S(1)} %collective-permute-done.17, bf16[2,128,2048]{2,1,0:T(8,128)(2,1)S(1)} %collective-permute-done.6, pred[]{:T(512)S(6)} %eq.28), kind=kLoop, calls=%fused_computation.7 | loop fusion | flops 3670016 | bytes 5242881 | tf_op jit(solution)/shard_map/broadcast_in_dim | solution.py:235
  (45 shorter events, 0.3 us)
Async XLA Ops:
  0.6 17.0 %collective-permute-start.3 = (bf16[2,128,2048]{2,1,0:T(8,128)(2,1)}, bf16[2,128,2048]{2,1,0:T(8,128)(2,1)S(1)}, u32[]{:S(2)}, u32[]{:S(2)}) collective-permute-start(bf16[2,128,2048]{2,1,0:T(8,128)(2,1)} %bitcast.55), channel_id=1, source_target_pairs={{8,128},{16,136},{24,144},{32,152},{40,160},{48,168},{56,176},{64,... | collective-permute-start | bytes 3145736 | tf_op jit(solution)/shard_map/ppermute | solution.py:179
  1.9 18.3 %collective-permute-start = (bf16[2,128,2048]{2,1,0:T(8,128)(2,1)}, bf16[2,128,2048]{2,1,0:T(8,128)(2,1)S(1)}, u32[]{:S(2)}, u32[]{:S(2)}) collective-permute-start(bf16[2,128,2048]{2,1,0:T(8,128)(2,1)} %bitcast.56), channel_id=1, source_target_pairs={{0,136},{8,144},{16,152},{24,160},{32,168},{40,176},{48,184},{56,1... | collective-permute-start | bytes 3145736 | tf_op jit(solution)/shard_map/ppermute | solution.py:179
  17.6 17.2 %copy-start.1 = (bf16[2,128,2048]{2,1,0:T(8,128)(2,1)}, bf16[2,128,2048]{2,1,0:T(8,128)(2,1)S(1)}, u32[]{:S(2)}) copy-start(bf16[2,128,2048]{2,1,0:T(8,128)(2,1)S(1)} %collective-permute-done.3) | copy-start | bytes 3145732
  17.6 15.9 %collective-permute-start.4 = (bf16[2,128,2048]{2,1,0:T(8,128)(2,1)S(1)}, bf16[2,128,2048]{2,1,0:T(8,128)(2,1)S(1)}, u32[]{:S(2)}, u32[]{:S(2)}) collective-permute-start(bf16[2,128,2048]{2,1,0:T(8,128)(2,1)S(1)} %collective-permute-done.3), channel_id=1, source_target_pairs={{136,128},{144,136},{152,144},{160,152},{168,160},{176,168},{184,1... | collective-permute-start | bytes 3145736 | tf_op jit(solution)/shard_map/ppermute | solution.py:179
  18.9 18.5 %collective-permute-start.2 = (bf16[2,128,2048]{2,1,0:T(8,128)(2,1)}, bf16[2,128,2048]{2,1,0:T(8,128)(2,1)}, u32[]{:S(2)}, u32[]{:S(2)}) collective-permute-start(bf16[2,128,2048]{2,1,0:T(8,128)(2,1)} %bitcast.57), channel_id=1, source_target_pairs={{0,128},{8,136},{16,144},{24,152},{32,160},{40,168},{48,176},{56,1... | collective-permute-start | bytes 3145736 | tf_op jit(solution)/shard_map/ppermute | solution.py:179
  20.2 17.2 %collective-permute-start.1 = (bf16[2,128,2048]{2,1,0:T(8,128)(2,1)S(1)}, bf16[2,128,2048]{2,1,0:T(8,128)(2,1)}, u32[]{:S(2)}, u32[]{:S(2)}) collective-permute-start(bf16[2,128,2048]{2,1,0:T(8,128)(2,1)S(1)} %collective-permute-done), channel_id=1, source_target_pairs={{128,136},{136,144},{144,152},{152,160},{160,168},{168,176},{176,1... | collective-permute-start | bytes 3145736 | tf_op jit(solution)/shard_map/ppermute | solution.py:179
  33.5 15.8 %collective-permute-start.5 = (bf16[2,128,2048]{2,1,0:T(8,128)(2,1)S(1)}, bf16[2,128,2048]{2,1,0:T(8,128)(2,1)}, u32[]{:S(2)}, u32[]{:S(2)}) collective-permute-start(bf16[2,128,2048]{2,1,0:T(8,128)(2,1)S(1)} %collective-permute-done.4), channel_id=1, source_target_pairs={{136,128},{144,136},{152,144},{160,152},{168,160},{176,168},{184,1... | collective-permute-start | bytes 3145736 | tf_op jit(solution)/shard_map/ppermute | solution.py:179
  49.3 3.3 %copy-start.2 = (bf16[2,128,2048]{2,1,0:T(8,128)(2,1)}, bf16[2,128,2048]{2,1,0:T(8,128)(2,1)S(1)}, u32[]{:S(2)}) copy-start(bf16[2,128,2048]{2,1,0:T(8,128)(2,1)S(1)} %get-tuple-element.218.refs_1_) | copy-start | bytes 3145732 | tf_op jit(solution)/shard_map/cond
  49.3 3.3 %copy-start.3 = (bf16[2,128,2048]{2,1,0:T(8,128)(2,1)}, bf16[2,128,2048]{2,1,0:T(8,128)(2,1)S(1)}, u32[]{:S(2)}) copy-start(bf16[2,128,2048]{2,1,0:T(8,128)(2,1)S(1)} %get-tuple-element.221.refs_4_) | copy-start | bytes 3145732 | tf_op jit(solution)/shard_map/cond
  82.8 1.2 collective-permute-start.7
  84.1 11.0 %collective-permute-start.8 = (f32[2,32]{1,0:T(2,128)S(1)}, f32[2,32]{1,0:T(2,128)S(1)}, u32[]{:S(2)}, u32[]{:S(2)}) collective-permute-start(f32[2,32]{1,0:T(2,128)S(1)} %get-tuple-element.264), channel_id=1, source_target_pairs={{0,7},{1,0},{2,1},{3,2},{4,3},{5,4},{6,5},{7,6},{8,15},{9,8},{10,9... | collective-permute-start | bytes 776 | tf_op jit(solution)/shard_map/ppermute | solution.py:145
  87.6 17.2 %collective-permute-start.15 = (bf16[2,128,2048]{2,1,0:T(8,128)(2,1)}, bf16[2,128,2048]{2,1,0:T(8,128)(2,1)}, u32[]{:S(2)}, u32[]{:S(2)}) collective-permute-start(bf16[2,128,2048]{2,1,0:T(8,128)(2,1)} %get-tuple-element.250), channel_id=1, source_target_pairs={{136,128},{144,136},{152,144},{160,152},{168,160},{176,168},{184,1... | collective-permute-start | bytes 3145736 | tf_op jit(solution)/shard_map/ppermute | solution.py:179
  88.9 17.4 %collective-permute-start.16 = (bf16[2,128,2048]{2,1,0:T(8,128)(2,1)}, bf16[2,128,2048]{2,1,0:T(8,128)(2,1)S(1)}, u32[]{:S(2)}, u32[]{:S(2)}) collective-permute-start(bf16[2,128,2048]{2,1,0:T(8,128)(2,1)} %get-tuple-element.251), channel_id=1, source_target_pairs={{128,136},{136,144},{144,152},{152,160},{160,168},{168,176},{176,1... | collective-permute-start | bytes 3145736 | tf_op jit(solution)/shard_map/ppermute | solution.py:179
  94.3 3.2 %collective-permute-start.9 = (f32[2,32]{1,0:T(2,128)S(1)}, f32[2,32]{1,0:T(2,128)S(1)}, u32[]{:S(2)}, u32[]{:S(2)}) collective-permute-start(f32[2,32]{1,0:T(2,128)S(1)} %get-tuple-element.264), channel_id=1, source_target_pairs={{0,6},{1,7},{2,0},{3,1},{4,2},{5,3},{6,4},{7,5},{8,14},{9,15},{10,... | collective-permute-start | bytes 776 | tf_op jit(solution)/shard_map/ppermute | solution.py:145
  94.9 3.3 %collective-permute-start.10 = (f32[2,32]{1,0:T(2,128)S(1)}, f32[2,32]{1,0:T(2,128)S(1)}, u32[]{:S(2)}, u32[]{:S(2)}) collective-permute-start(f32[2,32]{1,0:T(2,128)S(1)} %get-tuple-element.264), channel_id=1, source_target_pairs={{0,5},{1,6},{2,7},{3,0},{4,1},{5,2},{6,3},{7,4},{8,13},{9,14},{10,... | collective-permute-start | bytes 776 | tf_op jit(solution)/shard_map/ppermute | solution.py:145
  95.1 4.1 %collective-permute-start.11 = (f32[2,32]{1,0:T(2,128)S(1)}, f32[2,32]{1,0:T(2,128)S(1)}, u32[]{:S(2)}, u32[]{:S(2)}) collective-permute-start(f32[2,32]{1,0:T(2,128)S(1)} %get-tuple-element.264), channel_id=1, source_target_pairs={{0,4},{1,5},{2,6},{3,7},{4,0},{5,1},{6,2},{7,3},{8,12},{9,13},{10,... | collective-permute-start | bytes 776 | tf_op jit(solution)/shard_map/ppermute | solution.py:145
  97.5 4.8 %collective-permute-start.12 = (f32[2,32]{1,0:T(2,128)S(1)}, f32[2,32]{1,0:T(2,128)S(1)}, u32[]{:S(2)}, u32[]{:S(2)}) collective-permute-start(f32[2,32]{1,0:T(2,128)S(1)} %get-tuple-element.264), channel_id=1, source_target_pairs={{0,3},{1,4},{2,5},{3,6},{4,7},{5,0},{6,1},{7,2},{8,11},{9,12},{10,... | collective-permute-start | bytes 776 | tf_op jit(solution)/shard_map/ppermute | solution.py:145
  98.3 4.1 %collective-permute-start.13 = (f32[2,32]{1,0:T(2,128)S(1)}, f32[2,32]{1,0:T(2,128)S(1)}, u32[]{:S(2)}, u32[]{:S(2)}) collective-permute-start(f32[2,32]{1,0:T(2,128)S(1)} %get-tuple-element.264), channel_id=1, source_target_pairs={{0,2},{1,3},{2,4},{3,5},{4,6},{5,7},{6,0},{7,1},{8,10},{9,11},{10,... | collective-permute-start | bytes 776 | tf_op jit(solution)/shard_map/ppermute | solution.py:145
  99.2 4.5 %collective-permute-start.14 = (f32[2,32]{1,0:T(2,128)S(1)}, f32[2,32]{1,0:T(2,128)S(1)}, u32[]{:S(2)}, u32[]{:S(2)}) collective-permute-start(f32[2,32]{1,0:T(2,128)S(1)} %get-tuple-element.264), channel_id=1, source_target_pairs={{0,1},{1,2},{2,3},{3,4},{4,5},{5,6},{6,7},{7,0},{8,9},{9,10},{10,1... | collective-permute-start | bytes 776 | tf_op jit(solution)/shard_map/ppermute | solution.py:145
  107.7 27.1 %collective-permute-start.19 = (bf16[2,128,2048]{2,1,0:T(8,128)(2,1)}, bf16[2,128,2048]{2,1,0:T(8,128)(2,1)S(1)}, u32[]{:S(2)}, u32[]{:S(2)}) collective-permute-start(bf16[2,128,2048]{2,1,0:T(8,128)(2,1)} %add.141), channel_id=1, source_target_pairs={{128,136},{136,144},{144,152},{152,160},{160,168},{168,176},{176,1... | collective-permute-start | bytes 3145736 | tf_op jit(solution)/shard_map/ppermute | solution.py:179
  112.3 22.4 %collective-permute-start.18 = (f32[2,32]{1,0:T(2,128)S(1)}, f32[2,32]{1,0:T(2,128)S(1)}, u32[]{:S(2)}, u32[]{:S(2)}) collective-permute-start(f32[2,32]{1,0:T(2,128)S(1)} %fusion.4), channel_id=1, source_target_pairs={{0,64},{8,72},{16,80},{24,88},{32,96},{40,104},{48,112},{56,120},{... | collective-permute-start | bytes 776 | tf_op jit(solution)/shard_map/ppermute | solution.py:155
  131.0 27.7 %collective-permute-start.6 = (bf16[2,128,2048]{2,1,0:T(8,128)(2,1)}, bf16[2,128,2048]{2,1,0:T(8,128)(2,1)S(1)}, u32[]{:S(2)}, u32[]{:S(2)}) collective-permute-start(bf16[2,128,2048]{2,1,0:T(8,128)(2,1)} %get-tuple-element.248), channel_id=1, source_target_pairs={{128,0},{136,8},{144,16},{152,24},{160,32},{168,40},{176,48},{184,... | collective-permute-start | bytes 3145736 | tf_op jit(solution)/shard_map/ppermute | solution.py:179
  134.0 24.7 %collective-permute-start.17 = (bf16[2,128,2048]{2,1,0:T(8,128)(2,1)S(1)}, bf16[2,128,2048]{2,1,0:T(8,128)(2,1)S(1)}, u32[]{:S(2)}, u32[]{:S(2)}) collective-permute-start(bf16[2,128,2048]{2,1,0:T(8,128)(2,1)S(1)} %add.138), channel_id=1, source_target_pairs={{136,0},{144,8},{152,16},{160,24},{168,32},{176,40},{184,48},{192,... | collective-permute-start | bytes 3145736 | tf_op jit(solution)/shard_map/ppermute | solution.py:179
  134.7 11.4 %collective-permute-start.21 = (f32[2,32]{1,0:T(2,128)S(1)}, f32[2,32]{1,0:T(2,128)S(1)}, u32[]{:S(2)}, u32[]{:S(2)}) collective-permute-start(f32[2,32]{1,0:T(2,128)S(1)} %add.140), channel_id=1, source_target_pairs={{0,56},{8,0},{16,8},{24,16},{32,24},{40,32},{48,40},{56,48},{64,12... | collective-permute-start | bytes 776 | tf_op jit(solution)/shard_map/ppermute | solution.py:145
  145.4 5.9 %collective-permute-start.22 = (f32[2,32]{1,0:T(2,128)S(1)}, f32[2,32]{1,0:T(2,128)S(1)}, u32[]{:S(2)}, u32[]{:S(2)}) collective-permute-start(f32[2,32]{1,0:T(2,128)S(1)} %add.140), channel_id=1, source_target_pairs={{0,48},{8,56},{16,0},{24,8},{32,16},{40,24},{48,32},{56,40},{64,11... | collective-permute-start | bytes 776 | tf_op jit(solution)/shard_map/ppermute | solution.py:145
  145.4 7.1 %collective-permute-start.23 = (f32[2,32]{1,0:T(2,128)S(1)}, f32[2,32]{1,0:T(2,128)S(1)}, u32[]{:S(2)}, u32[]{:S(2)}) collective-permute-start(f32[2,32]{1,0:T(2,128)S(1)} %add.140), channel_id=1, source_target_pairs={{0,40},{8,48},{16,56},{24,0},{32,8},{40,16},{48,24},{56,32},{64,10... | collective-permute-start | bytes 776 | tf_op jit(solution)/shard_map/ppermute | solution.py:145
  145.4 12.8 %copy-start = (f32[2,32]{1,0:T(2,128)S(1)}, f32[2,32]{1,0:T(2,128)}, u32[]{:S(2)}) copy-start(f32[2,32]{1,0:T(2,128)} %param.8) | copy-start | bytes 772
  146.1 7.5 %collective-permute-start.24 = (f32[2,32]{1,0:T(2,128)S(1)}, f32[2,32]{1,0:T(2,128)S(1)}, u32[]{:S(2)}, u32[]{:S(2)}) collective-permute-start(f32[2,32]{1,0:T(2,128)S(1)} %add.140), channel_id=1, source_target_pairs={{0,32},{8,40},{16,48},{24,56},{32,0},{40,8},{48,16},{56,24},{64,96... | collective-permute-start | bytes 776 | tf_op jit(solution)/shard_map/ppermute | solution.py:145
  151.2 5.4 %collective-permute-start.25 = (f32[2,32]{1,0:T(2,128)S(1)}, f32[2,32]{1,0:T(2,128)S(1)}, u32[]{:S(2)}, u32[]{:S(2)}) collective-permute-start(f32[2,32]{1,0:T(2,128)S(1)} %add.140), channel_id=1, source_target_pairs={{0,24},{8,32},{16,40},{24,48},{32,56},{40,0},{48,8},{56,16},{64,88... | collective-permute-start | bytes 776 | tf_op jit(solution)/shard_map/ppermute | solution.py:145
  152.5 5.6 %collective-permute-start.26 = (f32[2,32]{1,0:T(2,128)S(1)}, f32[2,32]{1,0:T(2,128)S(1)}, u32[]{:S(2)}, u32[]{:S(2)}) collective-permute-start(f32[2,32]{1,0:T(2,128)S(1)} %add.140), channel_id=1, source_target_pairs={{0,16},{8,24},{16,32},{24,40},{32,48},{40,56},{48,0},{56,8},{64,80... | collective-permute-start | bytes 776 | tf_op jit(solution)/shard_map/ppermute | solution.py:145
  153.6 4.5 %collective-permute-start.27 = (f32[2,32]{1,0:T(2,128)S(1)}, f32[2,32]{1,0:T(2,128)S(1)}, u32[]{:S(2)}, u32[]{:S(2)}) collective-permute-start(f32[2,32]{1,0:T(2,128)S(1)} %add.140), channel_id=1, source_target_pairs={{0,8},{8,16},{16,24},{24,32},{32,40},{40,48},{48,56},{56,0},{64,72... | collective-permute-start | bytes 776 | tf_op jit(solution)/shard_map/ppermute | solution.py:145
  156.7 13.0 %collective-permute-start.20 = (bf16[2,128,2048]{2,1,0:T(8,128)(2,1)S(1)}, bf16[2,128,2048]{2,1,0:T(8,128)(2,1)S(1)}, u32[]{:S(2)}, u32[]{:S(2)}) collective-permute-start(bf16[2,128,2048]{2,1,0:T(8,128)(2,1)S(1)} %add.142), channel_id=1, source_target_pairs={{128,8},{136,16},{144,24},{152,32},{160,40},{168,48},{176,56},{184... | collective-permute-start | bytes 3145736 | tf_op jit(solution)/shard_map/ppermute | solution.py:179

commit v12 on v7

--- a/solution.py
+++ b/solution.py
@@ -43,42 +43,47 @@
     k = jnp.concatenate([piece[0] for piece in slots], axis=0)
     v = jnp.concatenate([piece[1] for piece in slots], axis=0)
     allowed = allow_ref[...] > 0
+    rows = q.shape[0]
     lane = lax.broadcasted_iota(jnp.int32, (1, width), 1)
     first = lane < half
-    heads = []
-    att_parts = []
-    for j in range(2):
-        head = pair * 2 + j
-        g_logit = gains_ref[0, head]
-        g_value = gains_ref[1, head]
-        mine = first if j == 0 else jnp.logical_not(first)
-        q_h = jnp.where(mine, q, jnp.zeros_like(q))
-        raw = lax.dot_general(q_h, k, (((1,), (1,)), ((), ())), preferred_element_type=jnp.float32)
-        logits = jnp.where(allowed, (g_logit * inv_root) * raw, masked_score)
-        top = jnp.max(logits, axis=1, keepdims=True)
-        lifted = jnp.exp(logits - top)
-        chances = lifted * (1.0 / jnp.sum(lifted, axis=1, keepdims=True))
-        p_low = chances.astype(jnp.bfloat16)
-        att_parts.append(jnp.dot(p_low, v, preferred_element_type=jnp.float32) * g_value)
-        heads.append((g_logit, g_value, mine, raw, chances, p_low))
-    attended = jnp.where(first, att_parts[0], att_parts[1]).astype(jnp.bfloat16)
+    upper_rows = lax.broadcasted_iota(jnp.int32, (2 * rows, 1), 0) < rows
+    gl0, gl1 = gains_ref[0, pair * 2], gains_ref[0, pair * 2 + 1]
+    gv0, gv1 = gains_ref[1, pair * 2], gains_ref[1, pair * 2 + 1]
+    zero_q = jnp.zeros_like(q)
+    q2 = jnp.concatenate([jnp.where(first, q, zero_q), jnp.where(first, zero_q, q)], axis=0)
+    do2 = jnp.concatenate([jnp.where(first, do, zero_q), jnp.where(first, zero_q, do)], axis=0)
+    row_logit = jnp.where(upper_rows, gl0 * inv_root, gl1 * inv_root)
+    row_value = jnp.where(upper_rows, gv0, gv1)
+    lane_value = jnp.where(first, gv0, gv1)
+    lane_factor = jnp.where(first, gl0 * inv_root, gl1 * inv_root)
+    raw = lax.dot_general(q2, k, (((1,), (1,)), ((), ())), preferred_element_type=jnp.float32)
+    logits = jnp.where(allowed, row_logit * raw, masked_score)
+    top = jnp.max(logits, axis=1, keepdims=True)
+    lifted = jnp.exp(logits - top)
+    chances = lifted * (1.0 / jnp.sum(lifted, axis=1, keepdims=True))
+    p_low = chances.astype(jnp.bfloat16)
+    pv = jnp.dot(p_low, v, preferred_element_type=jnp.float32)
+    attended = jnp.where(first, pv[:rows] * gv0, pv[rows:] * gv1).astype(jnp.bfloat16)
     out_ref[0] = attended
     prod = do.astype(jnp.float32) * attended.astype(jnp.float32)
-    dq_parts, dk_parts, dv_parts, logit_terms = [], [], [], []
-    for g_logit, g_value, mine, raw, chances, p_low in heads:
-        do_h = jnp.where(mine, do, jnp.zeros_like(do))
-        slope = lax.dot_general(do_h, v, (((1,), (1,)), ((), ())), preferred_element_type=jnp.float32) * g_value
-        carried = jnp.sum(jnp.where(mine, prod, 0.0), axis=1, keepdims=True)
-        score_grad = chances * (slope - carried)
-        score_low = score_grad.astype(jnp.bfloat16)
-        factor = g_logit * inv_root
-        dq_parts.append(jnp.dot(score_low, k, preferred_element_type=jnp.float32) * factor)
-        dk_parts.append(lax.dot_general(score_low, q, (((0,), (0,)), ((), ())), preferred_element_type=jnp.float32) * factor)
-        dv_parts.append(lax.dot_general(p_low, do, (((0,), (0,)), ((), ())), preferred_element_type=jnp.float32) * g_value)
-        logit_terms.append(jnp.sum(score_grad * raw) * inv_root)
-    out_ref[1] = jnp.where(first, dq_parts[0], dq_parts[1]).astype(jnp.bfloat16)
-    key_grad = jnp.where(first, dk_parts[0], dk_parts[1]).astype(jnp.bfloat16)
-    value_grad = jnp.where(first, dv_parts[0], dv_parts[1]).astype(jnp.bfloat16)
+    carried = jnp.concatenate(
+        [jnp.sum(jnp.where(first, prod, 0.0), axis=1, keepdims=True),
+         jnp.sum(jnp.where(first, 0.0, prod), axis=1, keepdims=True)],
+        axis=0,
+    )
+    slope = lax.dot_general(do2, v, (((1,), (1,)), ((), ())), preferred_element_type=jnp.float32) * row_value
+    score_grad = chances * (slope - carried)
+    score_low = score_grad.astype(jnp.bfloat16)
+    dq_raw = jnp.dot(score_low, k, preferred_element_type=jnp.float32)
+    out_ref[1] = jnp.where(first, dq_raw[:rows] * (gl0 * inv_root), dq_raw[rows:] * (gl1 * inv_root)).astype(jnp.bfloat16)
+    key_grad = (
+        lax.dot_general(score_low, q2, (((0,), (0,)), ((), ())), preferred_element_type=jnp.float32) * lane_factor
+    ).astype(jnp.bfloat16)
+    value_grad = (
+        lax.dot_general(p_low, do2, (((0,), (0,)), ((), ())), preferred_element_type=jnp.float32) * lane_value
+    ).astype(jnp.bfloat16)
+    weighted = score_grad * raw
+    logit_terms = [jnp.sum(weighted[:rows]) * inv_root, jnp.sum(weighted[rows:]) * inv_root]
     value_prod = v.astype(jnp.float32) * value_grad.astype(jnp.float32)
     value_terms = [jnp.sum(jnp.where(first, value_prod, 0.0)), jnp.sum(jnp.where(first, 0.0, value_prod))]
     zero_block = jnp.zeros((BLOCK, width), jnp.bfloat16)

time: 175 us -> 170 us (0.971)
  starting transfers between devices: 121 us -> 116 us
    ppermute x5, starting transfers between devices: 75.9 us -> 71.1 us  [exchange_add(): lax.ppermute(value, axis, [(i, i ^ stride) for i in range(count)])]
where the time goes in v12:
time: 170 us; the launch traced here: 168 us
  starting transfers between devices  116 us (68%)
  waiting for transfers between devices  37.7 us (22%)
  other arithmetic  7.43 us (4%)
  local copies, waits for them, and re-layouts  5.75 us (3%)
    ppermute x5, starting transfers between devices, exchange_add(): lax.ppermute(value, axis, [(i, i ^ stride) for i in range(count)])  71.1 us
    ppermute x12, starting transfers between devices, across(): return lax.ppermute(value, ('phase', 'seq'), pairs)  29.9 us
    ppermute x12, waiting for transfers between devices, across(): return lax.ppermute(value, ('phase', 'seq'), pairs)  22.5 us
    ppermute x4, starting transfers between devices, ring_shift(): return lax.ppermute(value, 'seq', pairs)  14.8 us
    ppermute x5, waiting for transfers between devices, exchange_add(): lax.ppermute(value, axis, [(i, i ^ stride) for i in range(count)])  9.64 us
    another operation x9, local copies, waits for them, and re-layouts  5.66 us
    ppermute x4, waiting for transfers between devices, ring_shift(): return lax.ppermute(value, 'seq', pairs)  5.63 us
  transfers between devices with their start and end apart: 21, of which 10 were waited for; matrix products, arithmetic and copies ran while one was open for 3% of the time, Pallas kernels for 0%

profile of v12, /device:TPU:8, one launch (start us, length us, event | category | flops | bytes accessed | tf_op | source)
XLA Modules:
  0.0 167.6 jit_solution(7223101205437061822)
XLA Ops:
  0.6 0.7 collective-permute-start.3
  1.4 3.9 %collective-permute-start = (bf16[2,128,2048]{2,1,0:T(8,128)(2,1)}, bf16[2,128,2048]{2,1,0:T(8,128)(2,1)S(1)}, u32[]{:S(2)}, u32[]{:S(2)}) collective-permute-start(bf16[2,128,2048]{2,1,0:T(8,128)(2,1)} %bitcast.29), channel_id=1, source_target_pairs={{0,136},{8,144},{16,152},{24,160},{32,168},{40,176},{48,184},{56,1... | collective-permute-start | bytes 3145736 | tf_op jit(solution)/shard_map/ppermute | solution.py:190
  5.3 0.0 collective-permute-done.3
  5.3 0.0 copy-start.1
  5.3 0.7 collective-permute-start.4
  6.0 15.0 %collective-permute-start.2 = (bf16[2,128,2048]{2,1,0:T(8,128)(2,1)}, bf16[2,128,2048]{2,1,0:T(8,128)(2,1)}, u32[]{:S(2)}, u32[]{:S(2)}) collective-permute-start(bf16[2,128,2048]{2,1,0:T(8,128)(2,1)} %bitcast.30), channel_id=1, source_target_pairs={{0,128},{8,136},{16,144},{24,152},{32,160},{40,168},{48,176},{56,1... | collective-permute-start | bytes 3145736 | tf_op jit(solution)/shard_map/ppermute | solution.py:190
  21.0 0.0 collective-permute-done
  21.0 1.6 collective-permute-start.1
  22.6 0.0 collective-permute-done.4
  22.6 1.6 collective-permute-start.5
  24.3 0.0 copy-done.1
  24.3 0.8 slice_bitcast_fusion.1
  25.0 0.2 reduce-window.8
  25.2 0.2 reduce-window_1_clone.1
  25.4 0.7 bitcast_subtract_fusion
  26.1 0.7 compare_convert_fusion.2
  26.8 0.1 compare_convert_fusion.1
  26.8 0.0 collective-permute-done.2
  26.8 0.0 collective-permute-done.1
  26.8 0.0 collective-permute-done.5
  26.8 4.9 %conditional.1 = (bf16[2,128,2048]{2,1,0:T(8,128)(2,1)}, bf16[2,128,2048]{2,1,0:T(8,128)(2,1)}, bf16[2,128,2048]{2,1,0:T(8,128)(2,1)S(1)}, bf16[2,128,2048]{2,1,...) conditional(s32[]{:T(128)} %convert_element_type.45, () %tuple.45, ...), branch_computations={%region_2.3_spmd, %region_3.6_spmd} | conditional | flops 3221225472 | bytes 23072892 | solution.py:220
  26.9 1.1 broadcast.46
  28.0 1.1 broadcast.46.clone
  29.1 0.1 broadcast.46.clone.1
  29.2 1.1 broadcast.46.clone.2
  30.4 0.1 broadcast.46.clone.3
  30.5 0.1 broadcast.46.clone.4
  30.6 1.2 broadcast.46.clone.5
  31.8 1.6 collective-permute-start.11
  33.4 0.7 collective-permute-start.12
  34.1 49.9 %collective-permute-start.7 = (f32[2,32]{1,0:T(2,128)S(1)}, f32[2,32]{1,0:T(2,128)S(1)}, u32[]{:S(2)}, u32[]{:S(2)}) collective-permute-start(f32[2,32]{1,0:T(2,128)S(1)} %get-tuple-element.248), channel_id=1, source_target_pairs={{0,128},{128,0},{1,129},{129,1},{2,130},{130,2},{3,131},{131,3},{4... | collective-permute-start | bytes 776 | tf_op jit(solution)/shard_map/ppermute | solution.py:166
  84.1 0.8 collective-permute-done.7
  84.9 0.4 collective-permute-start.8
  85.3 3.1 %collective-permute-done.8 = f32[2,32]{1,0:T(2,128)S(1)} collective-permute-done((f32[2,32]{1,0:T(2,128)S(1)}, f32[2,32]{1,0:T(2,128)S(1)}, u32[]{:S(2)}, u32[]{:S(2)}) %collective-permute-start.8) | collective-permute-done | bytes 288 | tf_op jit(solution)/shard_map/ppermute | solution.py:166
  88.5 1.5 collective-permute-start.9
  90.0 2.1 %collective-permute-done.9 = f32[2,32]{1,0:T(2,128)S(1)} collective-permute-done((f32[2,32]{1,0:T(2,128)S(1)}, f32[2,32]{1,0:T(2,128)S(1)}, u32[]{:S(2)}, u32[]{:S(2)}) %collective-permute-start.9) | collective-permute-done | bytes 288 | tf_op jit(solution)/shard_map/ppermute | solution.py:166
  92.1 3.0 %collective-permute-start.10 = (f32[2,32]{1,0:T(2,128)S(1)}, f32[2,32]{1,0:T(2,128)S(1)}, u32[]{:S(2)}, u32[]{:S(2)}) collective-permute-start(f32[2,32]{1,0:T(2,128)S(1)} %add.109), channel_id=1, source_target_pairs={{0,4},{1,5},{2,6},{3,7},{4,0},{5,1},{6,2},{7,3},{8,12},{9,13},{10,... | collective-permute-start | bytes 776 | tf_op jit(solution)/shard_map/ppermute | solution.py:166
  95.1 2.1 %collective-permute-done.10 = f32[2,32]{1,0:T(2,128)S(1)} collective-permute-done((f32[2,32]{1,0:T(2,128)S(1)}, f32[2,32]{1,0:T(2,128)S(1)}, u32[]{:S(2)}, u32[]{:S(2)}) %collective-permute-start.10) | collective-permute-done | bytes 288 | tf_op jit(solution)/shard_map/ppermute | solution.py:166
  97.1 0.0 collective-permute-done.11
  97.1 0.0 collective-permute-done.12
  97.1 1.4 add.114
  98.5 0.7 collective-permute-start.15
  99.3 16.2 %collective-permute-start.14 = (f32[2,32]{1,0:T(2,128)S(1)}, f32[2,32]{1,0:T(2,128)S(1)}, u32[]{:S(2)}, u32[]{:S(2)}) collective-permute-start(f32[2,32]{1,0:T(2,128)S(1)} %add.110), channel_id=1, source_target_pairs={{0,64},{8,72},{16,80},{24,88},{32,96},{40,104},{48,112},{56,120},{... | collective-permute-start | bytes 776 | tf_op jit(solution)/shard_map/ppermute | solution.py:166
  115.4 1.6 collective-permute-done.14
  117.0 0.0 collective-permute-done.15
  117.0 5.9 %collective-permute-start.17 = (f32[1,2,32]{2,1,0:T(2,128)S(1)}, f32[1,2,32]{2,1,0:T(2,128)S(1)}, u32[]{:S(2)}, u32[]{:S(2)}) collective-permute-start(f32[1,2,32]{2,1,0:T(2,128)S(1)} %bitcast.23), channel_id=1, source_target_pairs={{0,56},{8,0},{16,8},{24,16},{32,24},{40,32},{48,40},{56,48},{64,12... | collective-permute-start | bytes 776 | tf_op jit(solution)/shard_map/ppermute | solution.py:147
  122.9 1.3 collective-permute-done.17
  124.2 1.7 %collective-permute-start.18 = (f32[2,2,32]{2,1,0:T(2,128)S(1)}, f32[2,2,32]{2,1,0:T(2,128)S(1)}, u32[]{:S(2)}, u32[]{:S(2)}) collective-permute-start(f32[2,2,32]{2,1,0:T(2,128)S(1)} %pad_maximum_fusion.3), channel_id=1, source_target_pairs={{0,48},{8,56},{16,0},{24,8},{32,16},{40,24},{48,32},{56,40},{64,11... | collective-permute-start | bytes 1544 | tf_op jit(solution)/shard_map/ppermute | solution.py:147
  125.9 2.8 %collective-permute-done.18 = f32[2,2,32]{2,1,0:T(2,128)S(1)} collective-permute-done((f32[2,2,32]{2,1,0:T(2,128)S(1)}, f32[2,2,32]{2,1,0:T(2,128)S(1)}, u32[]{:S(2)}, u32[]{:S(2)}) %collective-permute-start.18) | collective-permute-done | bytes 544 | tf_op jit(solution)/shard_map/ppermute | solution.py:147
  128.7 2.9 %collective-permute-start.19 = (f32[4,2,32]{2,1,0:T(2,128)S(1)}, f32[4,2,32]{2,1,0:T(2,128)S(1)}, u32[]{:S(2)}, u32[]{:S(2)}) collective-permute-start(f32[4,2,32]{2,1,0:T(2,128)S(1)} %pad_maximum_fusion.2), channel_id=1, source_target_pairs={{0,48},{8,56},{16,0},{24,8},{32,16},{40,24},{48,32},{56,40},{64,11... | collective-permute-start | bytes 3080 | tf_op jit(solution)/shard_map/ppermute | solution.py:147
  131.6 1.6 collective-permute-done.19
  133.2 4.2 %collective-permute-start.20 = (f32[6,2,32]{2,1,0:T(2,128)S(1)}, f32[6,2,32]{2,1,0:T(2,128)S(1)}, u32[]{:S(2)}, u32[]{:S(2)}) collective-permute-start(f32[6,2,32]{2,1,0:T(2,128)S(1)} %pad_maximum_fusion.1), channel_id=1, source_target_pairs={{0,48},{8,56},{16,0},{24,8},{32,16},{40,24},{48,32},{56,40},{64,11... | collective-permute-start | bytes 4616 | tf_op jit(solution)/shard_map/ppermute | solution.py:147
  137.4 1.3 collective-permute-start.6
  138.7 1.6 add.111
  140.3 1.3 collective-permute-start.13
  141.6 0.0 copy-start
  141.7 0.4 add.115
  142.0 0.7 collective-permute-start.16
  142.8 0.0 collective-permute-done.20
  142.9 0.5 fusion.10
  143.4 6.6 %collective-permute-done.6 = bf16[2,128,2048]{2,1,0:T(8,128)(2,1)S(1)} collective-permute-done((bf16[2,128,2048]{2,1,0:T(8,128)(2,1)}, bf16[2,128,2048]{2,1,0:T(8,128)(2,1)S(1)}, u32[]{:S(2)}, u32[]{:S(2)}) %collective-permute-start.6) | collective-permute-done | bytes 1048608 | tf_op jit(solution)/shard_map/ppermute | solution.py:190
  150.0 15.9 %collective-permute-done.13 = bf16[2,128,2048]{2,1,0:T(8,128)(2,1)S(1)} collective-permute-done((bf16[2,128,2048]{2,1,0:T(8,128)(2,1)S(1)}, bf16[2,128,2048]{2,1,0:T(8,128)(2,1)S(1)}, u32[]{:S(2)}, u32[]{:S(2)}) %collective-permute-start.13) | collective-permute-done | bytes 1048608 | tf_op jit(solution)/shard_map/ppermute | solution.py:190
  165.9 0.0 collective-permute-done.16
  165.9 1.7 %fusion.1 = bf16[1,2,128,2048]{3,2,1,0:T(8,128)(2,1)} fusion(bf16[2,128,2048]{2,1,0:T(8,128)(2,1)} %get-tuple-element.258, bf16[2,128,2048]{2,1,0:T(8,128)(2,1)S(1)} %collective-permute-done.16, bf16[2,128,2048]{2,1,0:T(8,128)(2,1)S(1)} %collective-permute-done.13, bf16[2,128,2048]{2,1,0:T(8,128)(2,1)S(1)} %collective-permute-done.6, pred[]{:T(512)S(6)} %eq.28), kind=kLoop, calls=%fused_computation.7 | loop fusion | flops 3670016 | bytes 5242881 | tf_op jit(solution)/shard_map/broadcast_in_dim | solution.py:246
  (22 shorter events, 0.1 us)
Async XLA Ops:
  0.6 4.6 %collective-permute-start.3 = (bf16[2,128,2048]{2,1,0:T(8,128)(2,1)}, bf16[2,128,2048]{2,1,0:T(8,128)(2,1)S(1)}, u32[]{:S(2)}, u32[]{:S(2)}) collective-permute-start(bf16[2,128,2048]{2,1,0:T(8,128)(2,1)} %bitcast.28), channel_id=1, source_target_pairs={{8,128},{16,136},{24,144},{32,152},{40,160},{48,168},{56,176},{64,... | collective-permute-start | bytes 3145736 | tf_op jit(solution)/shard_map/ppermute | solution.py:190
  1.4 19.6 %collective-permute-start = (bf16[2,128,2048]{2,1,0:T(8,128)(2,1)}, bf16[2,128,2048]{2,1,0:T(8,128)(2,1)S(1)}, u32[]{:S(2)}, u32[]{:S(2)}) collective-permute-start(bf16[2,128,2048]{2,1,0:T(8,128)(2,1)} %bitcast.29), channel_id=1, source_target_pairs={{0,136},{8,144},{16,152},{24,160},{32,168},{40,176},{48,184},{56,1... | collective-permute-start | bytes 3145736 | tf_op jit(solution)/shard_map/ppermute | solution.py:190
  5.3 19.0 %copy-start.1 = (bf16[2,128,2048]{2,1,0:T(8,128)(2,1)}, bf16[2,128,2048]{2,1,0:T(8,128)(2,1)S(1)}, u32[]{:S(2)}) copy-start(bf16[2,128,2048]{2,1,0:T(8,128)(2,1)S(1)} %collective-permute-done.3) | copy-start | bytes 3145732
  5.3 17.4 %collective-permute-start.4 = (bf16[2,128,2048]{2,1,0:T(8,128)(2,1)S(1)}, bf16[2,128,2048]{2,1,0:T(8,128)(2,1)S(1)}, u32[]{:S(2)}, u32[]{:S(2)}) collective-permute-start(bf16[2,128,2048]{2,1,0:T(8,128)(2,1)S(1)} %collective-permute-done.3), channel_id=1, source_target_pairs={{136,128},{144,136},{152,144},{160,152},{168,160},{176,168},{184,1... | collective-permute-start | bytes 3145736 | tf_op jit(solution)/shard_map/ppermute | solution.py:190
  6.0 20.8 %collective-permute-start.2 = (bf16[2,128,2048]{2,1,0:T(8,128)(2,1)}, bf16[2,128,2048]{2,1,0:T(8,128)(2,1)}, u32[]{:S(2)}, u32[]{:S(2)}) collective-permute-start(bf16[2,128,2048]{2,1,0:T(8,128)(2,1)} %bitcast.30), channel_id=1, source_target_pairs={{0,128},{8,136},{16,144},{24,152},{32,160},{40,168},{48,176},{56,1... | collective-permute-start | bytes 3145736 | tf_op jit(solution)/shard_map/ppermute | solution.py:190
  21.0 5.8 %collective-permute-start.1 = (bf16[2,128,2048]{2,1,0:T(8,128)(2,1)S(1)}, bf16[2,128,2048]{2,1,0:T(8,128)(2,1)}, u32[]{:S(2)}, u32[]{:S(2)}) collective-permute-start(bf16[2,128,2048]{2,1,0:T(8,128)(2,1)S(1)} %collective-permute-done), channel_id=1, source_target_pairs={{128,136},{136,144},{144,152},{152,160},{160,168},{168,176},{176,1... | collective-permute-start | bytes 3145736 | tf_op jit(solution)/shard_map/ppermute | solution.py:190
  22.6 4.2 %collective-permute-start.5 = (bf16[2,128,2048]{2,1,0:T(8,128)(2,1)S(1)}, bf16[2,128,2048]{2,1,0:T(8,128)(2,1)}, u32[]{:S(2)}, u32[]{:S(2)}) collective-permute-start(bf16[2,128,2048]{2,1,0:T(8,128)(2,1)S(1)} %collective-permute-done.4), channel_id=1, source_target_pairs={{136,128},{144,136},{152,144},{160,152},{168,160},{176,168},{184,1... | collective-permute-start | bytes 3145736 | tf_op jit(solution)/shard_map/ppermute | solution.py:190
  31.8 65.3 %collective-permute-start.11 = (bf16[2,128,2048]{2,1,0:T(8,128)(2,1)}, bf16[2,128,2048]{2,1,0:T(8,128)(2,1)}, u32[]{:S(2)}, u32[]{:S(2)}) collective-permute-start(bf16[2,128,2048]{2,1,0:T(8,128)(2,1)} %get-tuple-element.249), channel_id=1, source_target_pairs={{136,128},{144,136},{152,144},{160,152},{168,160},{176,168},{184,1... | collective-permute-start | bytes 3145736 | tf_op jit(solution)/shard_map/ppermute | solution.py:190
  33.4 63.7 %collective-permute-start.12 = (bf16[2,128,2048]{2,1,0:T(8,128)(2,1)}, bf16[2,128,2048]{2,1,0:T(8,128)(2,1)S(1)}, u32[]{:S(2)}, u32[]{:S(2)}) collective-permute-start(bf16[2,128,2048]{2,1,0:T(8,128)(2,1)} %get-tuple-element.250), channel_id=1, source_target_pairs={{128,136},{136,144},{144,152},{152,160},{160,168},{168,176},{176,1... | collective-permute-start | bytes 3145736 | tf_op jit(solution)/shard_map/ppermute | solution.py:190
  34.1 50.7 %collective-permute-start.7 = (f32[2,32]{1,0:T(2,128)S(1)}, f32[2,32]{1,0:T(2,128)S(1)}, u32[]{:S(2)}, u32[]{:S(2)}) collective-permute-start(f32[2,32]{1,0:T(2,128)S(1)} %get-tuple-element.248), channel_id=1, source_target_pairs={{0,128},{128,0},{1,129},{129,1},{2,130},{130,2},{3,131},{131,3},{4... | collective-permute-start | bytes 776 | tf_op jit(solution)/shard_map/ppermute | solution.py:166
  84.9 3.6 %collective-permute-start.8 = (f32[2,32]{1,0:T(2,128)S(1)}, f32[2,32]{1,0:T(2,128)S(1)}, u32[]{:S(2)}, u32[]{:S(2)}) collective-permute-start(f32[2,32]{1,0:T(2,128)S(1)} %add.107), channel_id=1, source_target_pairs={{0,1},{1,0},{2,3},{3,2},{4,5},{5,4},{6,7},{7,6},{8,9},{9,8},{10,11... | collective-permute-start | bytes 776 | tf_op jit(solution)/shard_map/ppermute | solution.py:166
  88.5 3.6 %collective-permute-start.9 = (f32[2,32]{1,0:T(2,128)S(1)}, f32[2,32]{1,0:T(2,128)S(1)}, u32[]{:S(2)}, u32[]{:S(2)}) collective-permute-start(f32[2,32]{1,0:T(2,128)S(1)} %add.108), channel_id=1, source_target_pairs={{0,2},{1,3},{2,0},{3,1},{4,6},{5,7},{6,4},{7,5},{8,10},{9,11},{10,... | collective-permute-start | bytes 776 | tf_op jit(solution)/shard_map/ppermute | solution.py:166
  92.1 5.1 %collective-permute-start.10 = (f32[2,32]{1,0:T(2,128)S(1)}, f32[2,32]{1,0:T(2,128)S(1)}, u32[]{:S(2)}, u32[]{:S(2)}) collective-permute-start(f32[2,32]{1,0:T(2,128)S(1)} %add.109), channel_id=1, source_target_pairs={{0,4},{1,5},{2,6},{3,7},{4,0},{5,1},{6,2},{7,3},{8,12},{9,13},{10,... | collective-permute-start | bytes 776 | tf_op jit(solution)/shard_map/ppermute | solution.py:166
  98.5 18.5 %collective-permute-start.15 = (bf16[2,128,2048]{2,1,0:T(8,128)(2,1)}, bf16[2,128,2048]{2,1,0:T(8,128)(2,1)S(1)}, u32[]{:S(2)}, u32[]{:S(2)}) collective-permute-start(bf16[2,128,2048]{2,1,0:T(8,128)(2,1)} %add.114), channel_id=1, source_target_pairs={{128,136},{136,144},{144,152},{152,160},{160,168},{168,176},{176,1... | collective-permute-start | bytes 3145736 | tf_op jit(solution)/shard_map/ppermute | solution.py:190
  99.3 17.7 %collective-permute-start.14 = (f32[2,32]{1,0:T(2,128)S(1)}, f32[2,32]{1,0:T(2,128)S(1)}, u32[]{:S(2)}, u32[]{:S(2)}) collective-permute-start(f32[2,32]{1,0:T(2,128)S(1)} %add.110), channel_id=1, source_target_pairs={{0,64},{8,72},{16,80},{24,88},{32,96},{40,104},{48,112},{56,120},{... | collective-permute-start | bytes 776 | tf_op jit(solution)/shard_map/ppermute | solution.py:166
  117.0 7.2 %collective-permute-start.17 = (f32[1,2,32]{2,1,0:T(2,128)S(1)}, f32[1,2,32]{2,1,0:T(2,128)S(1)}, u32[]{:S(2)}, u32[]{:S(2)}) collective-permute-start(f32[1,2,32]{2,1,0:T(2,128)S(1)} %bitcast.23), channel_id=1, source_target_pairs={{0,56},{8,0},{16,8},{24,16},{32,24},{40,32},{48,40},{56,48},{64,12... | collective-permute-start | bytes 776 | tf_op jit(solution)/shard_map/ppermute | solution.py:147
  124.2 4.5 %collective-permute-start.18 = (f32[2,2,32]{2,1,0:T(2,128)S(1)}, f32[2,2,32]{2,1,0:T(2,128)S(1)}, u32[]{:S(2)}, u32[]{:S(2)}) collective-permute-start(f32[2,2,32]{2,1,0:T(2,128)S(1)} %pad_maximum_fusion.3), channel_id=1, source_target_pairs={{0,48},{8,56},{16,0},{24,8},{32,16},{40,24},{48,32},{56,40},{64,11... | collective-permute-start | bytes 1544 | tf_op jit(solution)/shard_map/ppermute | solution.py:147
  128.7 4.5 %collective-permute-start.19 = (f32[4,2,32]{2,1,0:T(2,128)S(1)}, f32[4,2,32]{2,1,0:T(2,128)S(1)}, u32[]{:S(2)}, u32[]{:S(2)}) collective-permute-start(f32[4,2,32]{2,1,0:T(2,128)S(1)} %pad_maximum_fusion.2), channel_id=1, source_target_pairs={{0,48},{8,56},{16,0},{24,8},{32,16},{40,24},{48,32},{56,40},{64,11... | collective-permute-start | bytes 3080 | tf_op jit(solution)/shard_map/ppermute | solution.py:147
  133.2 9.6 %collective-permute-start.20 = (f32[6,2,32]{2,1,0:T(2,128)S(1)}, f32[6,2,32]{2,1,0:T(2,128)S(1)}, u32[]{:S(2)}, u32[]{:S(2)}) collective-permute-start(f32[6,2,32]{2,1,0:T(2,128)S(1)} %pad_maximum_fusion.1), channel_id=1, source_target_pairs={{0,48},{8,56},{16,0},{24,8},{32,16},{40,24},{48,32},{56,40},{64,11... | collective-permute-start | bytes 4616 | tf_op jit(solution)/shard_map/ppermute | solution.py:147
  137.4 12.6 %collective-permute-start.6 = (bf16[2,128,2048]{2,1,0:T(8,128)(2,1)}, bf16[2,128,2048]{2,1,0:T(8,128)(2,1)S(1)}, u32[]{:S(2)}, u32[]{:S(2)}) collective-permute-start(bf16[2,128,2048]{2,1,0:T(8,128)(2,1)} %get-tuple-element.247), channel_id=1, source_target_pairs={{128,0},{136,8},{144,16},{152,24},{160,32},{168,40},{176,48},{184,... | collective-permute-start | bytes 3145736 | tf_op jit(solution)/shard_map/ppermute | solution.py:190
  140.3 25.5 %collective-permute-start.13 = (bf16[2,128,2048]{2,1,0:T(8,128)(2,1)S(1)}, bf16[2,128,2048]{2,1,0:T(8,128)(2,1)S(1)}, u32[]{:S(2)}, u32[]{:S(2)}) collective-permute-start(bf16[2,128,2048]{2,1,0:T(8,128)(2,1)S(1)} %add.111), channel_id=1, source_target_pairs={{136,0},{144,8},{152,16},{160,24},{168,32},{176,40},{184,48},{192,... | collective-permute-start | bytes 3145736 | tf_op jit(solution)/shard_map/ppermute | solution.py:190
  141.6 1.3 copy-start
  142.0 23.8 %collective-permute-start.16 = (bf16[2,128,2048]{2,1,0:T(8,128)(2,1)S(1)}, bf16[2,128,2048]{2,1,0:T(8,128)(2,1)S(1)}, u32[]{:S(2)}, u32[]{:S(2)}) collective-permute-start(bf16[2,128,2048]{2,1,0:T(8,128)(2,1)S(1)} %add.115), channel_id=1, source_target_pairs={{128,8},{136,16},{144,24},{152,32},{160,40},{168,48},{176,56},{184... | collective-permute-start | bytes 3145736 | tf_op jit(solution)/shard_map/ppermute | solution.py:190
